TPU v7x, 256 devices: a whole 4x4x8 slice. The times are simulated.
256 devices in a mesh: section: 16 (over y_lo, x, core), expert: 16 (over z, y_hi).
Axes of the slice: x: 4, y: 4 (y_hi: 2, y_lo: 2; y = y_hi * 2 + y_lo), z: 8, core: 2. Of those that a mesh axis runs over, the one named last changes fastest.
Arguments:
- activations: bfloat16 [16384, 8192], P('section', 'expert'), may hold values from -12 to 12
- modality: int32 [16384], P('section'), may hold values from 0 to 1
- selected: int32 [16, 256], P('section'), may hold values from 0 to 1023, as said below
- routes: int32 [4096, 1], P('section'), may hold values from 0 to 15, as said below
- norm_gain: float32 [2, 8192], P(None, 'expert'), may hold values from 0.1 to 1.9
- router: float32 [8192], P('expert'), may hold values from -0.0625 to 0.0625
- gate_w: bfloat16 [16, 3072, 8192], P('expert', 'section'), may hold values from -0.0625 to 0.0625
- up_w: bfloat16 [16, 3072, 8192], P('expert', 'section'), may hold values from -0.0625 to 0.0625
- down_w: bfloat16 [16, 3072, 8192], P('expert', 'section'), may hold values from -0.21875 to 0.21875
Outputs:
- block_out: bfloat16 [16384, 8192], P('section', 'expert')
Inputs may be any that keep to these rules, and one draw needn't show every extreme that they name: Each row of selected lists 256 different positions in rising order, the first and the last position among them. `routes`: among the 256 rows of one section group no expert is named more than 24 times, and some expert exactly 24 times; the entry for selected[s, j] is below 8 if that token's modality is 0, and 8 or more if it is 1.
All inputs are finite; a program needn't handle non-finite values.
Results may differ from a plain program's by a relative error of at most 0.0075.
Values may be sent and summed in bfloat16 or wider, within the bound.
No kernel may reach another device: no remote copies, remote signals or barrier semaphores. Data moves between devices by JAX's collectives and lax.ppermute only.
A program may use at most 128 MiB of HBM per device.

v0:
```python
import jax
import jax.numpy as jnp
from jax import lax
from jax.sharding import PartitionSpec as P

D = 8192


EPS = 1e-05


def passed_along(block, axis, distance):
    devices = range(lax.axis_size(axis))
    route = [((i - distance) % len(devices), i) for i in devices]
    return lax.ppermute(block, axis, route)


def feature_product(block, weight):
    return lax.dot_general(
        block, weight, (((1,), (1,)), ((), ())), preferred_element_type=jnp.float32
    )


def body(activations, modality, selected, routes, norm_gain, router, gate_w, up_w, down_w):
    arrived = passed_along(activations, "section", 1)
    picks = selected[0]
    picked = arrived[picks].astype(jnp.float32)
    kinds = modality[picks]
    gains = jnp.where(kinds[:, None] == 1, norm_gain[1][None, :], norm_gain[0][None, :])
    squares, router_terms = lax.psum(
        (jnp.sum(picked * picked, axis=1), jnp.sum(picked * gains * router[None, :], axis=1)),
        "expert",
    )
    scale = lax.rsqrt(squares / D + EPS)
    normed = (picked * scale[:, None] * gains).astype(jnp.bfloat16)
    score = jax.nn.sigmoid(scale * router_terms)
    sel_count = picks.shape[0]
    expert_count = lax.axis_size("expert") * gate_w.shape[0]
    capacity = max(2, 3 * sel_count // (2 * expert_count))
    experts = routes[:, 0]
    onehot = (experts[:, None] == jnp.arange(expert_count, dtype=jnp.int32)[None, :]).astype(
        jnp.int32
    )
    ranks = jnp.cumsum(onehot, axis=0) - 1
    slot = jnp.sum(ranks * onehot, axis=1)
    target = experts * capacity + slot
    placing = (
        target[None, :] == jnp.arange(expert_count * capacity, dtype=jnp.int32)[:, None]
    ).astype(jnp.bfloat16)
    feature_width = normed.shape[1]
    buffer = jnp.dot(placing, normed, preferred_element_type=jnp.float32).astype(jnp.bfloat16)
    buffer = buffer.reshape(expert_count, capacity, feature_width)
    arrived_rows = lax.all_to_all(buffer, "expert", split_axis=0, concat_axis=2, tiled=True)
    block = lax.all_gather(arrived_rows, "section", axis=1, tiled=True)[0]
    gate = feature_product(block, gate_w[0])
    upper = feature_product(block, up_w[0])
    hidden = (jax.nn.silu(gate) * upper).astype(jnp.bfloat16)[None][0]
    part = jnp.dot(hidden, down_w[0], preferred_element_type=jnp.float32)
    summed = lax.psum_scatter(
        lax.optimization_barrier(part.astype(jnp.bfloat16))
        .astype(jnp.float32)
        .astype(jnp.bfloat16),
        "section",
        scatter_dimension=0,
        tiled=True,
    )
    expert_out = summed[None]
    gathered_back = lax.all_to_all(expert_out, "expert", split_axis=2, concat_axis=0, tiled=True)
    flat_back = gathered_back.reshape(expert_count * capacity, feature_width)
    rows_out = jnp.dot(placing.T, flat_back, preferred_element_type=jnp.float32)
    result = arrived.astype(jnp.float32).at[picks].add(score[:, None] * rows_out)
    return result.astype(jnp.bfloat16)


def solution(mesh):
    placed = (
        P("section", "expert"),
        P("section"),
        P("section", None),
        P("section", None),
        P(None, "expert"),
        P("expert"),
        P("expert", "section", None),
        P("expert", "section", None),
        P("expert", "section", None),
    )
    return jax.shard_map(
        body, mesh=mesh, in_specs=placed, out_specs=P("section", "expert"), check_vma=False
    )
```

profile of v0, /device:TPU:8, one launch (start us, length us, event | category | flops | bytes accessed | tf_op | source)
XLA Modules:
  0.0 329.9 jit_solution(17080276669654069664)
XLA Ops:
  6.5 0.0 copy-start
  6.5 0.0 copy-start.1
  6.5 0.0 all-gather.2.cloned.1.call-start
  6.5 0.0 collective-permute-start
  6.6 0.8 fusion.30
  7.4 0.6 reduce-window.6
  8.0 0.2 slice_reduce_fusion
  8.2 0.7 compare_select_fusion
  8.9 1.9 gather_fusion.1
  10.8 0.8 fusion.29
  11.6 0.7 multiply_add_fusion
  12.3 0.8 fusion.31
  13.0 10.2 %collective-permute-done = bf16[1024,512]{1,0:T(8,128)(2,1)} collective-permute-done((bf16[1024,512]{1,0:T(8,128)(2,1)}, bf16[1024,512]{1,0:T(8,128)(2,1)}, u32[]{:S(2)}, u32[]{:S(2)}) %collective-permute-start) | collective-permute-done | bytes 1048608 | tf_op jit(solution)/shard_map/ppermute | solution.py:15
  23.2 2.6 gather_fusion
  25.8 0.0 copy-done.1
  25.8 0.3 fusion.20
  26.0 44.2 %all-reduce = (f32[256]{0:T(256)S(1)}, f32[256]{0:T(256)S(1)}) all-reduce(f32[256]{0:T(256)S(1)} %get-tuple-element.6, f32[256]{0:T(256)S(1)} %get-tuple-element.5), channel_id=1, replica_groups=mesh['section'=16,'expert'=16] {'expert'}, use_global_device_ids=true, to_apply=%region_1.2 | all-reduce | flops 512 | bytes 4096 | tf_op jit(solution)/shard_map/psum | solution.py:30
  70.3 0.4 convolution_convert_fusion.1
  70.7 17.2 %all_to_all.33 = bf16[16,24,512]{2,1,0:T(8,128)(2,1)S(1)} all-to-all(bf16[16,24,512]{2,1,0:T(8,128)(2,1)S(1)} %bitcast.72), channel_id=1, replica_groups=mesh['section'=16,'expert'=16] {'expert'}, dimensions={0} | all-to-all | bytes 786432 | tf_op jit(solution)/shard_map/all_to_all | solution.py:53
  87.8 0.8 copy.22
  88.6 0.0 all-gather.2.cloned.1.call-update
  88.6 0.0 reduce-scatter.2.cloned.1.call-start
  88.7 38.2 %all-gather.2.cloned.1.call-done = bf16[1,384,8192]{2,1,0:T(8,128)(2,1)} async-done(((bf16[1,24,8192]{2,1,0:T(8,128)(2,1)}), bf16[1,384,8192]{2,1,0:T(8,128)(2,1)}) %all-gather.2.cloned.1.call-update) | async-done | bytes 6291472 | tf_op jit(solution)/shard_map/all_gather | solution.py:54
  126.9 0.0 copy-start.2
  126.9 0.0 copy-start.3
  126.9 6.1 %fusion.2 = f32[384,192]{0,1:T(8,128)S(1)} fusion(bf16[1,384,8192]{2,1,0:T(8,128)(2,1)} %all-gather.2.cloned.1.call-done, bf16[1,192,8192]{2,1,0:T(8,128)(2,1)} %param.15), kind=kOutput, calls=%fused_computation.6 | convolution fusion | flops 1207959552 | bytes 9732096 | tf_op jit(solution)/shard_map/dot_general | solution.py:19
  133.0 0.0 copy-done.2
  133.0 0.3 copy-done.3
  133.3 2.2 fusion.12
  135.6 0.0 copy-done
  135.6 4.5 %convolution_convert_fusion = bf16[384,8192]{1,0:T(8,128)(2,1)} fusion(bf16[384,192]{0,1:T(8,128)(2,1)S(1)} %fusion.12, bf16[1,192,8192]{2,1,0:T(8,128)(2,1)S(1)} %copy-done), kind=kOutput, calls=%fused_computation.3 | convolution fusion | flops 1211105280 | bytes 9584640 | tf_op jit(solution)/shard_map/dot_general | solution.py:58
  140.1 0.0 reduce-scatter.2.cloned.1.call-update
  140.1 73.4 %reduce-scatter.2.cloned.1.call-done = bf16[24,8192]{1,0:T(8,128)(2,1)} async-done(((bf16[384,8192]{1,0:T(8,128)(2,1)}), bf16[24,8192]{1,0:T(8,128)(2,1)}) %reduce-scatter.2.cloned.1.call-update) | async-done | bytes 393232 | tf_op jit(solution)/shard_map/reduce_scatter | solution.py:59
  213.5 8.4 %copy.18 = bf16[1,24,8192]{1,0,2:T(2,128)(2,1)} copy(bf16[1,24,8192]{2,1,0:T(8,128)(2,1)} %bitcast.71) | data formatting | bytes 786432 | tf_op jit(solution)/shard_map/broadcast_in_dim | solution.py:67
  221.9 0.5 broadcast.80
  222.4 46.5 %reduce.2 = bf16[8192,24]{1,0:T(8,128)(2,1)} reduce(bf16[8192,1,24]{2,1,0:T(2,128)(2,1)} %bitcast.64, bf16[]{:T(256)} %broadcast.80), dimensions={1}, to_apply=%bitcast.58.reduce_sub_computation | reduce | bytes 786434
  269.0 4.9 %reshape.96 = bf16[16,2,6144]{2,1,0:T(2,128)(2,1)} reshape(bf16[8192,24]{1,0:T(8,128)(2,1)} %reduce.2) | data formatting | bytes 786432
  273.9 9.1 %all-to-all-start.1 = ((bf16[16,2,6144]{2,1,0:T(2,128)(2,1)}), bf16[16,2,6144]{2,1,0:T(2,128)(2,1)S(1)}, u32[]{:S(2)}, u32[]{:S(2)}) async-start(bf16[16,2,6144]{2,1,0:T(2,128)(2,1)} %reshape.96), calls=%async_computation.2 | async-start | bytes 786432 | tf_op jit(solution)/shard_map/all_to_all | solution.py:68
  282.9 2.8 convert_element_type.29
  285.8 10.7 %all-to-all-done.1 = bf16[16,2,6144]{2,1,0:T(2,128)(2,1)S(1)} async-done(((bf16[16,2,6144]{2,1,0:T(2,128)(2,1)}), bf16[16,2,6144]{2,1,0:T(2,128)(2,1)S(1)}, u32[]{:S(2)}, u32[]{:S(2)}) %all-to-all-start.1) | async-done | bytes 393248 | tf_op jit(solution)/shard_map/all_to_all | solution.py:68
  296.4 8.9 %reshape.97 = bf16[8192,1,24]{2,1,0:T(2,128)(2,1)} reshape(bf16[16,2,6144]{2,1,0:T(2,128)(2,1)S(1)} %all-to-all-done.1) | data formatting | bytes 786432
  305.4 8.0 %copy.19 = bf16[1,24,8192]{2,1,0:T(8,128)(2,1)S(1)} copy(bf16[1,24,8192]{1,0,2:T(2,128)(2,1)} %bitcast.65) | data formatting | bytes 786432 | tf_op jit(solution)/shard_map/all_to_all | solution.py:68
  313.4 0.1 copy.23
  313.5 0.2 copy.20
  313.8 1.2 convolution_multiply_fusion
  314.9 5.4 %scatter_fusion = f32[1024,512]{1,0:T(8,128)} fusion(f32[1024,512]{1,0:T(8,128)} %convert_element_type.29, s32[256]{0:T(256)S(1)} %bitcast.74, f32[256,512]{1,0:T(8,128)} %convolution_multiply_fusion), kind=kCustom, calls=%fused_computation.2 | custom fusion | flops 131072 | bytes 1573888 | tf_op jit(solution)/shard_map/scatter-add | solution.py:71
  320.4 2.7 convert_element_type.36
  (6 shorter events, 0.1 us)
Async XLA Ops:
  6.5 129.0 %copy-start = (bf16[1,192,8192]{2,1,0:T(8,128)(2,1)S(1)}, bf16[1,192,8192]{2,1,0:T(8,128)(2,1)}, u32[]{:S(2)}) copy-start(bf16[1,192,8192]{2,1,0:T(8,128)(2,1)} %param.17) | copy-start | bytes 9437188
  6.5 19.2 %copy-start.1 = (f32[512]{0:T(512)S(1)}, f32[512]{0:T(512)}, u32[]{:S(2)}) copy-start(f32[512]{0:T(512)} %param.14) | copy-start | bytes 6148
  6.5 120.4 %all-gather.2.cloned.1.call-start = ((), (), s32[]{:S(2)}) async-start(), calls=%async_computation.3 | async-start | bytes 6684672 | tf_op jit(solution)/shard_map/all_gather | solution.py:54
  6.5 16.6 %collective-permute-start = (bf16[1024,512]{1,0:T(8,128)(2,1)}, bf16[1024,512]{1,0:T(8,128)(2,1)}, u32[]{:S(2)}, u32[]{:S(2)}) collective-permute-start(bf16[1024,512]{1,0:T(8,128)(2,1)} %param.9), channel_id=1, source_target_pairs={{240,0},{0,16},{16,32},{32,48},{48,64},{64,80},{80,96},{96,112},{1... | collective-permute-start | bytes 3145736 | tf_op jit(solution)/shard_map/ppermute | solution.py:15
  88.6 124.8 %reduce-scatter.2.cloned.1.call-start = ((), (), s32[]{:S(2)}) async-start(), calls=%async_computation.4 | async-start | bytes 6684672 | tf_op jit(solution)/shard_map/reduce_scatter | solution.py:59
  126.9 6.1 %copy-start.2 = (bf16[1,384,8192]{2,1,0:T(8,128)(2,1)S(1)}, bf16[1,384,8192]{2,1,0:T(8,128)(2,1)}, u32[]{:S(2)}) copy-start(bf16[1,384,8192]{2,1,0:T(8,128)(2,1)} %all-gather.2.cloned.1.call-done) | copy-start | bytes 18874372
  126.9 6.4 %copy-start.3 = (bf16[1,192,8192]{2,1,0:T(8,128)(2,1)S(1)}, bf16[1,192,8192]{2,1,0:T(8,128)(2,1)}, u32[]{:S(2)}) copy-start(bf16[1,192,8192]{2,1,0:T(8,128)(2,1)} %param.16) | copy-start | bytes 9437188
  273.9 22.6 %all-to-all-start.1 = ((bf16[16,2,6144]{2,1,0:T(2,128)(2,1)}), bf16[16,2,6144]{2,1,0:T(2,128)(2,1)S(1)}, u32[]{:S(2)}, u32[]{:S(2)}) async-start(bf16[16,2,6144]{2,1,0:T(2,128)(2,1)} %reshape.96), calls=%async_computation.2 | async-start | bytes 786432 | tf_op jit(solution)/shard_map/all_to_all | solution.py:68
Sparse Core Ops, SparseCore 0:
  88.8 38.1 all-gather.1
  140.2 73.2 reduce-scatter.1
where the time goes:
time: 333 us; the launch traced here: 330 us
  waiting for transfers between devices  132 us (40%)
  other arithmetic  61.4 us (18%)
  blocking collectives  61.4 us (18%)
  local copies, waits for them, and re-layouts  37.7 us (11%)
  matrix products  14.3 us (4%)
  between operations  13.5 us (4%)
  starting transfers between devices  9.11 us (3%)
    reduce_scatter x1, waiting for transfers between devices, body(): lax.psum_scatter(lax.optimization_barrier(part.astype(jnp.bfloat16)).asty...  73.4 us
    unnamed x1, other arithmetic  46.5 us
    psum x1, blocking collectives, body(): lax.psum((jnp.sum(picked * picked, axis=1), jnp.sum(picked * gains * rout...  44.2 us
    all_gather x1, waiting for transfers between devices, body(): block = lax.all_gather(arrived_rows, 'section', axis=1, tiled=True)[0]  38.2 us
    all_to_all x1, blocking collectives, body(): lax.all_to_all(buffer, 'expert', split_axis=0, concat_axis=2, tiled=True)  17.2 us
    unnamed x12, local copies, waits for them, and re-layouts  14.8 us
    all_to_all x1, waiting for transfers between devices, body(): lax.all_to_all(expert_out, 'expert', split_axis=2, concat_axis=0, tiled=T...  10.7 us
    ppermute x1, waiting for transfers between devices, passed_along(): return lax.ppermute(block, axis, route)  10.2 us
  transfers between devices with their start and end apart: 4, of which 4 were waited for; matrix products, arithmetic and copies ran while one was open for 3% of the time, Pallas kernels for 0%

commit v1 on v0

v1 whole, which is shorter than its diff:
```python
import jax
import jax.numpy as jnp
from jax import lax
from jax.sharding import PartitionSpec as P


EPS = 1e-05


def passed_along(block, axis, distance):
    devices = range(lax.axis_size(axis))
    route = [((i - distance) % len(devices), i) for i in devices]
    return lax.ppermute(block, axis, route)


def feature_product(block, weight):
    return lax.dot_general(
        block, weight, (((1,), (1,)), ((), ())), preferred_element_type=jnp.float32
    )


def slots_of(experts, expert_count):
    onehot = (experts[:, None] == jnp.arange(expert_count, dtype=jnp.int32)[None, :]).astype(
        jnp.int32
    )
    ranks = jnp.cumsum(onehot, axis=0) - 1
    return jnp.sum(ranks * onehot, axis=1)


def body(activations, modality, selected, routes, norm_gain, router, gate_w, up_w, down_w):
    n_section = lax.axis_size("section")
    sel_count = selected.shape[1]
    expert_count = lax.axis_size("expert") * gate_w.shape[0]
    capacity = max(2, 3 * sel_count // (2 * expert_count))
    groups = n_section

    arrived = passed_along(activations, "section", 1)

    sel_next = passed_along(selected, "section", -1)[0]
    routes_next = passed_along(routes, "section", -1)[:, 0]
    rows = activations[sel_next]
    target = routes_next * capacity + slots_of(routes_next, expert_count)
    placing = (
        target[None, :] == jnp.arange(expert_count * capacity, dtype=jnp.int32)[:, None]
    ).astype(jnp.bfloat16)
    feature_width = rows.shape[1]
    buffer = jnp.dot(placing, rows, preferred_element_type=jnp.float32).astype(jnp.bfloat16)
    buffer = buffer.reshape(expert_count, capacity, feature_width)
    mine = lax.all_to_all(buffer, "expert", split_axis=0, concat_axis=2, tiled=True)[0]

    n_exp_dev = lax.axis_size("expert")
    local_width = router.shape[0]
    tables = jnp.concatenate([norm_gain, router[None, :]], axis=0)
    tables = jnp.broadcast_to(tables[None], (n_exp_dev,) + tables.shape)
    tables = lax.all_to_all(tables, "expert", split_axis=0, concat_axis=0, tiled=True)
    tables = tables.transpose(1, 0, 2).reshape(tables.shape[1], n_exp_dev * local_width)
    gains_all = tables[:2]
    router_all = tables[2]
    expert_id = lax.axis_index("expert")
    kind = (expert_id >= expert_count // 2).astype(jnp.int32)
    gains = lax.dynamic_index_in_dim(gains_all, kind, axis=0, keepdims=False)
    picked = mine.astype(jnp.float32)
    d = picked.shape[1]
    scale = lax.rsqrt(jnp.sum(picked * picked, axis=1) / d + EPS)
    normed = (picked * scale[:, None] * gains[None, :]).astype(jnp.bfloat16)
    score = jax.nn.sigmoid(scale * jnp.sum(picked * gains[None, :] * router_all[None, :], axis=1))
    score_home = passed_along(score, "section", 1)

    block = lax.all_gather(normed, "section", axis=0, tiled=True)
    gate = feature_product(block, gate_w[0])
    upper = feature_product(block, up_w[0])
    hidden = (jax.nn.silu(gate) * upper).astype(jnp.bfloat16)
    hidden_width = hidden.shape[1]
    hidden = jnp.roll(hidden.reshape(groups, capacity, hidden_width), 1, axis=0).reshape(
        groups * capacity, hidden_width
    )
    part = jnp.dot(hidden, down_w[0], preferred_element_type=jnp.float32)
    summed = lax.psum_scatter(
        lax.optimization_barrier(part.astype(jnp.bfloat16))
        .astype(jnp.float32)
        .astype(jnp.bfloat16),
        "section",
        scatter_dimension=0,
        tiled=True,
    )
    update_rows = score_home[:, None] * summed.astype(jnp.float32)
    outgoing = update_rows.reshape(capacity, n_exp_dev, local_width).transpose(1, 0, 2)
    back = lax.all_to_all(outgoing, "expert", split_axis=0, concat_axis=0, tiled=True)
    flat_back = back.reshape(expert_count * capacity, local_width)

    picks = selected[0]
    experts = routes[:, 0]
    position = experts * capacity + slots_of(experts, expert_count)
    update = flat_back[position]
    result = arrived.astype(jnp.float32).at[picks].add(update)
    return result.astype(jnp.bfloat16)


def solution(mesh):
    placed = (
        P("section", "expert"),
        P("section"),
        P("section", None),
        P("section", None),
        P(None, "expert"),
        P("expert"),
        P("expert", "section", None),
        P("expert", "section", None),
        P("expert", "section", None),
    )
    return jax.shard_map(
        body, mesh=mesh, in_specs=placed, out_specs=P("section", "expert"), check_vma=False
    )
```

time: 333 us -> 236 us (0.71)
  blocking collectives: 61.4 us -> 0 us
  other arithmetic: 61.4 us -> 18 us
  local copies, waits for them, and re-layouts: 37.7 us -> 14.9 us
  starting transfers between devices: 9.11 us -> 26.7 us
  waiting for transfers between devices: 132 us -> 147 us
    unnamed x1, other arithmetic: 46.5 us -> 0.08 us
    psum x1 -> x0, blocking collectives: 44.2 us -> none  [body(): lax.psum((jnp.sum(picked * picked, axis=1), jnp.sum(picked * gains * rout...]
    all_to_all x1 -> x0, blocking collectives: 17.2 us -> none  [body(): lax.all_to_all(buffer, 'expert', split_axis=0, concat_axis=2, tiled=True)]
    ppermute x1 -> x4, waiting for transfers between devices: 10.2 us -> 27.1 us  [passed_along(): return lax.ppermute(block, axis, route)]
    all_to_all x1 -> x3, starting transfers between devices: 9.06 us -> 23.2 us  [the longest x1 10.6 us: body(): lax.all_to_all(tables, 'expert', split_axis=0, concat_axis=0, tiled=True)]
    unnamed x12 -> x16, local copies, waits for them, and re-layouts: 14.8 us -> 2.42 us
    all_to_all x4 -> x0, local copies, waits for them, and re-layouts: 9.02 us -> none  [the longest x3 8.24 us: body(): lax.all_to_all(expert_out, 'expert', split_axis=2, concat_axis=0, tiled=T...]
    broadcast_in_dim x1, local copies, waits for them, and re-layouts: 8.43 us -> 0.66 us  [body(): tables = jnp.broadcast_to(tables[None], (n_exp_dev,) + tables.shape)]
  transfers between devices with their start and end apart: 4 -> 9, of which waited for: 4 -> 6; matrix products, arithmetic and copies ran while one was open for 3% -> 8% of each run, Pallas kernels for 0% -> 0%
where the time goes in v1:
time: 236 us; the launch traced here: 234 us
  waiting for transfers between devices  147 us (62%)
  starting transfers between devices  26.7 us (11%)
  other arithmetic  18 us (8%)
  local copies, waits for them, and re-layouts  14.9 us (6%)
  matrix products  13.8 us (6%)
  between operations  13.6 us (6%)
    reduce_scatter x1, waiting for transfers between devices, body(): lax.psum_scatter(lax.optimization_barrier(part.astype(jnp.bfloat16)).asty...  68.2 us
    all_gather x1, waiting for transfers between devices, body(): block = lax.all_gather(normed, 'section', axis=0, tiled=True)  39 us
    ppermute x4, waiting for transfers between devices, passed_along(): return lax.ppermute(block, axis, route)  27.1 us
    all_to_all x1, starting transfers between devices, body(): lax.all_to_all(tables, 'expert', split_axis=0, concat_axis=0, tiled=True)  10.6 us
    all_to_all x1, starting transfers between devices, body(): lax.all_to_all(outgoing, 'expert', split_axis=0, concat_axis=0, tiled=True)  9.1 us
    dot_general x2, matrix products, feature_product(): lax.dot_general(block, weight, (((1,), (1,)), ((), ())), preferred_elemen...  8.29 us
    scatter-add x1, other arithmetic, body(): result = arrived.astype(jnp.float32).at[picks].add(update)  7.08 us
    all_to_all x1, waiting for transfers between devices, body(): lax.all_to_all(tables, 'expert', split_axis=0, concat_axis=0, tiled=True)  6.55 us
  transfers between devices with their start and end apart: 9, of which 6 were waited for; matrix products, arithmetic and copies ran while one was open for 8% of the time, Pallas kernels for 0%

profile of v1, /device:TPU:8, one launch (start us, length us, event | category | flops | bytes accessed | tf_op | source)
XLA Modules:
  0.0 234.0 jit_solution(3476341028551193657)
XLA Ops:
  6.5 2.1 collective-permute-start.1
  8.6 0.7 collective-permute-start.2
  9.3 0.7 pad_maximum_fusion.1
  10.0 0.7 broadcast_in_dim.5
  10.7 10.6 %all-to-all-start.1 = ((f32[16,3,512]{2,1,0:T(4,128)}), f32[16,3,512]{2,1,0:T(4,128)S(1)}, u32[]{:S(2)}, u32[]{:S(2)}) async-start(f32[16,3,512]{2,1,0:T(4,128)} %broadcast_in_dim.5), calls=%async_computation.1 | async-start | bytes 262144 | tf_op jit(solution)/shard_map/all_to_all | solution.py:55
  21.3 0.6 reduce-window.14
  21.9 0.2 slice_reduce_fusion.1
  22.1 0.1 fusion.20
  22.2 2.6 %gather_fusion = bf16[256,512]{1,0:T(8,128)(2,1)S(1)} fusion(bf16[1024,512]{1,0:T(8,128)(2,1)} %param.9, s32[1024]{0:T(1024)S(1)} %pad_clamp_fusion.1), kind=kCustom, calls=%fused_computation | custom fusion | bytes 525312 | tf_op jit(solution)/shard_map/gather | solution.py:41
  24.8 1.0 convolution_convert_fusion.1
  25.8 6.5 %all-to-all-done.1 = f32[16,3,512]{2,1,0:T(4,128)S(1)} async-done(((f32[16,3,512]{2,1,0:T(4,128)}), f32[16,3,512]{2,1,0:T(4,128)S(1)}, u32[]{:S(2)}, u32[]{:S(2)}) %all-to-all-start.1) | async-done | bytes 98336 | tf_op jit(solution)/shard_map/all_to_all | solution.py:55
  32.4 0.6 copy-done.1
  33.0 3.6 %all-to-all-start = ((bf16[16,24,512]{2,1,0:T(8,128)(2,1)}), bf16[16,24,512]{2,1,0:T(8,128)(2,1)S(1)}, u32[]{:S(2)}, u32[]{:S(2)}) async-start(bf16[16,24,512]{2,1,0:T(8,128)(2,1)} %bitcast.99), calls=%async_computation | async-start | bytes 786432 | tf_op jit(solution)/shard_map/all_to_all | solution.py:49
  36.6 1.5 slice.52
  38.2 1.5 slice.53
  39.7 0.5 broadcast.160
  40.3 2.7 %fusion.23 = (f32[8192]{0:T(1024)}, f32[1,8192]{1,0:T(1,128)}) fusion(f32[]{:T(128)} %broadcast.160, f32[2,8192]{1,0:T(2,128)} %bitcast.105, s32[]{:T(128)S(6)} %select_n.30), kind=kLoop, calls=%fused_computation.54 | loop fusion | bytes 98312 | tf_op jit(solution)/shard_map/jit(dynamic_index_in_dim)/dynamic_slice | solution.py:61
  43.0 1.4 mul.85
  44.3 1.4 copy.34
  45.7 6.1 %all-to-all-done = bf16[16,24,512]{2,1,0:T(8,128)(2,1)S(1)} async-done(((bf16[16,24,512]{2,1,0:T(8,128)(2,1)}), bf16[16,24,512]{2,1,0:T(8,128)(2,1)S(1)}, u32[]{:S(2)}, u32[]{:S(2)}) %all-to-all-start) | async-done | bytes 393248 | tf_op jit(solution)/shard_map/all_to_all | solution.py:49
  51.8 0.1 fusion.24
  51.8 0.1 copy.27
  51.9 1.0 fusion.13
  53.0 0.9 multiply_convert_fusion
  53.9 0.0 reduce-scatter.2.cloned.1.call-start
  53.9 39.0 %all-gather.2.cloned.1.call-done = bf16[384,8192]{1,0:T(8,128)(2,1)} async-done(((bf16[24,8192]{1,0:T(8,128)(2,1)}), bf16[384,8192]{1,0:T(8,128)(2,1)}) %all-gather.2.cloned.1.call-update) | async-done | bytes 6291472 | tf_op jit(solution)/shard_map/all_gather | solution.py:69
  93.0 6.1 %fusion.3 = f32[384,192]{0,1:T(8,128)S(1)} fusion(bf16[384,8192]{1,0:T(8,128)(2,1)} %all-gather.2.cloned.1.call-done, bf16[1,192,8192]{2,1,0:T(8,128)(2,1)} %param.14), kind=kOutput, calls=%fused_computation.7 | convolution fusion | flops 1207959552 | bytes 9732096 | tf_op jit(solution)/shard_map/dot_general | solution.py:17
  99.0 0.3 copy-done.6
  99.4 2.2 fusion.8
  101.6 0.1 slice_bitcast_fusion
  101.7 0.1 copy.19
  101.8 0.1 copy.20
  101.9 0.1 pad_maximum_fusion
  102.0 4.5 %convolution_convert_fusion = bf16[384,8192]{1,0:T(8,128)(2,1)} fusion(bf16[384,192]{1,0:T(8,128)(2,1)S(1)} %bitcast.100, bf16[1,192,8192]{2,1,0:T(8,128)(2,1)S(1)} %copy-done), kind=kOutput, calls=%fused_computation.3 | convolution fusion | flops 1211105280 | bytes 9584640 | tf_op jit(solution)/shard_map/dot_general | solution.py:77
  106.5 0.3 collective-permute-start.3
  106.8 4.8 %collective-permute-done.3 = f32[24]{0:T(128)S(1)} collective-permute-done((f32[24]{0:T(128)S(1)}, f32[24]{0:T(128)S(1)}, u32[]{:S(2)}, u32[]{:S(2)}) %collective-permute-start.3) | collective-permute-done | bytes 128 | tf_op jit(solution)/shard_map/ppermute | solution.py:13
  111.7 68.2 %reduce-scatter.2.cloned.1.call-done = bf16[24,8192]{1,0:T(8,128)(2,1)} async-done(((bf16[384,8192]{1,0:T(8,128)(2,1)}), bf16[24,8192]{1,0:T(8,128)(2,1)}) %reduce-scatter.2.cloned.1.call-update) | async-done | bytes 393232 | tf_op jit(solution)/shard_map/reduce_scatter | solution.py:78
  179.9 1.1 convert_multiply_fusion.2
  181.0 0.9 copy.33
  181.9 9.1 %all-to-all-start.2 = ((f32[16,24,512]{2,1,0:T(8,128)}), f32[16,24,512]{2,1,0:T(8,128)}, u32[]{:S(2)}, u32[]{:S(2)}) async-start(f32[16,24,512]{2,1,0:T(8,128)} %bitcast.96), calls=%async_computation.3 | async-start | bytes 1572864 | tf_op jit(solution)/shard_map/all_to_all | solution.py:88
  191.0 0.3 collective-permute-start
  191.3 0.6 reduce-window.16
  191.9 0.2 slice_reduce_fusion
  192.1 0.1 fusion.18
  192.3 22.2 %collective-permute-done = bf16[1024,512]{1,0:T(8,128)(2,1)} collective-permute-done((bf16[1024,512]{1,0:T(8,128)(2,1)}, bf16[1024,512]{1,0:T(8,128)(2,1)}, u32[]{:S(2)}, u32[]{:S(2)}) %collective-permute-start) | collective-permute-done | bytes 1048608 | tf_op jit(solution)/shard_map/ppermute | solution.py:13
  214.5 2.9 %convert_element_type.55 = f32[1024,512]{1,0:T(8,128)} convert(bf16[1024,512]{1,0:T(8,128)(2,1)} %collective-permute-done) | non-fusion elementwise | flops 524288 | bytes 3145728 | tf_op jit(solution)/shard_map/convert_element_type | solution.py:95
  217.4 7.1 %scatter_custom_fusion = f32[1024,512]{1,0:T(8,128)} fusion(f32[1024,512]{1,0:T(8,128)} %convert_element_type.55, s32[256]{0:T(256)S(1)} %bitcast.117, f32[384,512]{1,0:T(8,128)} %bitcast.22, s32[1024]{0:T(1024)S(1)} %pad_clamp_fusion), kind=kCustom, calls=%fused_computation.21 | custom fusion | flops 131072 | bytes 2097152 | tf_op jit(solution)/shard_map/scatter-add | solution.py:95
  224.5 2.7 %convert_element_type.69 = bf16[1024,512]{1,0:T(8,128)(2,1)} convert(f32[1024,512]{1,0:T(8,128)} %scatter_custom_fusion) | non-fusion elementwise | flops 524288 | bytes 3145728 | tf_op jit(solution)/shard_map/convert_element_type | solution.py:96
  (31 shorter events, 0.3 us)
Async XLA Ops:
  6.5 95.4 %copy-start = (bf16[1,192,8192]{2,1,0:T(8,128)(2,1)S(1)}, bf16[1,192,8192]{2,1,0:T(8,128)(2,1)}, u32[]{:S(2)}) copy-start(bf16[1,192,8192]{2,1,0:T(8,128)(2,1)} %param.16) | copy-start | bytes 9437188
  6.5 14.7 %collective-permute-start.1 = (s32[256,1]{0,1:T(1,128)}, s32[256,1]{0,1:T(1,128)S(1)}, u32[]{:S(2)}, u32[]{:S(2)}) collective-permute-start(s32[256,1]{0,1:T(1,128)} %param.11), channel_id=1, source_target_pairs={{16,0},{32,16},{48,32},{64,48},{80,64},{96,80},{112,96},{128,112},... | collective-permute-start | bytes 3080 | tf_op jit(solution)/shard_map/ppermute | solution.py:13
  8.6 13.6 %collective-permute-start.2 = (s32[1,256]{1,0:T(1,128)}, s32[1,256]{1,0:T(1,128)S(1)}, u32[]{:S(2)}, u32[]{:S(2)}) collective-permute-start(s32[1,256]{1,0:T(1,128)} %param.10), channel_id=1, source_target_pairs={{16,0},{32,16},{48,32},{64,48},{80,64},{96,80},{112,96},{128,112},... | collective-permute-start | bytes 3080 | tf_op jit(solution)/shard_map/ppermute | solution.py:13
  10.7 21.7 %all-to-all-start.1 = ((f32[16,3,512]{2,1,0:T(4,128)}), f32[16,3,512]{2,1,0:T(4,128)S(1)}, u32[]{:S(2)}, u32[]{:S(2)}) async-start(f32[16,3,512]{2,1,0:T(4,128)} %broadcast_in_dim.5), calls=%async_computation.1 | async-start | bytes 262144 | tf_op jit(solution)/shard_map/all_to_all | solution.py:55
  32.4 0.6 copy-start.1
  33.0 18.7 %all-to-all-start = ((bf16[16,24,512]{2,1,0:T(8,128)(2,1)}), bf16[16,24,512]{2,1,0:T(8,128)(2,1)S(1)}, u32[]{:S(2)}, u32[]{:S(2)}) async-start(bf16[16,24,512]{2,1,0:T(8,128)(2,1)} %bitcast.99), calls=%async_computation | async-start | bytes 786432 | tf_op jit(solution)/shard_map/all_to_all | solution.py:49
  36.6 56.4 %all-gather.2.cloned.1.call-start = ((), (), s32[]{:S(2)}) async-start(), calls=%async_computation.4 | async-start | bytes 6684672 | tf_op jit(solution)/shard_map/all_gather | solution.py:69
  51.8 1.2 copy-start.2
  53.9 126.0 %reduce-scatter.2.cloned.1.call-start = ((), (), s32[]{:S(2)}) async-start(), calls=%async_computation.5 | async-start | bytes 6684672 | tf_op jit(solution)/shard_map/reduce_scatter | solution.py:78
  93.0 6.1 %copy-start.5 = (bf16[384,8192]{1,0:T(8,128)(2,1)S(1)}, bf16[384,8192]{1,0:T(8,128)(2,1)}, u32[]{:S(2)}) copy-start(bf16[384,8192]{1,0:T(8,128)(2,1)} %all-gather.2.cloned.1.call-done) | copy-start | bytes 18874372
  93.0 6.4 %copy-start.6 = (bf16[1,192,8192]{2,1,0:T(8,128)(2,1)S(1)}, bf16[1,192,8192]{2,1,0:T(8,128)(2,1)}, u32[]{:S(2)}) copy-start(bf16[1,192,8192]{2,1,0:T(8,128)(2,1)} %param.15) | copy-start | bytes 9437188
  106.5 84.8 %copy-start.3 = (s32[256,1]{0,1:T(1,128)S(1)}, s32[256,1]{0,1:T(1,128)}, u32[]{:S(2)}) copy-start(s32[256,1]{0,1:T(1,128)} %param.11) | copy-start | bytes 3076
  106.5 85.8 %copy-start.4 = (s32[1,256]{1,0:T(1,128)S(1)}, s32[1,256]{1,0:T(1,128)}, u32[]{:S(2)}) copy-start(s32[1,256]{1,0:T(1,128)} %param.10) | copy-start | bytes 3076
  106.5 5.2 %collective-permute-start.3 = (f32[24]{0:T(128)S(1)}, f32[24]{0:T(128)S(1)}, u32[]{:S(2)}, u32[]{:S(2)}) collective-permute-start(f32[24]{0:T(128)S(1)} %get-tuple-element.9), channel_id=1, source_target_pairs={{240,0},{0,16},{16,32},{32,48},{48,64},{64,80},{80,96},{96,112},{1... | collective-permute-start | bytes 296 | tf_op jit(solution)/shard_map/ppermute | solution.py:13
  181.9 35.5 %all-to-all-start.2 = ((f32[16,24,512]{2,1,0:T(8,128)}), f32[16,24,512]{2,1,0:T(8,128)}, u32[]{:S(2)}, u32[]{:S(2)}) async-start(f32[16,24,512]{2,1,0:T(8,128)} %bitcast.96), calls=%async_computation.3 | async-start | bytes 1572864 | tf_op jit(solution)/shard_map/all_to_all | solution.py:88
  191.0 23.5 %collective-permute-start = (bf16[1024,512]{1,0:T(8,128)(2,1)}, bf16[1024,512]{1,0:T(8,128)(2,1)}, u32[]{:S(2)}, u32[]{:S(2)}) collective-permute-start(bf16[1024,512]{1,0:T(8,128)(2,1)} %param.9), channel_id=1, source_target_pairs={{240,0},{0,16},{16,32},{32,48},{48,64},{64,80},{80,96},{96,112},{1... | collective-permute-start | bytes 3145736 | tf_op jit(solution)/shard_map/ppermute | solution.py:13
Sparse Core Ops, SparseCore 0:
  54.0 38.8 all-gather.1
  106.6 73.2 reduce-scatter.1

commit v2 on v1

--- a/solution.py
+++ b/solution.py
@@ -7,9 +7,14 @@
 EPS = 1e-05
 
 
+SECTION = ("chip", "core")
+
+
 def passed_along(block, axis, distance):
-    devices = range(lax.axis_size(axis))
-    route = [((i - distance) % len(devices), i) for i in devices]
+    count = 1
+    for name in axis:
+        count *= lax.axis_size(name)
+    route = [((i - distance) % count, i) for i in range(count)]
     return lax.ppermute(block, axis, route)
 
 
@@ -28,16 +33,18 @@
 
 
 def body(activations, modality, selected, routes, norm_gain, router, gate_w, up_w, down_w):
-    n_section = lax.axis_size("section")
+    n_chip = lax.axis_size("chip")
+    n_core = lax.axis_size("core")
+    n_section = n_chip * n_core
     sel_count = selected.shape[1]
     expert_count = lax.axis_size("expert") * gate_w.shape[0]
     capacity = max(2, 3 * sel_count // (2 * expert_count))
     groups = n_section
 
-    arrived = passed_along(activations, "section", 1)
+    arrived = passed_along(activations, SECTION, 1)
 
-    sel_next = passed_along(selected, "section", -1)[0]
-    routes_next = passed_along(routes, "section", -1)[:, 0]
+    sel_next = passed_along(selected, SECTION, -1)[0]
+    routes_next = passed_along(routes, SECTION, -1)[:, 0]
     rows = activations[sel_next]
     target = routes_next * capacity + slots_of(routes_next, expert_count)
     placing = (
@@ -47,6 +54,7 @@
     buffer = jnp.dot(placing, rows, preferred_element_type=jnp.float32).astype(jnp.bfloat16)
     buffer = buffer.reshape(expert_count, capacity, feature_width)
     mine = lax.all_to_all(buffer, "expert", split_axis=0, concat_axis=2, tiled=True)[0]
+    arrived, mine = lax.optimization_barrier((arrived, mine))
 
     n_exp_dev = lax.axis_size("expert")
     local_width = router.shape[0]
@@ -64,25 +72,28 @@
     scale = lax.rsqrt(jnp.sum(picked * picked, axis=1) / d + EPS)
     normed = (picked * scale[:, None] * gains[None, :]).astype(jnp.bfloat16)
     score = jax.nn.sigmoid(scale * jnp.sum(picked * gains[None, :] * router_all[None, :], axis=1))
-    score_home = passed_along(score, "section", 1)
+    score_home = passed_along(score, SECTION, 1)
 
-    block = lax.all_gather(normed, "section", axis=0, tiled=True)
+    block = lax.all_gather(normed, "chip", axis=0, tiled=True)
+    block = lax.all_gather(block, "core", axis=0, tiled=True)
     gate = feature_product(block, gate_w[0])
     upper = feature_product(block, up_w[0])
     hidden = (jax.nn.silu(gate) * upper).astype(jnp.bfloat16)
     hidden_width = hidden.shape[1]
-    hidden = jnp.roll(hidden.reshape(groups, capacity, hidden_width), 1, axis=0).reshape(
-        groups * capacity, hidden_width
+    order = []
+    for core in range(n_core):
+        for chip in range(n_chip):
+            host = (chip * n_core + core - 1) % n_section
+            order.append((host % n_core) * n_chip + host // n_core)
+    hidden = jnp.take(
+        hidden.reshape(groups, capacity, hidden_width), jnp.array(order, jnp.int32), axis=0
+    ).reshape(groups * capacity, hidden_width)
+    part = jnp.dot(hidden, down_w[0], preferred_element_type=jnp.float32)
+    partial = (
+        lax.optimization_barrier(part.astype(jnp.bfloat16)).astype(jnp.float32).astype(jnp.bfloat16)
     )
-    part = jnp.dot(hidden, down_w[0], preferred_element_type=jnp.float32)
-    summed = lax.psum_scatter(
-        lax.optimization_barrier(part.astype(jnp.bfloat16))
-        .astype(jnp.float32)
-        .astype(jnp.bfloat16),
-        "section",
-        scatter_dimension=0,
-        tiled=True,
-    )
+    summed = lax.psum_scatter(partial, "core", scatter_dimension=0, tiled=True)
+    summed = lax.psum_scatter(summed, "chip", scatter_dimension=0, tiled=True)
     update_rows = score_home[:, None] * summed.astype(jnp.float32)
     outgoing = update_rows.reshape(capacity, n_exp_dev, local_width).transpose(1, 0, 2)
     back = lax.all_to_all(outgoing, "expert", split_axis=0, concat_axis=0, tiled=True)
@@ -97,17 +108,21 @@
 
 
 def solution(mesh):
+    n_section, n_expert = mesh.devices.shape
+    split = jax.sharding.Mesh(
+        mesh.devices.reshape(n_section // 2, 2, n_expert), ("chip", "core", "expert")
+    )
     placed = (
-        P("section", "expert"),
-        P("section"),
-        P("section", None),
-        P("section", None),
+        P(SECTION, "expert"),
+        P(SECTION),
+        P(SECTION, None),
+        P(SECTION, None),
         P(None, "expert"),
         P("expert"),
-        P("expert", "section", None),
-        P("expert", "section", None),
-        P("expert", "section", None),
+        P("expert", SECTION, None),
+        P("expert", SECTION, None),
+        P("expert", SECTION, None),
     )
     return jax.shard_map(
-        body, mesh=mesh, in_specs=placed, out_specs=P("section", "expert"), check_vma=False
+        body, mesh=split, in_specs=placed, out_specs=P(SECTION, "expert"), check_vma=False
     )

time: 236 us -> 257 us (1.089)
  waiting for transfers between devices: 147 us -> 171 us
  local copies, waits for them, and re-layouts: 14.9 us -> 9.34 us
    all_gather x1 -> x2, waiting for transfers between devices: 39 us -> 65.8 us  [the longest x1 41.2 us: body(): block = lax.all_gather(normed, 'chip', axis=0, tiled=True)]
    ppermute x4, waiting for transfers between devices: 27.1 us -> 4.76 us  [passed_along(): return lax.ppermute(block, axis, route)]
    all_to_all x1, waiting for transfers between devices: 0.01 us -> 16.4 us  [body(): lax.all_to_all(outgoing, 'expert', split_axis=0, concat_axis=0, tiled=True)]
    all_to_all x1, waiting for transfers between devices: 6.07 us -> 10.4 us  [body(): lax.all_to_all(buffer, 'expert', split_axis=0, concat_axis=2, tiled=True)[0]]
    dynamic_slice x2 -> x1, local copies, waits for them, and re-layouts: 3.22 us -> 0.63 us  [body(): gains = lax.dynamic_index_in_dim(gains_all, kind, axis=0, keepdims=False)]
    reduce_scatter x1 -> x2, waiting for transfers between devices: 68.2 us -> 67.6 us  [the longest x1 46.3 us: body(): summed = lax.psum_scatter(summed, 'chip', scatter_dimension=0, tiled=True)]
  transfers between devices with their start and end apart: 9 -> 11, of which waited for: 6 -> 8; matrix products, arithmetic and copies ran while one was open for 8% -> 5% of each run, Pallas kernels for 0% -> 0%
where the time goes in v2:
time: 257 us; the launch traced here: 255 us
  waiting for transfers between devices  171 us (67%)
  starting transfers between devices  28.7 us (11%)
  other arithmetic  18.7 us (7%)
  matrix products  13.8 us (5%)
  between operations  13.3 us (5%)
  local copies, waits for them, and re-layouts  9.34 us (4%)
    reduce_scatter x1, waiting for transfers between devices, body(): summed = lax.psum_scatter(summed, 'chip', scatter_dimension=0, tiled=True)  46.3 us
    all_gather x1, waiting for transfers between devices, body(): block = lax.all_gather(normed, 'chip', axis=0, tiled=True)  41.2 us
    all_gather x1, waiting for transfers between devices, body(): block = lax.all_gather(block, 'core', axis=0, tiled=True)  24.6 us
    reduce_scatter x1, waiting for transfers between devices, body(): summed = lax.psum_scatter(partial, 'core', scatter_dimension=0, tiled=True)  21.2 us
    all_to_all x1, waiting for transfers between devices, body(): lax.all_to_all(outgoing, 'expert', split_axis=0, concat_axis=0, tiled=True)  16.4 us
    all_to_all x1, starting transfers between devices, body(): lax.all_to_all(tables, 'expert', split_axis=0, concat_axis=0, tiled=True)  10.6 us
    all_to_all x1, waiting for transfers between devices, body(): lax.all_to_all(buffer, 'expert', split_axis=0, concat_axis=2, tiled=True)[0]  10.4 us
    all_to_all x1, starting transfers between devices, body(): lax.all_to_all(outgoing, 'expert', split_axis=0, concat_axis=0, tiled=True)  8.87 us
  transfers between devices with their start and end apart: 11, of which 8 were waited for; matrix products, arithmetic and copies ran while one was open for 5% of the time, Pallas kernels for 0%

profile of v2, /device:TPU:8, one launch (start us, length us, event | category | flops | bytes accessed | tf_op | source)
XLA Modules:
  0.0 255.3 jit_solution(224112072317687860)
XLA Ops:
  6.5 2.1 collective-permute-start.1
  8.6 0.7 collective-permute-start.2
  9.3 0.7 pad_maximum_fusion
  10.0 0.7 broadcast_in_dim.14
  10.7 10.6 %all-to-all-start.1 = ((f32[16,3,512]{2,1,0:T(4,128)}), f32[16,3,512]{2,1,0:T(4,128)S(1)}, u32[]{:S(2)}, u32[]{:S(2)}) async-start(f32[16,3,512]{2,1,0:T(4,128)} %broadcast_in_dim.14), calls=%async_computation.1 | async-start | bytes 262144 | tf_op jit(solution)/shard_map/all_to_all | solution.py:63
  21.3 0.6 reduce-window.14
  21.9 0.2 slice_reduce_fusion.1
  22.1 0.1 fusion.22
  22.3 2.6 %gather_fusion = bf16[256,512]{1,0:T(8,128)(2,1)S(1)} fusion(bf16[1024,512]{1,0:T(8,128)(2,1)} %param.10, s32[1024]{0:T(1024)S(1)} %pad_clamp_fusion.2), kind=kCustom, calls=%fused_computation | custom fusion | bytes 525312 | tf_op jit(solution)/shard_map/gather | solution.py:48
  24.8 1.0 convolution_convert_fusion.1
  25.9 6.5 %all-to-all-done.1 = f32[16,3,512]{2,1,0:T(4,128)S(1)} async-done(((f32[16,3,512]{2,1,0:T(4,128)}), f32[16,3,512]{2,1,0:T(4,128)S(1)}, u32[]{:S(2)}, u32[]{:S(2)}) %all-to-all-start.1) | async-done | bytes 98336 | tf_op jit(solution)/shard_map/all_to_all | solution.py:63
  32.4 0.6 copy-done.1
  33.0 5.9 %all-to-all-start = ((bf16[16,24,512]{2,1,0:T(8,128)(2,1)}), bf16[16,24,512]{2,1,0:T(8,128)(2,1)S(1)}, u32[]{:S(2)}, u32[]{:S(2)}) async-start(bf16[16,24,512]{2,1,0:T(8,128)(2,1)} %bitcast.5), calls=%async_computation | async-start | bytes 786432 | tf_op jit(solution)/shard_map/all_to_all | solution.py:56
  39.0 0.0 all-gather.3.cloned.1.call-start
  39.0 0.9 slice.36
  40.0 1.5 slice.37
  41.5 0.6 constant_dynamic-slice_fusion
  42.1 10.4 %all-to-all-done = bf16[16,24,512]{2,1,0:T(8,128)(2,1)S(1)} async-done(((bf16[16,24,512]{2,1,0:T(8,128)(2,1)}), bf16[16,24,512]{2,1,0:T(8,128)(2,1)S(1)}, u32[]{:S(2)}, u32[]{:S(2)}) %all-to-all-start) | async-done | bytes 393248 | tf_op jit(solution)/shard_map/all_to_all | solution.py:56
  52.5 1.0 fusion.13
  53.6 1.7 fusion.15
  55.3 0.0 all-gather.3.cloned.1.call-update
  55.3 0.0 all-gather.5.cloned.1.call-start
  55.3 41.2 %all-gather.3.cloned.1.call-done = bf16[192,8192]{1,0:T(8,128)(2,1)} async-done(((bf16[24,8192]{1,0:T(8,128)(2,1)}), bf16[192,8192]{1,0:T(8,128)(2,1)}) %all-gather.3.cloned.1.call-update) | async-done | bytes 3145744 | tf_op jit(solution)/shard_map/all_gather | solution.py:77
  96.5 0.0 all-gather.5.cloned.1.call-update
  96.6 0.0 reduce-scatter.3.cloned.1.call-start
  96.6 24.6 %all-gather.5.cloned.1.call-done = bf16[384,8192]{1,0:T(8,128)(2,1)} async-done(((bf16[192,8192]{1,0:T(8,128)(2,1)}), bf16[384,8192]{1,0:T(8,128)(2,1)}) %all-gather.5.cloned.1.call-update) | async-done | bytes 6291472 | tf_op jit(solution)/shard_map/all_gather | solution.py:78
  121.2 6.1 %fusion.3 = f32[384,192]{0,1:T(8,128)S(1)} fusion(bf16[384,8192]{1,0:T(8,128)(2,1)} %all-gather.5.cloned.1.call-done, bf16[1,192,8192]{2,1,0:T(8,128)(2,1)} %param.15), kind=kOutput, calls=%fused_computation.8 | convolution fusion | flops 1207959552 | bytes 9732096 | tf_op jit(solution)/shard_map/dot_general | solution.py:22
  127.3 0.3 copy-done.6
  127.6 2.2 fusion.8
  129.9 0.1 copy.18
  130.0 0.6 gather_fusion.1
  130.6 4.5 %convolution_convert_fusion = bf16[384,8192]{1,0:T(8,128)(2,1)} fusion(bf16[384,192]{1,0:T(8,128)(2,1)S(1)} %bitcast.89, bf16[1,192,8192]{2,1,0:T(8,128)(2,1)S(1)} %copy-done), kind=kOutput, calls=%fused_computation.4 | convolution fusion | flops 1211105280 | bytes 9584640 | tf_op jit(solution)/shard_map/dot_general | solution.py:91
  135.1 0.0 reduce-scatter.5.cloned.1.call-start
  135.1 21.2 %reduce-scatter.3.cloned.1.call-done = bf16[192,8192]{1,0:T(8,128)(2,1)} async-done(((bf16[384,8192]{1,0:T(8,128)(2,1)}), bf16[192,8192]{1,0:T(8,128)(2,1)}) %reduce-scatter.3.cloned.1.call-update) | async-done | bytes 3145744 | tf_op jit(solution)/shard_map/reduce_scatter | solution.py:95
  156.4 0.0 reduce-scatter.5.cloned.1.call-update
  156.4 0.4 collective-permute-start.3
  156.8 4.7 %collective-permute-done.3 = f32[24]{0:T(128)S(1)} collective-permute-done((f32[24]{0:T(128)S(1)}, f32[24]{0:T(128)S(1)}, u32[]{:S(2)}, u32[]{:S(2)}) %collective-permute-start.3) | collective-permute-done | bytes 128 | tf_op jit(solution)/shard_map/ppermute | solution.py:18
  161.5 46.3 %reduce-scatter.5.cloned.1.call-done = bf16[24,8192]{1,0:T(8,128)(2,1)} async-done(((bf16[192,8192]{1,0:T(8,128)(2,1)}), bf16[24,8192]{1,0:T(8,128)(2,1)}) %reduce-scatter.5.cloned.1.call-update) | async-done | bytes 393232 | tf_op jit(solution)/shard_map/reduce_scatter | solution.py:96
  207.9 1.1 convert_multiply_fusion.3
  209.0 0.9 copy.29
  209.9 8.9 %all-to-all-start.2 = ((f32[16,24,512]{2,1,0:T(8,128)}), f32[16,24,512]{2,1,0:T(8,128)}, u32[]{:S(2)}, u32[]{:S(2)}) async-start(f32[16,24,512]{2,1,0:T(8,128)} %bitcast.85), calls=%async_computation.4 | async-start | bytes 1572864 | tf_op jit(solution)/shard_map/all_to_all | solution.py:99
  218.8 0.6 reduce-window.16
  219.4 0.2 slice_reduce_fusion
  219.6 0.1 fusion.20
  219.8 2.9 %convert_element_type.42 = f32[1024,512]{1,0:T(8,128)} convert(bf16[1024,512]{1,0:T(8,128)(2,1)} %collective-permute-done) | non-fusion elementwise | flops 524288 | bytes 3145728 | tf_op jit(solution)/shard_map/convert_element_type | solution.py:106
  222.6 16.4 %all-to-all-done.2 = f32[16,24,512]{2,1,0:T(8,128)} async-done(((f32[16,24,512]{2,1,0:T(8,128)}), f32[16,24,512]{2,1,0:T(8,128)}, u32[]{:S(2)}, u32[]{:S(2)}) %all-to-all-start.2) | async-done | bytes 786464 | tf_op jit(solution)/shard_map/all_to_all | solution.py:99
  239.0 7.1 %scatter_custom_fusion = f32[1024,512]{1,0:T(8,128)} fusion(f32[1024,512]{1,0:T(8,128)} %convert_element_type.42, s32[256]{0:T(256)S(1)} %bitcast.105, f32[384,512]{1,0:T(8,128)} %bitcast.21, s32[1024]{0:T(1024)S(1)} %pad_clamp_fusion), kind=kCustom, calls=%fused_computation.23 | custom fusion | flops 131072 | bytes 2097152 | tf_op jit(solution)/shard_map/scatter-add | solution.py:106
  246.1 2.7 %convert_element_type.50 = bf16[1024,512]{1,0:T(8,128)(2,1)} convert(f32[1024,512]{1,0:T(8,128)} %scatter_custom_fusion) | non-fusion elementwise | flops 524288 | bytes 3145728 | tf_op jit(solution)/shard_map/convert_element_type | solution.py:107
  (32 shorter events, 0.2 us)
Async XLA Ops:
  6.5 124.1 %copy-start = (bf16[1,192,8192]{2,1,0:T(8,128)(2,1)S(1)}, bf16[1,192,8192]{2,1,0:T(8,128)(2,1)}, u32[]{:S(2)}) copy-start(bf16[1,192,8192]{2,1,0:T(8,128)(2,1)} %param.17) | copy-start | bytes 9437188
  6.5 14.7 %collective-permute-start.1 = (s32[256,1]{0,1:T(1,128)}, s32[256,1]{0,1:T(1,128)S(1)}, u32[]{:S(2)}, u32[]{:S(2)}) collective-permute-start(s32[256,1]{0,1:T(1,128)} %param.12), channel_id=1, source_target_pairs={{16,0},{32,16},{48,32},{64,48},{80,64},{96,80},{112,96},{128,112},... | collective-permute-start | bytes 3080 | tf_op jit(solution)/shard_map/ppermute | solution.py:18
  8.6 13.6 %collective-permute-start.2 = (s32[1,256]{1,0:T(1,128)}, s32[1,256]{1,0:T(1,128)S(1)}, u32[]{:S(2)}, u32[]{:S(2)}) collective-permute-start(s32[1,256]{1,0:T(1,128)} %param.11), channel_id=1, source_target_pairs={{16,0},{32,16},{48,32},{64,48},{80,64},{96,80},{112,96},{128,112},... | collective-permute-start | bytes 3080 | tf_op jit(solution)/shard_map/ppermute | solution.py:18
  9.3 43.2 %collective-permute-start = (bf16[1024,512]{1,0:T(8,128)(2,1)}, bf16[1024,512]{1,0:T(8,128)(2,1)}, u32[]{:S(2)}, u32[]{:S(2)}) collective-permute-start(bf16[1024,512]{1,0:T(8,128)(2,1)} %param.10), channel_id=1, source_target_pairs={{240,0},{0,16},{16,32},{32,48},{48,64},{64,80},{80,96},{96,112},{1... | collective-permute-start | bytes 3145736 | tf_op jit(solution)/shard_map/ppermute | solution.py:18
  10.7 21.7 %all-to-all-start.1 = ((f32[16,3,512]{2,1,0:T(4,128)}), f32[16,3,512]{2,1,0:T(4,128)S(1)}, u32[]{:S(2)}, u32[]{:S(2)}) async-start(f32[16,3,512]{2,1,0:T(4,128)} %broadcast_in_dim.14), calls=%async_computation.1 | async-start | bytes 262144 | tf_op jit(solution)/shard_map/all_to_all | solution.py:63
  32.4 0.6 copy-start.1
  32.4 64.2 %copy-start.4 = (s32[16]{0:T(128)S(1)}, s32[16]{0:T(128)}, u32[]{:S(2)}) copy-start(s32[16]{0:T(128)} %constant.71) | copy-start | bytes 196
  33.0 19.4 %all-to-all-start = ((bf16[16,24,512]{2,1,0:T(8,128)(2,1)}), bf16[16,24,512]{2,1,0:T(8,128)(2,1)S(1)}, u32[]{:S(2)}, u32[]{:S(2)}) async-start(bf16[16,24,512]{2,1,0:T(8,128)(2,1)} %bitcast.5), calls=%async_computation | async-start | bytes 786432 | tf_op jit(solution)/shard_map/all_to_all | solution.py:56
  39.0 57.6 %all-gather.3.cloned.1.call-start = ((), (), s32[]{:S(2)}) async-start(), calls=%async_computation.5 | async-start | bytes 3538944 | tf_op jit(solution)/shard_map/all_gather | solution.py:77
  55.3 65.9 %all-gather.5.cloned.1.call-start = ((), (), s32[]{:S(2)}) async-start(), calls=%async_computation.6 | async-start | bytes 9437184 | tf_op jit(solution)/shard_map/all_gather | solution.py:78
  96.6 59.8 %reduce-scatter.3.cloned.1.call-start = ((), (), s32[]{:S(2)}) async-start(), calls=%async_computation.7 | async-start | bytes 9437184 | tf_op jit(solution)/shard_map/reduce_scatter | solution.py:95
  121.2 6.1 %copy-start.5 = (bf16[384,8192]{1,0:T(8,128)(2,1)S(1)}, bf16[384,8192]{1,0:T(8,128)(2,1)}, u32[]{:S(2)}) copy-start(bf16[384,8192]{1,0:T(8,128)(2,1)} %all-gather.5.cloned.1.call-done) | copy-start | bytes 18874372
  121.2 6.4 %copy-start.6 = (bf16[1,192,8192]{2,1,0:T(8,128)(2,1)S(1)}, bf16[1,192,8192]{2,1,0:T(8,128)(2,1)}, u32[]{:S(2)}) copy-start(bf16[1,192,8192]{2,1,0:T(8,128)(2,1)} %param.16) | copy-start | bytes 9437188
  135.1 72.8 %reduce-scatter.5.cloned.1.call-start = ((), (), s32[]{:S(2)}) async-start(), calls=%async_computation.8 | async-start | bytes 3538944 | tf_op jit(solution)/shard_map/reduce_scatter | solution.py:96
  156.3 62.4 %copy-start.2 = (s32[256,1]{0,1:T(1,128)S(1)}, s32[256,1]{0,1:T(1,128)}, u32[]{:S(2)}) copy-start(s32[256,1]{0,1:T(1,128)} %param.12) | copy-start | bytes 3076
  156.3 63.4 %copy-start.3 = (s32[1,256]{1,0:T(1,128)S(1)}, s32[1,256]{1,0:T(1,128)}, u32[]{:S(2)}) copy-start(s32[1,256]{1,0:T(1,128)} %param.11) | copy-start | bytes 3076
  156.4 5.2 %collective-permute-start.3 = (f32[24]{0:T(128)S(1)}, f32[24]{0:T(128)S(1)}, u32[]{:S(2)}, u32[]{:S(2)}) collective-permute-start(f32[24]{0:T(128)S(1)} %get-tuple-element.11), channel_id=1, source_target_pairs={{240,0},{0,16},{16,32},{32,48},{48,64},{64,80},{80,96},{96,112},{1... | collective-permute-start | bytes 296 | tf_op jit(solution)/shard_map/ppermute | solution.py:18
  209.9 29.1 %all-to-all-start.2 = ((f32[16,24,512]{2,1,0:T(8,128)}), f32[16,24,512]{2,1,0:T(8,128)}, u32[]{:S(2)}, u32[]{:S(2)}) async-start(f32[16,24,512]{2,1,0:T(8,128)} %bitcast.85), calls=%async_computation.4 | async-start | bytes 1572864 | tf_op jit(solution)/shard_map/all_to_all | solution.py:99
Sparse Core Ops, SparseCore 0:
  55.4 41.0 all-gather.2
  98.3 22.8 all-gather.4
  135.2 21.1 reduce-scatter.2
  158.9 48.8 reduce-scatter.4

commit v3 on v1

--- a/solution.py
+++ b/solution.py
@@ -46,14 +46,26 @@
     feature_width = rows.shape[1]
     buffer = jnp.dot(placing, rows, preferred_element_type=jnp.float32).astype(jnp.bfloat16)
     buffer = buffer.reshape(expert_count, capacity, feature_width)
-    mine = lax.all_to_all(buffer, "expert", split_axis=0, concat_axis=2, tiled=True)[0]
-
     n_exp_dev = lax.axis_size("expert")
     local_width = router.shape[0]
     tables = jnp.concatenate([norm_gain, router[None, :]], axis=0)
-    tables = jnp.broadcast_to(tables[None], (n_exp_dev,) + tables.shape)
-    tables = lax.all_to_all(tables, "expert", split_axis=0, concat_axis=0, tiled=True)
-    tables = tables.transpose(1, 0, 2).reshape(tables.shape[1], n_exp_dev * local_width)
+    parts = []
+    rest = tables
+    for _ in range(3):
+        piece = rest.astype(jnp.bfloat16)
+        parts.append(piece)
+        rest = rest - piece.astype(jnp.float32)
+    table_rows = tables.shape[0]
+    extra = jnp.broadcast_to(
+        jnp.concatenate(parts, axis=0)[None], (expert_count, 3 * table_rows, local_width)
+    )
+    buffer = jnp.concatenate([buffer, extra], axis=1)
+    mine = lax.all_to_all(buffer, "expert", split_axis=0, concat_axis=2, tiled=True)[0]
+    arrived, mine = lax.optimization_barrier((arrived, mine))
+    coded = mine[capacity:].astype(jnp.float32).reshape(3, table_rows, mine.shape[1])
+    tables = (coded[0] + coded[1]) + coded[2]
+    mine = mine[:capacity]
+
     gains_all = tables[:2]
     router_all = tables[2]
     expert_id = lax.axis_index("expert")
@@ -67,6 +79,7 @@
     score_home = passed_along(score, "section", 1)
 
     block = lax.all_gather(normed, "section", axis=0, tiled=True)
+    block, score_home = lax.optimization_barrier((block, score_home))
     gate = feature_product(block, gate_w[0])
     upper = feature_product(block, up_w[0])
     hidden = (jax.nn.silu(gate) * upper).astype(jnp.bfloat16)
@@ -83,7 +96,7 @@
         scatter_dimension=0,
         tiled=True,
     )
-    update_rows = score_home[:, None] * summed.astype(jnp.float32)
+    update_rows = (score_home[:, None] * summed.astype(jnp.float32)).astype(jnp.bfloat16)
     outgoing = update_rows.reshape(capacity, n_exp_dev, local_width).transpose(1, 0, 2)
     back = lax.all_to_all(outgoing, "expert", split_axis=0, concat_axis=0, tiled=True)
     flat_back = back.reshape(expert_count * capacity, local_width)
@@ -91,7 +104,7 @@
     picks = selected[0]
     experts = routes[:, 0]
     position = experts * capacity + slots_of(experts, expert_count)
-    update = flat_back[position]
+    update = flat_back[position].astype(jnp.float32)
     result = arrived.astype(jnp.float32).at[picks].add(update)
     return result.astype(jnp.bfloat16)
 

time: 236 us -> 220 us (0.932)
  waiting for transfers between devices: 147 us -> 139 us
  local copies, waits for them, and re-layouts: 14.9 us -> 8.05 us
  starting transfers between devices: 26.7 us -> 22.8 us
  other arithmetic: 18 us -> 21.3 us
    ppermute x4, waiting for transfers between devices: 27.1 us -> 5.07 us  [passed_along(): return lax.ppermute(block, axis, route)]
    all_to_all x1, waiting for transfers between devices: 6.07 us -> 21.7 us  [body(): lax.all_to_all(buffer, 'expert', split_axis=0, concat_axis=2, tiled=True)[0]]
    all_to_all x1 -> x0, starting transfers between devices: 10.6 us -> none  [body(): lax.all_to_all(tables, 'expert', split_axis=0, concat_axis=0, tiled=True)]
    all_to_all x1, starting transfers between devices: 3.55 us -> 10.6 us  [body(): lax.all_to_all(buffer, 'expert', split_axis=0, concat_axis=2, tiled=True)[0]]
    all_to_all x1 -> x0, waiting for transfers between devices: 6.55 us -> none  [body(): lax.all_to_all(tables, 'expert', split_axis=0, concat_axis=0, tiled=True)]
    all_to_all x1, waiting for transfers between devices: 0.01 us -> 5.78 us  [body(): lax.all_to_all(outgoing, 'expert', split_axis=0, concat_axis=0, tiled=True)]
    all_gather x1, waiting for transfers between devices: 39 us -> 34.5 us  [body(): block = lax.all_gather(normed, 'section', axis=0, tiled=True)]
    reduce_scatter x1, waiting for transfers between devices: 68.2 us -> 72.2 us  [body(): lax.psum_scatter(lax.optimization_barrier(part.astype(jnp.bfloat16)).asty...]
  transfers between devices with their start and end apart: 9 -> 8, of which waited for: 6 -> 5; matrix products, arithmetic and copies ran while one was open for 8% -> 7% of each run, Pallas kernels for 0% -> 0%
where the time goes in v3:
time: 220 us; the launch traced here: 218 us
  waiting for transfers between devices  139 us (63%)
  starting transfers between devices  22.8 us (10%)
  other arithmetic  21.3 us (10%)
  between operations  13.6 us (6%)
  matrix products  13 us (6%)
  local copies, waits for them, and re-layouts  8.05 us (4%)
    reduce_scatter x1, waiting for transfers between devices, body(): lax.psum_scatter(lax.optimization_barrier(part.astype(jnp.bfloat16)).asty...  72.2 us
    all_gather x1, waiting for transfers between devices, body(): block = lax.all_gather(normed, 'section', axis=0, tiled=True)  34.5 us
    all_to_all x1, waiting for transfers between devices, body(): lax.all_to_all(buffer, 'expert', split_axis=0, concat_axis=2, tiled=True)[0]  21.7 us
    all_to_all x1, starting transfers between devices, body(): lax.all_to_all(buffer, 'expert', split_axis=0, concat_axis=2, tiled=True)[0]  10.6 us
    all_to_all x1, starting transfers between devices, body(): lax.all_to_all(outgoing, 'expert', split_axis=0, concat_axis=0, tiled=True)  9.06 us
    dot_general x2, matrix products, feature_product(): lax.dot_general(block, weight, (((1,), (1,)), ((), ())), preferred_elemen...  8.29 us
    scatter-add x1, other arithmetic, body(): result = arrived.astype(jnp.float32).at[picks].add(update)  6.15 us
    all_to_all x1, waiting for transfers between devices, body(): lax.all_to_all(outgoing, 'expert', split_axis=0, concat_axis=0, tiled=True)  5.78 us
  transfers between devices with their start and end apart: 8, of which 5 were waited for; matrix products, arithmetic and copies ran while one was open for 7% of the time, Pallas kernels for 0%

profile of v3, /device:TPU:8, one launch (start us, length us, event | category | flops | bytes accessed | tf_op | source)
XLA Modules:
  0.0 218.1 jit_solution(9796705658998784671)
XLA Ops:
  6.5 2.1 collective-permute-start.1
  8.6 0.7 collective-permute-start.2
  9.3 0.7 fusion.20
  10.0 0.7 fusion.19
  10.8 0.6 reduce-window.14
  11.4 0.2 slice_reduce_fusion.1
  11.6 0.1 fusion.16
  11.7 2.6 %gather_fusion = bf16[256,512]{1,0:T(8,128)(2,1)S(1)} fusion(bf16[1024,512]{1,0:T(8,128)(2,1)} %param.9, s32[1024]{0:T(1024)S(1)} %pad_clamp_fusion.1), kind=kCustom, calls=%fused_computation | custom fusion | bytes 525312 | tf_op jit(solution)/shard_map/gather | solution.py:41
  14.3 0.3 convolution_convert_fusion.1
  14.6 0.9 pad_maximum_fusion
  15.5 10.6 %all-to-all-start = ((bf16[16,33,512]{2,1,0:T(8,128)(2,1)}), bf16[16,33,512]{2,1,0:T(8,128)(2,1)}, u32[]{:S(2)}, u32[]{:S(2)}) async-start(bf16[16,33,512]{2,1,0:T(8,128)(2,1)} %pad_maximum_fusion), calls=%async_computation | async-start | bytes 1310720 | tf_op jit(solution)/shard_map/all_to_all | solution.py:63
  26.2 0.0 all-gather.2.cloned.1.call-start
  26.2 21.7 %all-to-all-done = bf16[16,33,512]{2,1,0:T(8,128)(2,1)} async-done(((bf16[16,33,512]{2,1,0:T(8,128)(2,1)}), bf16[16,33,512]{2,1,0:T(8,128)(2,1)}, u32[]{:S(2)}, u32[]{:S(2)}) %all-to-all-start) | async-done | bytes 540704 | tf_op jit(solution)/shard_map/all_to_all | solution.py:63
  47.9 1.3 copy.31
  49.2 0.1 pad.11
  49.2 0.4 copy.26
  49.7 0.1 slice_add_fusion
  49.9 0.3 fusion.9
  50.2 0.9 fusion.7
  51.1 0.0 reduce-scatter.2.cloned.1.call-start
  51.2 0.3 collective-permute-start.3
  51.4 5.1 %collective-permute-done.3 = f32[24]{0:T(128)S(1)} collective-permute-done((f32[24]{0:T(128)S(1)}, f32[24]{0:T(128)S(1)}, u32[]{:S(2)}, u32[]{:S(2)}) %collective-permute-start.3) | collective-permute-done | bytes 128 | tf_op jit(solution)/shard_map/ppermute | solution.py:13
  56.5 34.5 %all-gather.2.cloned.1.call-done = bf16[384,8192]{1,0:T(8,128)(2,1)} async-done(((bf16[24,8192]{1,0:T(8,128)(2,1)}), bf16[384,8192]{1,0:T(8,128)(2,1)}) %all-gather.2.cloned.1.call-update) | async-done | bytes 6291472 | tf_op jit(solution)/shard_map/all_gather | solution.py:81
  91.0 6.1 %fusion.3 = f32[384,192]{0,1:T(8,128)S(1)} fusion(bf16[384,8192]{1,0:T(8,128)(2,1)} %all-gather.2.cloned.1.call-done, bf16[1,192,8192]{2,1,0:T(8,128)(2,1)} %param.14), kind=kOutput, calls=%fused_computation.7 | convolution fusion | flops 1207959552 | bytes 9732096 | tf_op jit(solution)/shard_map/dot_general | solution.py:17
  97.1 0.3 copy-done.3
  97.5 2.2 %multiply_convert_fusion.1 = bf16[384,192]{0,1:T(8,128)(2,1)S(1)} fusion(f32[384,192]{0,1:T(8,128)S(1)} %fusion.3, bf16[384,8192]{1,0:T(8,128)(2,1)S(1)} %copy-done.2, bf16[1,192,8192]{2,1,0:T(8,128)(2,1)S(1)} %copy-done.3), kind=kOutput, calls=%fused_computation.25 | convolution fusion | flops 1208401920 | bytes 9879552 | tf_op jit(solution)/shard_map/dot_general | solution.py:17
  99.7 0.1 slice_bitcast_fusion
  99.8 0.1 copy.19
  99.9 0.1 copy.20
  100.0 0.1 pad_maximum_fusion.1
  100.1 4.5 %convolution_convert_fusion = bf16[384,8192]{1,0:T(8,128)(2,1)} fusion(bf16[384,192]{1,0:T(8,128)(2,1)S(1)} %bitcast.92, bf16[1,192,8192]{2,1,0:T(8,128)(2,1)S(1)} %copy-done), kind=kOutput, calls=%fused_computation.3 | convolution fusion | flops 1211105280 | bytes 9584640 | tf_op jit(solution)/shard_map/dot_general | solution.py:90
  104.5 0.0 reduce-scatter.2.cloned.1.call-update
  104.6 0.7 copy-done.1
  105.2 0.6 reduce-window.16
  105.8 72.2 %reduce-scatter.2.cloned.1.call-done = bf16[24,8192]{1,0:T(8,128)(2,1)} async-done(((bf16[384,8192]{1,0:T(8,128)(2,1)}), bf16[24,8192]{1,0:T(8,128)(2,1)}) %reduce-scatter.2.cloned.1.call-update) | async-done | bytes 393232 | tf_op jit(solution)/shard_map/reduce_scatter | solution.py:91
  177.9 1.1 multiply_convert_fusion
  179.1 0.8 copy.32
  179.9 9.1 %all-to-all-start.1 = ((bf16[16,24,512]{2,1,0:T(8,128)(2,1)}), bf16[16,24,512]{2,1,0:T(8,128)(2,1)S(1)}, u32[]{:S(2)}, u32[]{:S(2)}) async-start(bf16[16,24,512]{2,1,0:T(8,128)(2,1)} %bitcast.89), calls=%async_computation.2 | async-start | bytes 786432 | tf_op jit(solution)/shard_map/all_to_all | solution.py:101
  188.9 0.8 slice_reduce_fusion
  189.7 1.3 reduce-window.19
  191.0 0.7 slice.64
  191.6 0.8 fusion.14
  192.4 0.7 compare_select_fusion
  193.1 0.7 compare_select_fusion.1
  193.8 2.9 %convert_element_type.71 = f32[1024,512]{1,0:T(8,128)} convert(bf16[1024,512]{1,0:T(8,128)(2,1)} %collective-permute-done) | non-fusion elementwise | flops 524288 | bytes 3145728 | tf_op jit(solution)/shard_map/convert_element_type | solution.py:108
  196.6 5.8 %all-to-all-done.1 = bf16[16,24,512]{2,1,0:T(8,128)(2,1)S(1)} async-done(((bf16[16,24,512]{2,1,0:T(8,128)(2,1)}), bf16[16,24,512]{2,1,0:T(8,128)(2,1)S(1)}, u32[]{:S(2)}, u32[]{:S(2)}) %all-to-all-start.1) | async-done | bytes 393248 | tf_op jit(solution)/shard_map/all_to_all | solution.py:101
  202.4 6.2 %scatter_custom_fusion = f32[1024,512]{1,0:T(8,128)} fusion(f32[1024,512]{1,0:T(8,128)} %convert_element_type.71, s32[256]{0:T(256)S(1)} %bitcast.108, bf16[384,512]{1,0:T(8,128)(2,1)S(1)} %bitcast.88, s32[1024]{0:T(1024)S(1)} %pad_clamp_fusion), kind=kCustom, calls=%fused_computation.21 | custom fusion | flops 262144 | bytes 2494464 | tf_op jit(solution)/shard_map/scatter-add | solution.py:108
  208.6 2.7 %convert_element_type.82 = bf16[1024,512]{1,0:T(8,128)(2,1)} convert(f32[1024,512]{1,0:T(8,128)} %scatter_custom_fusion) | non-fusion elementwise | flops 524288 | bytes 3145728 | tf_op jit(solution)/shard_map/convert_element_type | solution.py:109
  (26 shorter events, 0.3 us)
Async XLA Ops:
  6.5 93.5 %copy-start = (bf16[1,192,8192]{2,1,0:T(8,128)(2,1)S(1)}, bf16[1,192,8192]{2,1,0:T(8,128)(2,1)}, u32[]{:S(2)}) copy-start(bf16[1,192,8192]{2,1,0:T(8,128)(2,1)} %param.16) | copy-start | bytes 9437188
  6.5 4.2 %collective-permute-start.1 = (s32[256,1]{0,1:T(1,128)}, s32[256,1]{0,1:T(1,128)S(1)}, u32[]{:S(2)}, u32[]{:S(2)}) collective-permute-start(s32[256,1]{0,1:T(1,128)} %param.11), channel_id=1, source_target_pairs={{16,0},{32,16},{48,32},{64,48},{80,64},{96,80},{112,96},{128,112},... | collective-permute-start | bytes 3080 | tf_op jit(solution)/shard_map/ppermute | solution.py:13
  8.6 3.1 %collective-permute-start.2 = (s32[1,256]{1,0:T(1,128)}, s32[1,256]{1,0:T(1,128)S(1)}, u32[]{:S(2)}, u32[]{:S(2)}) collective-permute-start(s32[1,256]{1,0:T(1,128)} %param.10), channel_id=1, source_target_pairs={{16,0},{32,16},{48,32},{64,48},{80,64},{96,80},{112,96},{128,112},... | collective-permute-start | bytes 3080 | tf_op jit(solution)/shard_map/ppermute | solution.py:13
  9.3 40.3 %collective-permute-start = (bf16[1024,512]{1,0:T(8,128)(2,1)}, bf16[1024,512]{1,0:T(8,128)(2,1)}, u32[]{:S(2)}, u32[]{:S(2)}) collective-permute-start(bf16[1024,512]{1,0:T(8,128)(2,1)} %param.9), channel_id=1, source_target_pairs={{240,0},{0,16},{16,32},{32,48},{48,64},{64,80},{80,96},{96,112},{1... | collective-permute-start | bytes 3145736 | tf_op jit(solution)/shard_map/ppermute | solution.py:13
  15.5 32.4 %all-to-all-start = ((bf16[16,33,512]{2,1,0:T(8,128)(2,1)}), bf16[16,33,512]{2,1,0:T(8,128)(2,1)}, u32[]{:S(2)}, u32[]{:S(2)}) async-start(bf16[16,33,512]{2,1,0:T(8,128)(2,1)} %pad_maximum_fusion), calls=%async_computation | async-start | bytes 1310720 | tf_op jit(solution)/shard_map/all_to_all | solution.py:63
  26.2 64.9 %all-gather.2.cloned.1.call-start = ((), (), s32[]{:S(2)}) async-start(), calls=%async_computation.3 | async-start | bytes 6684672 | tf_op jit(solution)/shard_map/all_gather | solution.py:81
  51.1 126.8 %reduce-scatter.2.cloned.1.call-start = ((), (), s32[]{:S(2)}) async-start(), calls=%async_computation.4 | async-start | bytes 6684672 | tf_op jit(solution)/shard_map/reduce_scatter | solution.py:91
  51.2 5.3 %collective-permute-start.3 = (f32[24]{0:T(128)S(1)}, f32[24]{0:T(128)S(1)}, u32[]{:S(2)}, u32[]{:S(2)}) collective-permute-start(f32[24]{0:T(128)S(1)} %get-tuple-element.17), channel_id=1, source_target_pairs={{240,0},{0,16},{16,32},{32,48},{48,64},{64,80},{80,96},{96,112},{1... | collective-permute-start | bytes 296 | tf_op jit(solution)/shard_map/ppermute | solution.py:13
  91.0 6.1 %copy-start.2 = (bf16[384,8192]{1,0:T(8,128)(2,1)S(1)}, bf16[384,8192]{1,0:T(8,128)(2,1)}, u32[]{:S(2)}) copy-start(bf16[384,8192]{1,0:T(8,128)(2,1)} %all-gather.2.cloned.1.call-done) | copy-start | bytes 18874372
  91.0 6.4 %copy-start.3 = (bf16[1,192,8192]{2,1,0:T(8,128)(2,1)S(1)}, bf16[1,192,8192]{2,1,0:T(8,128)(2,1)}, u32[]{:S(2)}) copy-start(bf16[1,192,8192]{2,1,0:T(8,128)(2,1)} %param.15) | copy-start | bytes 9437188
  104.5 0.7 copy-start.1
  179.9 22.6 %all-to-all-start.1 = ((bf16[16,24,512]{2,1,0:T(8,128)(2,1)}), bf16[16,24,512]{2,1,0:T(8,128)(2,1)S(1)}, u32[]{:S(2)}, u32[]{:S(2)}) async-start(bf16[16,24,512]{2,1,0:T(8,128)(2,1)} %bitcast.89), calls=%async_computation.2 | async-start | bytes 786432 | tf_op jit(solution)/shard_map/all_to_all | solution.py:101
Sparse Core Ops, SparseCore 0:
  51.2 39.7 all-gather.1
  104.7 73.2 reduce-scatter.1

commit v4 on v3

--- a/solution.py
+++ b/solution.py
@@ -88,14 +88,14 @@
         groups * capacity, hidden_width
     )
     part = jnp.dot(hidden, down_w[0], preferred_element_type=jnp.float32)
-    summed = lax.psum_scatter(
-        lax.optimization_barrier(part.astype(jnp.bfloat16))
-        .astype(jnp.float32)
-        .astype(jnp.bfloat16),
+    parts_in = lax.all_to_all(
+        part.astype(jnp.bfloat16).reshape(groups, capacity, part.shape[1]),
         "section",
-        scatter_dimension=0,
+        split_axis=0,
+        concat_axis=0,
         tiled=True,
     )
+    summed = jnp.sum(parts_in.astype(jnp.float32), axis=0).astype(jnp.bfloat16)
     update_rows = (score_home[:, None] * summed.astype(jnp.float32)).astype(jnp.bfloat16)
     outgoing = update_rows.reshape(capacity, n_exp_dev, local_width).transpose(1, 0, 2)
     back = lax.all_to_all(outgoing, "expert", split_axis=0, concat_axis=0, tiled=True)

time: 220 us -> 243 us (1.10)
  waiting for transfers between devices: 139 us -> 153 us
  starting transfers between devices: 22.8 us -> 27.8 us
  other arithmetic: 21.3 us -> 24.8 us
    all_to_all x0 -> x1, waiting for transfers between devices: none -> 83.6 us  [body(): lax.all_to_all(part.astype(jnp.bfloat16).reshape(groups, capacity, part.s...]
    reduce_scatter x1 -> x0, waiting for transfers between devices: 72.2 us -> none  [body(): lax.psum_scatter(lax.optimization_barrier(part.astype(jnp.bfloat16)).asty...]
    all_to_all x0 -> x1, starting transfers between devices: none -> 5.57 us  [body(): lax.all_to_all(part.astype(jnp.bfloat16).reshape(groups, capacity, part.s...]
    reduce_sum x0 -> x1, other arithmetic: none -> 3.88 us  [body(): summed = jnp.sum(parts_in.astype(jnp.float32), axis=0).astype(jnp.bfloat16)]
    all_to_all x1, waiting for transfers between devices: 5.78 us -> 8.21 us  [body(): lax.all_to_all(outgoing, 'expert', split_axis=0, concat_axis=0, tiled=True)]
where the time goes in v4:
time: 243 us; the launch traced here: 240 us
  waiting for transfers between devices  153 us (63%)
  starting transfers between devices  27.8 us (11%)
  other arithmetic  24.8 us (10%)
  between operations  13.6 us (6%)
  matrix products  13 us (5%)
  local copies, waits for them, and re-layouts  7.73 us (3%)
    all_to_all x1, waiting for transfers between devices, body(): lax.all_to_all(part.astype(jnp.bfloat16).reshape(groups, capacity, part.s...  83.6 us
    all_gather x1, waiting for transfers between devices, body(): block = lax.all_gather(normed, 'section', axis=0, tiled=True)  34.7 us
    all_to_all x1, waiting for transfers between devices, body(): lax.all_to_all(buffer, 'expert', split_axis=0, concat_axis=2, tiled=True)[0]  21.7 us
    all_to_all x1, starting transfers between devices, body(): lax.all_to_all(buffer, 'expert', split_axis=0, concat_axis=2, tiled=True)[0]  10.6 us
    all_to_all x1, starting transfers between devices, body(): lax.all_to_all(outgoing, 'expert', split_axis=0, concat_axis=0, tiled=True)  8.67 us
    dot_general x2, matrix products, feature_product(): lax.dot_general(block, weight, (((1,), (1,)), ((), ())), preferred_elemen...  8.29 us
    all_to_all x1, waiting for transfers between devices, body(): lax.all_to_all(outgoing, 'expert', split_axis=0, concat_axis=0, tiled=True)  8.21 us
    scatter-add x1, other arithmetic, body(): result = arrived.astype(jnp.float32).at[picks].add(update)  6.15 us
  transfers between devices with their start and end apart: 8, of which 5 were waited for; matrix products, arithmetic and copies ran while one was open for 7% of the time, Pallas kernels for 0%

profile of v4, /device:TPU:8, one launch (start us, length us, event | category | flops | bytes accessed | tf_op | source)
XLA Modules:
  0.0 240.3 jit_solution(9934175087993221117)
XLA Ops:
  6.5 2.1 collective-permute-start.1
  8.6 0.7 collective-permute-start.2
  9.3 0.7 fusion.21
  10.0 0.7 fusion.20
  10.8 0.6 reduce-window.14
  11.4 0.2 slice_reduce_fusion.1
  11.6 0.1 fusion.17
  11.7 2.6 %gather_fusion = bf16[256,512]{1,0:T(8,128)(2,1)S(1)} fusion(bf16[1024,512]{1,0:T(8,128)(2,1)} %param.9, s32[1024]{0:T(1024)S(1)} %pad_clamp_fusion.1), kind=kCustom, calls=%fused_computation | custom fusion | bytes 525312 | tf_op jit(solution)/shard_map/gather | solution.py:41
  14.3 0.3 convolution_convert_fusion.1
  14.6 0.9 pad_maximum_fusion
  15.5 10.6 %all-to-all-start = ((bf16[16,33,512]{2,1,0:T(8,128)(2,1)}), bf16[16,33,512]{2,1,0:T(8,128)(2,1)}, u32[]{:S(2)}, u32[]{:S(2)}) async-start(bf16[16,33,512]{2,1,0:T(8,128)(2,1)} %pad_maximum_fusion), calls=%async_computation | async-start | bytes 1310720 | tf_op jit(solution)/shard_map/all_to_all | solution.py:63
  26.2 0.0 all-gather.2.cloned.1.call-start
  26.2 21.7 %all-to-all-done = bf16[16,33,512]{2,1,0:T(8,128)(2,1)} async-done(((bf16[16,33,512]{2,1,0:T(8,128)(2,1)}), bf16[16,33,512]{2,1,0:T(8,128)(2,1)}, u32[]{:S(2)}, u32[]{:S(2)}) %all-to-all-start) | async-done | bytes 540704 | tf_op jit(solution)/shard_map/all_to_all | solution.py:63
  47.9 1.3 copy.29
  49.2 0.1 pad.11
  49.2 0.4 copy.24
  49.7 0.1 slice_add_fusion
  49.9 0.3 fusion.9
  50.2 0.9 fusion.7
  51.1 0.1 collective-permute-start.3
  51.2 5.2 %collective-permute-done.3 = f32[24]{0:T(128)} collective-permute-done((f32[24]{0:T(128)S(1)}, f32[24]{0:T(128)}, u32[]{:S(2)}, u32[]{:S(2)}) %collective-permute-start.3) | collective-permute-done | bytes 128 | tf_op jit(solution)/shard_map/ppermute | solution.py:13
  56.4 34.7 %all-gather.2.cloned.1.call-done = bf16[384,8192]{1,0:T(8,128)(2,1)} async-done(((bf16[24,8192]{1,0:T(8,128)(2,1)}), bf16[384,8192]{1,0:T(8,128)(2,1)}) %all-gather.2.cloned.1.call-update) | async-done | bytes 6291472 | tf_op jit(solution)/shard_map/all_gather | solution.py:81
  91.0 6.1 %fusion.3 = f32[384,192]{0,1:T(8,128)S(1)} fusion(bf16[384,8192]{1,0:T(8,128)(2,1)} %all-gather.2.cloned.1.call-done, bf16[1,192,8192]{2,1,0:T(8,128)(2,1)} %param.14), kind=kOutput, calls=%fused_computation.7 | convolution fusion | flops 1207959552 | bytes 9732096 | tf_op jit(solution)/shard_map/dot_general | solution.py:17
  97.1 0.3 copy-done.3
  97.5 2.2 multiply_convert_fusion
  99.7 0.1 slice_bitcast_fusion
  99.8 0.1 copy.18
  99.9 0.1 copy.19
  100.0 0.1 pad_maximum_fusion.1
  100.1 4.5 %convolution_convert_fusion = bf16[384,8192]{1,0:T(8,128)(2,1)} fusion(bf16[384,192]{1,0:T(8,128)(2,1)S(1)} %bitcast.94, bf16[1,192,8192]{2,1,0:T(8,128)(2,1)S(1)} %copy-done), kind=kOutput, calls=%fused_computation.3 | convolution fusion | flops 1211105280 | bytes 9584640 | tf_op jit(solution)/shard_map/dot_general | solution.py:90
  104.5 5.6 %all-to-all-start.1 = ((bf16[16,24,8192]{2,1,0:T(8,128)(2,1)}), bf16[16,24,8192]{2,1,0:T(8,128)(2,1)}, u32[]{:S(2)}, u32[]{:S(2)}) async-start(bf16[16,24,8192]{2,1,0:T(8,128)(2,1)} %bitcast.84), calls=%async_computation.1 | async-start | bytes 12582912 | tf_op jit(solution)/shard_map/all_to_all | solution.py:91
  110.1 0.6 reduce-window.16
  110.7 83.6 %all-to-all-done.1 = bf16[16,24,8192]{2,1,0:T(8,128)(2,1)} async-done(((bf16[16,24,8192]{2,1,0:T(8,128)(2,1)}), bf16[16,24,8192]{2,1,0:T(8,128)(2,1)}, u32[]{:S(2)}, u32[]{:S(2)}) %all-to-all-start.1) | async-done | bytes 6291488 | tf_op jit(solution)/shard_map/all_to_all | solution.py:91
  194.3 3.9 %reduce_sum.53 = bf16[24,8192]{1,0:T(8,128)(2,1)S(1)} reduce(bf16[16,24,8192]{2,1,0:T(8,128)(2,1)} %all-to-all-done.1, bf16[]{:T(256)} %constant.41.clone.1), dimensions={0}, to_apply=%region_5.6 | reduce | flops 2949120 | bytes 6684674 | tf_op jit(solution)/shard_map/reduce_sum | solution.py:98
  198.2 0.1 copy.25
  198.3 0.7 fusion.10
  199.0 1.0 copy.20
  200.0 8.7 %all-to-all-start.2 = ((bf16[16,24,512]{2,1,0:T(8,128)(2,1)}), bf16[16,24,512]{2,1,0:T(8,128)(2,1)S(1)}, u32[]{:S(2)}, u32[]{:S(2)}) async-start(bf16[16,24,512]{2,1,0:T(8,128)(2,1)} %copy.20), calls=%async_computation.2 | async-start | bytes 786432 | tf_op jit(solution)/shard_map/all_to_all | solution.py:101
  208.7 0.8 slice_reduce_fusion
  209.4 1.3 reduce-window.19
  210.7 0.7 slice.64
  211.4 0.8 fusion.15
  212.2 0.7 compare_select_fusion
  212.9 0.7 compare_select_fusion.1
  213.5 2.9 %convert_element_type.76 = f32[1024,512]{1,0:T(8,128)} convert(bf16[1024,512]{1,0:T(8,128)(2,1)} %collective-permute-done) | non-fusion elementwise | flops 524288 | bytes 3145728 | tf_op jit(solution)/shard_map/convert_element_type | solution.py:108
  216.4 8.2 %all-to-all-done.2 = bf16[16,24,512]{2,1,0:T(8,128)(2,1)S(1)} async-done(((bf16[16,24,512]{2,1,0:T(8,128)(2,1)}), bf16[16,24,512]{2,1,0:T(8,128)(2,1)S(1)}, u32[]{:S(2)}, u32[]{:S(2)}) %all-to-all-start.2) | async-done | bytes 393248 | tf_op jit(solution)/shard_map/all_to_all | solution.py:101
  224.6 6.2 %scatter_custom_fusion = f32[1024,512]{1,0:T(8,128)} fusion(f32[1024,512]{1,0:T(8,128)} %convert_element_type.76, s32[256]{0:T(256)S(1)} %bitcast.110, bf16[384,512]{1,0:T(8,128)(2,1)S(1)} %bitcast.90, s32[1024]{0:T(1024)S(1)} %pad_clamp_fusion), kind=kCustom, calls=%fused_computation.22 | custom fusion | flops 262144 | bytes 2494464 | tf_op jit(solution)/shard_map/scatter-add | solution.py:108
  230.8 2.7 %convert_element_type.88 = bf16[1024,512]{1,0:T(8,128)(2,1)} convert(f32[1024,512]{1,0:T(8,128)} %scatter_custom_fusion) | non-fusion elementwise | flops 524288 | bytes 3145728 | tf_op jit(solution)/shard_map/convert_element_type | solution.py:109
  (27 shorter events, 0.3 us)
Async XLA Ops:
  6.5 93.5 %copy-start = (bf16[1,192,8192]{2,1,0:T(8,128)(2,1)S(1)}, bf16[1,192,8192]{2,1,0:T(8,128)(2,1)}, u32[]{:S(2)}) copy-start(bf16[1,192,8192]{2,1,0:T(8,128)(2,1)} %param.16) | copy-start | bytes 9437188
  6.5 4.2 %collective-permute-start.1 = (s32[256,1]{0,1:T(1,128)}, s32[256,1]{0,1:T(1,128)S(1)}, u32[]{:S(2)}, u32[]{:S(2)}) collective-permute-start(s32[256,1]{0,1:T(1,128)} %param.11), channel_id=1, source_target_pairs={{16,0},{32,16},{48,32},{64,48},{80,64},{96,80},{112,96},{128,112},... | collective-permute-start | bytes 3080 | tf_op jit(solution)/shard_map/ppermute | solution.py:13
  8.6 3.1 %collective-permute-start.2 = (s32[1,256]{1,0:T(1,128)}, s32[1,256]{1,0:T(1,128)S(1)}, u32[]{:S(2)}, u32[]{:S(2)}) collective-permute-start(s32[1,256]{1,0:T(1,128)} %param.10), channel_id=1, source_target_pairs={{16,0},{32,16},{48,32},{64,48},{80,64},{96,80},{112,96},{128,112},... | collective-permute-start | bytes 3080 | tf_op jit(solution)/shard_map/ppermute | solution.py:13
  9.3 40.3 %collective-permute-start = (bf16[1024,512]{1,0:T(8,128)(2,1)}, bf16[1024,512]{1,0:T(8,128)(2,1)}, u32[]{:S(2)}, u32[]{:S(2)}) collective-permute-start(bf16[1024,512]{1,0:T(8,128)(2,1)} %param.9), channel_id=1, source_target_pairs={{240,0},{0,16},{16,32},{32,48},{48,64},{64,80},{80,96},{96,112},{1... | collective-permute-start | bytes 3145736 | tf_op jit(solution)/shard_map/ppermute | solution.py:13
  15.5 32.4 %all-to-all-start = ((bf16[16,33,512]{2,1,0:T(8,128)(2,1)}), bf16[16,33,512]{2,1,0:T(8,128)(2,1)}, u32[]{:S(2)}, u32[]{:S(2)}) async-start(bf16[16,33,512]{2,1,0:T(8,128)(2,1)} %pad_maximum_fusion), calls=%async_computation | async-start | bytes 1310720 | tf_op jit(solution)/shard_map/all_to_all | solution.py:63
  26.2 64.9 %all-gather.2.cloned.1.call-start = ((), (), s32[]{:S(2)}) async-start(), calls=%async_computation.3 | async-start | bytes 6684672 | tf_op jit(solution)/shard_map/all_gather | solution.py:81
  51.1 5.3 %collective-permute-start.3 = (f32[24]{0:T(128)S(1)}, f32[24]{0:T(128)}, u32[]{:S(2)}, u32[]{:S(2)}) collective-permute-start(f32[24]{0:T(128)S(1)} %get-tuple-element.17), channel_id=1, source_target_pairs={{240,0},{0,16},{16,32},{32,48},{48,64},{64,80},{80,96},{96,112},{1... | collective-permute-start | bytes 296 | tf_op jit(solution)/shard_map/ppermute | solution.py:13
  91.0 6.1 %copy-start.2 = (bf16[384,8192]{1,0:T(8,128)(2,1)S(1)}, bf16[384,8192]{1,0:T(8,128)(2,1)}, u32[]{:S(2)}) copy-start(bf16[384,8192]{1,0:T(8,128)(2,1)} %all-gather.2.cloned.1.call-done) | copy-start | bytes 18874372
  91.0 6.4 %copy-start.3 = (bf16[1,192,8192]{2,1,0:T(8,128)(2,1)S(1)}, bf16[1,192,8192]{2,1,0:T(8,128)(2,1)}, u32[]{:S(2)}) copy-start(bf16[1,192,8192]{2,1,0:T(8,128)(2,1)} %param.15) | copy-start | bytes 9437188
  104.5 5.6 %copy-start.1 = (s32[256,1]{0,1:T(1,128)S(1)}, s32[256,1]{0,1:T(1,128)}, u32[]{:S(2)}) copy-start(s32[256,1]{0,1:T(1,128)} %param.11) | copy-start | bytes 3076
  104.5 89.8 %all-to-all-start.1 = ((bf16[16,24,8192]{2,1,0:T(8,128)(2,1)}), bf16[16,24,8192]{2,1,0:T(8,128)(2,1)}, u32[]{:S(2)}, u32[]{:S(2)}) async-start(bf16[16,24,8192]{2,1,0:T(8,128)(2,1)} %bitcast.84), calls=%async_computation.1 | async-start | bytes 12582912 | tf_op jit(solution)/shard_map/all_to_all | solution.py:91
  200.0 24.6 %all-to-all-start.2 = ((bf16[16,24,512]{2,1,0:T(8,128)(2,1)}), bf16[16,24,512]{2,1,0:T(8,128)(2,1)S(1)}, u32[]{:S(2)}, u32[]{:S(2)}) async-start(bf16[16,24,512]{2,1,0:T(8,128)(2,1)} %copy.20), calls=%async_computation.2 | async-start | bytes 786432 | tf_op jit(solution)/shard_map/all_to_all | solution.py:101
Sparse Core Ops, SparseCore 0:
  51.2 39.7 all-gather.1

commit v5 on v4

--- a/solution.py
+++ b/solution.py
@@ -78,24 +78,31 @@
     score = jax.nn.sigmoid(scale * jnp.sum(picked * gains[None, :] * router_all[None, :], axis=1))
     score_home = passed_along(score, "section", 1)
 
-    block = lax.all_gather(normed, "section", axis=0, tiled=True)
-    block, score_home = lax.optimization_barrier((block, score_home))
-    gate = feature_product(block, gate_w[0])
-    upper = feature_product(block, up_w[0])
+    half = d // 2
+    block_a = lax.all_gather(normed[:, :half], "section", axis=0, tiled=True)
+    block_b = lax.all_gather(normed[:, half:], "section", axis=0, tiled=True)
+    block_a, score_home = lax.optimization_barrier((block_a, score_home))
+    gate = feature_product(block_a, gate_w[0, :, :half]) + feature_product(block_b, gate_w[0, :, half:])
+    upper = feature_product(block_a, up_w[0, :, :half]) + feature_product(block_b, up_w[0, :, half:])
     hidden = (jax.nn.silu(gate) * upper).astype(jnp.bfloat16)
     hidden_width = hidden.shape[1]
     hidden = jnp.roll(hidden.reshape(groups, capacity, hidden_width), 1, axis=0).reshape(
         groups * capacity, hidden_width
     )
-    part = jnp.dot(hidden, down_w[0], preferred_element_type=jnp.float32)
-    parts_in = lax.all_to_all(
-        part.astype(jnp.bfloat16).reshape(groups, capacity, part.shape[1]),
-        "section",
-        split_axis=0,
-        concat_axis=0,
-        tiled=True,
-    )
-    summed = jnp.sum(parts_in.astype(jnp.float32), axis=0).astype(jnp.bfloat16)
+    pieces = []
+    for columns in (slice(0, half), slice(half, d)):
+        part = jnp.dot(hidden, down_w[0, :, columns], preferred_element_type=jnp.float32)
+        pieces.append(
+            lax.psum_scatter(
+                lax.optimization_barrier(part.astype(jnp.bfloat16))
+                .astype(jnp.float32)
+                .astype(jnp.bfloat16),
+                "section",
+                scatter_dimension=0,
+                tiled=True,
+            )
+        )
+    summed = jnp.concatenate(pieces, axis=1)
     update_rows = (score_home[:, None] * summed.astype(jnp.float32)).astype(jnp.bfloat16)
     outgoing = update_rows.reshape(capacity, n_exp_dev, local_width).transpose(1, 0, 2)
     back = lax.all_to_all(outgoing, "expert", split_axis=0, concat_axis=0, tiled=True)

time: 243 us -> 311 us (1.28)
  waiting for transfers between devices: 153 us -> 239 us
  other arithmetic: 24.8 us -> 10.8 us
  starting transfers between devices: 27.8 us -> 22.7 us
    reduce_scatter x0 -> x2, waiting for transfers between devices: none -> 131 us  [body(): lax.psum_scatter(lax.optimization_barrier(part.astype(jnp.bfloat16)).asty...]
    all_to_all x1 -> x0, waiting for transfers between devices: 83.6 us -> none  [body(): lax.all_to_all(part.astype(jnp.bfloat16).reshape(groups, capacity, part.s...]
    all_gather x1 -> x2, waiting for transfers between devices: 34.7 us -> 67.1 us  [the longest x1 40.4 us: body(): block_b = lax.all_gather(normed[:, half:], 'section', axis=0, tiled=True)]
    all_to_all x1 -> x0, starting transfers between devices: 5.57 us -> none  [body(): lax.all_to_all(part.astype(jnp.bfloat16).reshape(groups, capacity, part.s...]
    all_to_all x1, waiting for transfers between devices: 8.21 us -> 12.8 us  [body(): lax.all_to_all(outgoing, 'expert', split_axis=0, concat_axis=0, tiled=True)]
    reduce_sum x1 -> x0, other arithmetic: 3.88 us -> none  [body(): summed = jnp.sum(parts_in.astype(jnp.float32), axis=0).astype(jnp.bfloat16)]
    dot_general x2 -> x4, matrix products: 8.29 us -> 9.33 us  [feature_product(): lax.dot_general(block, weight, (((1,), (1,)), ((), ())), preferred_elemen...]
  transfers between devices with their start and end apart: 8 -> 10, of which waited for: 5 -> 7; matrix products, arithmetic and copies ran while one was open for 7% -> 4% of each run, Pallas kernels for 0% -> 0%
where the time goes in v5:
time: 311 us; the launch traced here: 308 us
  waiting for transfers between devices  239 us (77%)
  starting transfers between devices  22.7 us (7%)
  matrix products  14.9 us (5%)
  between operations  13.5 us (4%)
  other arithmetic  10.8 us (3%)
  local copies, waits for them, and re-layouts  7.66 us (2%)
    reduce_scatter x2, waiting for transfers between devices, body(): lax.psum_scatter(lax.optimization_barrier(part.astype(jnp.bfloat16)).asty...  131 us
    all_gather x1, waiting for transfers between devices, body(): block_b = lax.all_gather(normed[:, half:], 'section', axis=0, tiled=True)  40.4 us
    all_gather x1, waiting for transfers between devices, body(): block_a = lax.all_gather(normed[:, :half], 'section', axis=0, tiled=True)  26.7 us
    all_to_all x1, waiting for transfers between devices, body(): lax.all_to_all(buffer, 'expert', split_axis=0, concat_axis=2, tiled=True)[0]  21.7 us
    all_to_all x1, waiting for transfers between devices, body(): lax.all_to_all(outgoing, 'expert', split_axis=0, concat_axis=0, tiled=True)  12.8 us
    all_to_all x1, starting transfers between devices, body(): lax.all_to_all(buffer, 'expert', split_axis=0, concat_axis=2, tiled=True)[0]  10.6 us
    dot_general x4, matrix products, feature_product(): lax.dot_general(block, weight, (((1,), (1,)), ((), ())), preferred_elemen...  9.33 us
    all_to_all x1, starting transfers between devices, body(): lax.all_to_all(outgoing, 'expert', split_axis=0, concat_axis=0, tiled=True)  8.92 us
  transfers between devices with their start and end apart: 10, of which 7 were waited for; matrix products, arithmetic and copies ran while one was open for 4% of the time, Pallas kernels for 0%

profile of v5, /device:TPU:8, one launch (start us, length us, event | category | flops | bytes accessed | tf_op | source)
XLA Modules:
  0.0 308.4 jit_solution(3256144085192003870)
XLA Ops:
  6.5 2.1 collective-permute-start.1
  8.6 0.7 collective-permute-start.2
  9.3 0.7 fusion.38
  10.0 0.7 fusion.37
  10.8 0.6 reduce-window.14
  11.4 0.2 slice_reduce_fusion.1
  11.6 0.1 fusion.34
  11.7 2.6 gather_fusion
  14.3 0.3 convolution_convert_fusion.2
  14.6 0.9 pad_maximum_fusion
  15.5 10.6 %all-to-all-start = ((bf16[16,33,512]{2,1,0:T(8,128)(2,1)}), bf16[16,33,512]{2,1,0:T(8,128)(2,1)S(1)}, u32[]{:S(2)}, u32[]{:S(2)}) async-start(bf16[16,33,512]{2,1,0:T(8,128)(2,1)} %pad_maximum_fusion), calls=%async_computation | async-start | bytes 1310720 | tf_op jit(solution)/shard_map/all_to_all | solution.py:63
  26.2 21.7 %all-to-all-done = bf16[16,33,512]{2,1,0:T(8,128)(2,1)S(1)} async-done(((bf16[16,33,512]{2,1,0:T(8,128)(2,1)}), bf16[16,33,512]{2,1,0:T(8,128)(2,1)S(1)}, u32[]{:S(2)}, u32[]{:S(2)}) %all-to-all-start) | async-done | bytes 540704 | tf_op jit(solution)/shard_map/all_to_all | solution.py:63
  47.8 0.2 copy.34
  48.0 0.1 pad.13
  48.1 0.4 copy.28
  48.7 0.3 fusion.26
  49.0 0.2 fusion.24
  49.2 0.8 fusion.40
  50.0 0.7 all-gather.5.cloned.1.call-update
  50.8 0.1 collective-permute-start.3
  50.9 5.1 %collective-permute-done.3 = f32[24]{0:T(128)S(1)} collective-permute-done((f32[24]{0:T(128)S(1)}, f32[24]{0:T(128)S(1)}, u32[]{:S(2)}, u32[]{:S(2)}) %collective-permute-start.3) | collective-permute-done | bytes 128 | tf_op jit(solution)/shard_map/ppermute | solution.py:13
  55.9 26.7 %all-gather.3.cloned.1.call-done = bf16[384,4096]{1,0:T(8,128)(2,1)} async-done(((bf16[24,4096]{1,0:T(8,128)(2,1)}), bf16[384,4096]{1,0:T(8,128)(2,1)}) %all-gather.3.cloned.1.call-update) | async-done | bytes 3145744 | tf_op jit(solution)/shard_map/all_gather | solution.py:82
  82.7 40.4 %all-gather.5.cloned.1.call-done = bf16[384,4096]{1,0:T(8,128)(2,1)} async-done(((bf16[24,4096]{1,0:T(8,128)(2,1)}), bf16[384,4096]{1,0:T(8,128)(2,1)}) %all-gather.5.cloned.1.call-update) | async-done | bytes 3145744 | tf_op jit(solution)/shard_map/all_gather | solution.py:83
  123.1 3.7 %fusion.6 = f32[384,192]{0,1:T(8,128)S(1)} fusion(bf16[384,4096]{1,0:T(8,128)(2,1)} %all-gather.5.cloned.1.call-done, bf16[1,192,8192]{2,1,0:T(8,128)(2,1)} %param.14), kind=kOutput, calls=%fused_computation.11 | convolution fusion | flops 603979776 | bytes 5013504 | tf_op jit(solution)/shard_map/dot_general | solution.py:17
  126.8 3.2 %fusion.16 = f32[384,192]{0,1:T(8,128)S(1)} fusion(f32[384,192]{0,1:T(8,128)S(1)} %fusion.6, bf16[384,4096]{1,0:T(8,128)(2,1)} %all-gather.3.cloned.1.call-done, bf16[1,192,8192]{2,1,0:T(8,128)(2,1)S(1)} %copy-done.5), kind=kOutput, calls=%fused_computation.25 | convolution fusion | flops 604053504 | bytes 5308416 | tf_op jit(solution)/shard_map/dot_general | solution.py:17
  130.1 1.2 fusion.2
  131.3 0.7 copy-done.7
  132.0 1.2 multiply_convert_fusion.1
  133.2 0.1 slice_bitcast_fusion
  133.3 0.1 copy.19
  133.4 0.1 copy.20
  133.6 0.3 copy-done
  133.9 2.7 convolution_convert_fusion.1
  136.6 0.2 reduce-scatter.5.cloned.1.call-start
  136.8 2.6 convolution_convert_fusion
  139.5 0.6 reduce-window.16
  140.1 63.7 %reduce-scatter.3.cloned.1.call-done = bf16[24,4096]{1,0:T(8,128)(2,1)} async-done(((bf16[384,4096]{1,0:T(8,128)(2,1)}), bf16[24,4096]{1,0:T(8,128)(2,1)}) %reduce-scatter.3.cloned.1.call-update) | async-done | bytes 196624 | tf_op jit(solution)/shard_map/reduce_scatter | solution.py:96
  203.8 0.9 copy.36
  204.8 67.6 %reduce-scatter.5.cloned.1.call-done = bf16[24,4096]{1,0:T(8,128)(2,1)} async-done(((bf16[384,4096]{1,0:T(8,128)(2,1)}), bf16[24,4096]{1,0:T(8,128)(2,1)}) %reduce-scatter.5.cloned.1.call-update) | async-done | bytes 196624 | tf_op jit(solution)/shard_map/reduce_scatter | solution.py:96
  272.4 0.9 copy.35
  273.3 0.9 fusion.29
  274.3 8.9 %all-to-all-start.1 = ((bf16[16,24,512]{2,1,0:T(8,128)(2,1)}), bf16[16,24,512]{2,1,0:T(8,128)(2,1)S(1)}, u32[]{:S(2)}, u32[]{:S(2)}) async-start(bf16[16,24,512]{2,1,0:T(8,128)(2,1)} %fusion.29), calls=%async_computation.3 | async-start | bytes 786432 | tf_op jit(solution)/shard_map/all_to_all | solution.py:108
  283.2 0.2 slice_reduce_fusion
  283.4 0.1 fusion.32
  283.6 0.3 convert_element_type.78
  283.9 12.8 %all-to-all-done.1 = bf16[16,24,512]{2,1,0:T(8,128)(2,1)S(1)} async-done(((bf16[16,24,512]{2,1,0:T(8,128)(2,1)}), bf16[16,24,512]{2,1,0:T(8,128)(2,1)S(1)}, u32[]{:S(2)}, u32[]{:S(2)}) %all-to-all-start.1) | async-done | bytes 393248 | tf_op jit(solution)/shard_map/all_to_all | solution.py:108
  296.7 4.0 %scatter_custom_fusion = f32[1024,512]{1,0:T(8,128)S(1)} fusion(f32[1024,512]{1,0:T(8,128)S(1)} %convert_element_type.78, s32[256]{0:T(256)S(1)} %bitcast.131, bf16[384,512]{1,0:T(8,128)(2,1)S(1)} %bitcast.110, s32[1024]{0:T(1024)S(1)} %pad_clamp_fusion), kind=kCustom, calls=%fused_computation.35 | custom fusion | flops 262144 | bytes 2494464 | tf_op jit(solution)/shard_map/scatter-add | solution.py:115
  300.8 1.1 convert_element_type.90
  (47 shorter events, 0.6 us)
Async XLA Ops:
  6.5 4.2 %collective-permute-start.1 = (s32[256,1]{0,1:T(1,128)}, s32[256,1]{0,1:T(1,128)S(1)}, u32[]{:S(2)}, u32[]{:S(2)}) collective-permute-start(s32[256,1]{0,1:T(1,128)} %param.11), channel_id=1, source_target_pairs={{16,0},{32,16},{48,32},{64,48},{80,64},{96,80},{112,96},{128,112},... | collective-permute-start | bytes 3080 | tf_op jit(solution)/shard_map/ppermute | solution.py:13
  8.6 3.1 collective-permute-start.2
  9.3 39.1 %collective-permute-start = (bf16[1024,512]{1,0:T(8,128)(2,1)}, bf16[1024,512]{1,0:T(8,128)(2,1)S(1)}, u32[]{:S(2)}, u32[]{:S(2)}) collective-permute-start(bf16[1024,512]{1,0:T(8,128)(2,1)} %param.9), channel_id=1, source_target_pairs={{240,0},{0,16},{16,32},{32,48},{48,64},{64,80},{80,96},{96,112},{1... | collective-permute-start | bytes 3145736 | tf_op jit(solution)/shard_map/ppermute | solution.py:13
  15.5 32.3 %all-to-all-start = ((bf16[16,33,512]{2,1,0:T(8,128)(2,1)}), bf16[16,33,512]{2,1,0:T(8,128)(2,1)S(1)}, u32[]{:S(2)}, u32[]{:S(2)}) async-start(bf16[16,33,512]{2,1,0:T(8,128)(2,1)} %pad_maximum_fusion), calls=%async_computation | async-start | bytes 1310720 | tf_op jit(solution)/shard_map/all_to_all | solution.py:63
  26.1 56.6 %all-gather.3.cloned.1.call-start = ((), (), s32[]{:S(2)}) async-start(), calls=%async_computation.4 | async-start | bytes 3342336 | tf_op jit(solution)/shard_map/all_gather | solution.py:82
  48.4 78.3 %copy-start.1 = (bf16[1024,512]{1,0:T(8,128)(2,1)}, bf16[1024,512]{1,0:T(8,128)(2,1)S(1)}, u32[]{:S(2)}) copy-start(bf16[1024,512]{1,0:T(8,128)(2,1)S(1)} %collective-permute-done) | copy-start | bytes 3145732
  50.0 73.1 %all-gather.5.cloned.1.call-start = ((), (), s32[]{:S(2)}) async-start(), calls=%async_computation.5 | async-start | bytes 3342336 | tf_op jit(solution)/shard_map/all_gather | solution.py:83
  50.7 153.1 %reduce-scatter.3.cloned.1.call-start = ((), (), s32[]{:S(2)}) async-start(), calls=%async_computation.6 | async-start | bytes 3342336 | tf_op jit(solution)/shard_map/reduce_scatter | solution.py:96
  50.8 5.2 %collective-permute-start.3 = (f32[24]{0:T(128)S(1)}, f32[24]{0:T(128)S(1)}, u32[]{:S(2)}, u32[]{:S(2)}) collective-permute-start(f32[24]{0:T(128)S(1)} %get-tuple-element.19), channel_id=1, source_target_pairs={{240,0},{0,16},{16,32},{32,48},{48,64},{64,80},{80,96},{96,112},{1... | collective-permute-start | bytes 296 | tf_op jit(solution)/shard_map/ppermute | solution.py:13
  123.1 3.7 %copy-start.5 = (bf16[1,192,8192]{2,1,0:T(8,128)(2,1)S(1)}, bf16[1,192,8192]{2,1,0:T(8,128)(2,1)}, u32[]{:S(2)}) copy-start(bf16[1,192,8192]{2,1,0:T(8,128)(2,1)} %param.14) | copy-start | bytes 9437188
  123.1 7.0 %copy-start.8 = (bf16[384,4096]{1,0:T(8,128)(2,1)S(1)}, bf16[384,4096]{1,0:T(8,128)(2,1)}, u32[]{:S(2)}) copy-start(bf16[384,4096]{1,0:T(8,128)(2,1)} %all-gather.5.cloned.1.call-done) | copy-start | bytes 9437188
  126.8 3.3 %copy-start.6 = (bf16[1,192,8192]{2,1,0:T(8,128)(2,1)S(1)}, bf16[1,192,8192]{2,1,0:T(8,128)(2,1)}, u32[]{:S(2)}) copy-start(bf16[1,192,8192]{2,1,0:T(8,128)(2,1)} %param.15) | copy-start | bytes 9437188
  130.1 1.9 copy-start.7
  132.0 1.9 copy-start
  136.6 2.9 copy-start.3
  136.6 135.8 %reduce-scatter.5.cloned.1.call-start = ((), (), s32[]{:S(2)}) async-start(), calls=%async_computation.7 | async-start | bytes 3342336 | tf_op jit(solution)/shard_map/reduce_scatter | solution.py:96
  139.5 144.1 %copy-start.4 = (s32[1,256]{1,0:T(1,128)S(1)}, s32[1,256]{1,0:T(1,128)}, u32[]{:S(2)}) copy-start(s32[1,256]{1,0:T(1,128)} %param.10) | copy-start | bytes 3076
  139.5 144.1 %copy-start.2 = (bf16[1024,512]{1,0:T(8,128)(2,1)S(1)}, bf16[1024,512]{1,0:T(8,128)(2,1)}, u32[]{:S(2)}) copy-start(bf16[1024,512]{1,0:T(8,128)(2,1)} %copy-done.1) | copy-start | bytes 3145732
  274.3 22.4 %all-to-all-start.1 = ((bf16[16,24,512]{2,1,0:T(8,128)(2,1)}), bf16[16,24,512]{2,1,0:T(8,128)(2,1)S(1)}, u32[]{:S(2)}, u32[]{:S(2)}) async-start(bf16[16,24,512]{2,1,0:T(8,128)(2,1)} %fusion.29), calls=%async_computation.3 | async-start | bytes 786432 | tf_op jit(solution)/shard_map/all_to_all | solution.py:108
Sparse Core Ops, SparseCore 0:
  50.1 32.5 all-gather.2
  84.5 38.5 all-gather.4
  136.7 67.0 reduce-scatter.2
  206.2 66.1 reduce-scatter.4

commit v6 on v4

--- a/solution.py
+++ b/solution.py
@@ -87,15 +87,14 @@
     hidden = jnp.roll(hidden.reshape(groups, capacity, hidden_width), 1, axis=0).reshape(
         groups * capacity, hidden_width
     )
-    part = jnp.dot(hidden, down_w[0], preferred_element_type=jnp.float32)
-    parts_in = lax.all_to_all(
-        part.astype(jnp.bfloat16).reshape(groups, capacity, part.shape[1]),
-        "section",
-        split_axis=0,
-        concat_axis=0,
-        tiled=True,
-    )
-    summed = jnp.sum(parts_in.astype(jnp.float32), axis=0).astype(jnp.bfloat16)
+    part = jnp.dot(hidden, down_w[0], preferred_element_type=jnp.float32).astype(jnp.bfloat16)
+    part = part.reshape(groups, capacity, part.shape[1])
+    me = lax.axis_index("section")
+    total = part[me].astype(jnp.float32)
+    for shift in range(1, groups):
+        outgoing_part = lax.dynamic_index_in_dim(part, (me + shift) % groups, axis=0, keepdims=False)
+        total = total + passed_along(outgoing_part, "section", shift).astype(jnp.float32)
+    summed = total.astype(jnp.bfloat16)
     update_rows = (score_home[:, None] * summed.astype(jnp.float32)).astype(jnp.bfloat16)
     outgoing = update_rows.reshape(capacity, n_exp_dev, local_width).transpose(1, 0, 2)
     back = lax.all_to_all(outgoing, "expert", split_axis=0, concat_axis=0, tiled=True)

time: 243 us -> 264 us (1.086)
  starting transfers between devices: 27.8 us -> 79.1 us
  waiting for transfers between devices: 153 us -> 123 us
  local copies, waits for them, and re-layouts: 7.73 us -> 11.2 us
    all_to_all x1 -> x0, waiting for transfers between devices: 83.6 us -> none  [body(): lax.all_to_all(part.astype(jnp.bfloat16).reshape(groups, capacity, part.s...]
    ppermute x4 -> x19, starting transfers between devices: 2.85 us -> 56.3 us  [passed_along(): return lax.ppermute(block, axis, route)]
    ppermute x4 -> x19, waiting for transfers between devices: 5.17 us -> 56.8 us  [passed_along(): return lax.ppermute(block, axis, route)]
    all_to_all x1 -> x0, starting transfers between devices: 5.57 us -> none  [body(): lax.all_to_all(part.astype(jnp.bfloat16).reshape(groups, capacity, part.s...]
    reduce_sum x1 -> x0, other arithmetic: 3.88 us -> none  [body(): summed = jnp.sum(parts_in.astype(jnp.float32), axis=0).astype(jnp.bfloat16)]
    all_to_all x1, starting transfers between devices: 8.67 us -> 12.1 us  [body(): lax.all_to_all(outgoing, 'expert', split_axis=0, concat_axis=0, tiled=True)]
    convert_element_type x1, other arithmetic: 0.71 us -> 3.61 us  [body(): (score_home[:, None] * summed.astype(jnp.float32)).astype(jnp.bfloat16)]
    dot_general x1, matrix products: 4.47 us -> 1.81 us  [body(): jnp.dot(hidden, down_w[0], preferred_element_type=jnp.float32)]
  transfers between devices with their start and end apart: 8 -> 22, of which waited for: 5 -> 12; matrix products, arithmetic and copies ran while one was open for 7% -> 7% of each run, Pallas kernels for 0% -> 0%
where the time goes in v6:
time: 264 us; the launch traced here: 262 us
  waiting for transfers between devices  123 us (47%)
  starting transfers between devices  79.1 us (30%)
  other arithmetic  25 us (9%)
  between operations  14 us (5%)
  local copies, waits for them, and re-layouts  11.2 us (4%)
  matrix products  10.4 us (4%)
    ppermute x19, waiting for transfers between devices, passed_along(): return lax.ppermute(block, axis, route)  56.8 us
    ppermute x19, starting transfers between devices, passed_along(): return lax.ppermute(block, axis, route)  56.3 us
    all_gather x1, waiting for transfers between devices, body(): block = lax.all_gather(normed, 'section', axis=0, tiled=True)  34.4 us
    all_to_all x1, waiting for transfers between devices, body(): lax.all_to_all(buffer, 'expert', split_axis=0, concat_axis=2, tiled=True)[0]  21.7 us
    all_to_all x1, starting transfers between devices, body(): lax.all_to_all(outgoing, 'expert', split_axis=0, concat_axis=0, tiled=True)  12.1 us
    all_to_all x1, starting transfers between devices, body(): lax.all_to_all(buffer, 'expert', split_axis=0, concat_axis=2, tiled=True)[0]  10.6 us
    all_to_all x1, waiting for transfers between devices, body(): lax.all_to_all(outgoing, 'expert', split_axis=0, concat_axis=0, tiled=True)  9.98 us
    dot_general x2, matrix products, feature_product(): lax.dot_general(block, weight, (((1,), (1,)), ((), ())), preferred_elemen...  8.29 us
  transfers between devices with their start and end apart: 22, of which 12 were waited for; matrix products, arithmetic and copies ran while one was open for 7% of the time, Pallas kernels for 0%

profile of v6, /device:TPU:8, one launch (start us, length us, event | category | flops | bytes accessed | tf_op | source)
XLA Modules:
  0.0 262.4 jit_solution(13757375251044513129)
XLA Ops:
  6.5 2.1 collective-permute-start.1
  8.6 0.7 collective-permute-start.2
  9.3 0.7 fusion.35
  10.0 0.7 fusion.34
  11.7 2.6 gather_fusion
  14.6 0.9 pad_maximum_fusion
  15.5 10.6 %all-to-all-start = ((bf16[16,33,512]{2,1,0:T(8,128)(2,1)}), bf16[16,33,512]{2,1,0:T(8,128)(2,1)}, u32[]{:S(2)}, u32[]{:S(2)}) async-start(bf16[16,33,512]{2,1,0:T(8,128)(2,1)} %pad_maximum_fusion), calls=%async_computation | async-start | bytes 1310720 | tf_op jit(solution)/shard_map/all_to_all | solution.py:63
  26.2 21.7 %all-to-all-done = bf16[16,33,512]{2,1,0:T(8,128)(2,1)} async-done(((bf16[16,33,512]{2,1,0:T(8,128)(2,1)}), bf16[16,33,512]{2,1,0:T(8,128)(2,1)}, u32[]{:S(2)}, u32[]{:S(2)}) %all-to-all-start) | async-done | bytes 540704 | tf_op jit(solution)/shard_map/all_to_all | solution.py:63
  47.9 1.3 copy.31
  50.2 0.9 fusion.7
  51.6 5.1 %collective-permute-done.3 = f32[24]{0:T(128)S(1)} collective-permute-done((f32[24]{0:T(128)S(1)}, f32[24]{0:T(128)S(1)}, u32[]{:S(2)}, u32[]{:S(2)}) %collective-permute-start.3) | collective-permute-done | bytes 128 | tf_op jit(solution)/shard_map/ppermute | solution.py:13
  56.7 34.4 %all-gather.2.cloned.1.call-done = bf16[384,8192]{1,0:T(8,128)(2,1)} async-done(((bf16[24,8192]{1,0:T(8,128)(2,1)}), bf16[384,8192]{1,0:T(8,128)(2,1)}) %all-gather.2.cloned.1.call-update) | async-done | bytes 6291472 | tf_op jit(solution)/shard_map/all_gather | solution.py:81
  91.0 6.1 %fusion.3 = f32[384,192]{0,1:T(8,128)S(1)} fusion(bf16[384,8192]{1,0:T(8,128)(2,1)} %all-gather.2.cloned.1.call-done, bf16[1,192,8192]{2,1,0:T(8,128)(2,1)} %param.14), kind=kOutput, calls=%fused_computation.7 | convolution fusion | flops 1207959552 | bytes 9732096 | tf_op jit(solution)/shard_map/dot_general | solution.py:17
  97.5 2.2 multiply_convert_fusion.1
  100.1 1.8 convolution_convert_fusion
  101.9 2.1 dynamic-slice_bitcast_fusion.14
  104.0 1.0 copy-done.1
  105.0 1.9 collective-permute-start.10
  106.9 1.2 collective-permute-start.11
  108.0 1.4 collective-permute-start.13
  109.4 1.8 collective-permute-start.14
  111.2 7.9 %collective-permute-done.10 = bf16[24,8192]{1,0:T(8,128)(2,1)S(1)} collective-permute-done((bf16[24,8192]{1,0:T(8,128)(2,1)S(1)}, bf16[24,8192]{1,0:T(8,128)(2,1)S(1)}, u32[]{:S(2)}, u32[]{:S(2)}) %collective-permute-start.10) | collective-permute-done | bytes 393248 | tf_op jit(solution)/shard_map/ppermute | solution.py:13
  119.1 23.7 %collective-permute-start.15 = (bf16[24,8192]{1,0:T(8,128)(2,1)S(1)}, bf16[24,8192]{1,0:T(8,128)(2,1)S(1)}, u32[]{:S(2)}, u32[]{:S(2)}) collective-permute-start(bf16[24,8192]{1,0:T(8,128)(2,1)S(1)} %get-tuple-element.19), channel_id=1, source_target_pairs={{64,0},{80,16},{96,32},{112,48},{128,64},{144,80},{160,96},{176,11... | collective-permute-start | bytes 1179656 | tf_op jit(solution)/shard_map/ppermute | solution.py:13
  142.8 16.3 %collective-permute-start.16 = (bf16[24,8192]{1,0:T(8,128)(2,1)S(1)}, bf16[24,8192]{1,0:T(8,128)(2,1)S(1)}, u32[]{:S(2)}, u32[]{:S(2)}) collective-permute-start(bf16[24,8192]{1,0:T(8,128)(2,1)S(1)} %get-tuple-element.18), channel_id=1, source_target_pairs={{48,0},{64,16},{80,32},{96,48},{112,64},{128,80},{144,96},{160,112... | collective-permute-start | bytes 1179656 | tf_op jit(solution)/shard_map/ppermute | solution.py:13
  159.6 1.6 collective-permute-start.18
  161.2 1.3 collective-permute-start.5
  162.5 3.5 %collective-permute-done.16 = bf16[24,8192]{1,0:T(8,128)(2,1)S(1)} collective-permute-done((bf16[24,8192]{1,0:T(8,128)(2,1)S(1)}, bf16[24,8192]{1,0:T(8,128)(2,1)S(1)}, u32[]{:S(2)}, u32[]{:S(2)}) %collective-permute-start.16) | collective-permute-done | bytes 393248 | tf_op jit(solution)/shard_map/ppermute | solution.py:13
  165.9 9.8 %collective-permute-done.17 = bf16[24,8192]{1,0:T(8,128)(2,1)S(1)} collective-permute-done((bf16[24,8192]{1,0:T(8,128)(2,1)S(1)}, bf16[24,8192]{1,0:T(8,128)(2,1)S(1)}, u32[]{:S(2)}, u32[]{:S(2)}) %collective-permute-start.17) | collective-permute-done | bytes 393248 | tf_op jit(solution)/shard_map/ppermute | solution.py:13
  175.7 4.4 %collective-permute-done.18 = bf16[24,8192]{1,0:T(8,128)(2,1)S(1)} collective-permute-done((bf16[24,8192]{1,0:T(8,128)(2,1)S(1)}, bf16[24,8192]{1,0:T(8,128)(2,1)S(1)}, u32[]{:S(2)}, u32[]{:S(2)}) %collective-permute-start.18) | collective-permute-done | bytes 393248 | tf_op jit(solution)/shard_map/ppermute | solution.py:13
  181.3 3.4 %collective-permute-start.9 = (bf16[24,8192]{1,0:T(8,128)(2,1)S(1)}, bf16[24,8192]{1,0:T(8,128)(2,1)}, u32[]{:S(2)}, u32[]{:S(2)}) collective-permute-start(bf16[24,8192]{1,0:T(8,128)(2,1)S(1)} %get-tuple-element.25), channel_id=1, source_target_pairs={{160,0},{176,16},{192,32},{208,48},{224,64},{240,80},{0,96},{16,11... | collective-permute-start | bytes 1179656 | tf_op jit(solution)/shard_map/ppermute | solution.py:13
  185.3 1.3 reduce-window.16
  186.6 2.3 collective-permute-done.6
  188.8 2.5 collective-permute-done.7
  191.3 10.2 %collective-permute-done.8 = bf16[24,8192]{1,0:T(8,128)(2,1)} collective-permute-done((bf16[24,8192]{1,0:T(8,128)(2,1)}, bf16[24,8192]{1,0:T(8,128)(2,1)}, u32[]{:S(2)}, u32[]{:S(2)}) %collective-permute-start.8) | collective-permute-done | bytes 393248 | tf_op jit(solution)/shard_map/ppermute | solution.py:13
  201.5 11.2 %collective-permute-done.9 = bf16[24,8192]{1,0:T(8,128)(2,1)} collective-permute-done((bf16[24,8192]{1,0:T(8,128)(2,1)S(1)}, bf16[24,8192]{1,0:T(8,128)(2,1)}, u32[]{:S(2)}, u32[]{:S(2)}) %collective-permute-start.9) | collective-permute-done | bytes 393248 | tf_op jit(solution)/shard_map/ppermute | solution.py:13
  212.7 3.6 %multiply_convert_fusion = bf16[24,8192]{1,0:T(8,128)(2,1)S(1)} fusion(f32[24]{0:T(128)} %copy-done.13, bf16[24,8192]{1,0:T(8,128)(2,1)} %copy-done.10, bf16[24,8192]{1,0:T(8,128)(2,1)} %copy-done.9, bf16[24,8192]{1,0:T(8,128)(2,1)} %copy-done.8, bf16[24,8192]{1,0:T(8,128)(2,1)} %copy-done.7, bf16[24,8192]{1,0:T(8,128)(2,1)} %copy-done.6, ...), kind=kLoop, calls=%fused_computation.33 | loop fusion | flops 6881280 | bytes 6684772 | tf_op jit(solution)/shard_map/convert_element_type | solution.py:98
  216.3 0.8 copy.32
  217.1 12.1 %all-to-all-start.1 = ((bf16[16,24,512]{2,1,0:T(8,128)(2,1)}), bf16[16,24,512]{2,1,0:T(8,128)(2,1)S(1)}, u32[]{:S(2)}, u32[]{:S(2)}) async-start(bf16[16,24,512]{2,1,0:T(8,128)(2,1)} %bitcast.127), calls=%async_computation.1 | async-start | bytes 786432 | tf_op jit(solution)/shard_map/all_to_all | solution.py:100
  229.2 0.7 slice_reduce_fusion
  229.9 1.2 reduce-window.19
  231.1 0.7 slice.64
  231.8 0.8 fusion.29
  232.6 0.7 compare_select_fusion
  233.2 0.7 compare_select_fusion.1
  233.9 2.8 %convert_element_type.123 = f32[1024,512]{1,0:T(8,128)} convert(bf16[1024,512]{1,0:T(8,128)(2,1)} %collective-permute-done) | non-fusion elementwise | flops 524288 | bytes 3145728 | tf_op jit(solution)/shard_map/convert_element_type | solution.py:107
  236.8 10.0 %all-to-all-done.1 = bf16[16,24,512]{2,1,0:T(8,128)(2,1)S(1)} async-done(((bf16[16,24,512]{2,1,0:T(8,128)(2,1)}), bf16[16,24,512]{2,1,0:T(8,128)(2,1)S(1)}, u32[]{:S(2)}, u32[]{:S(2)}) %all-to-all-start.1) | async-done | bytes 393248 | tf_op jit(solution)/shard_map/all_to_all | solution.py:100
  246.8 6.1 %scatter_custom_fusion = f32[1024,512]{1,0:T(8,128)} fusion(f32[1024,512]{1,0:T(8,128)} %convert_element_type.123, s32[256]{0:T(256)S(1)} %bitcast.146, bf16[384,512]{1,0:T(8,128)(2,1)S(1)} %bitcast.126, s32[1024]{0:T(1024)S(1)} %pad_clamp_fusion), kind=kCustom, calls=%fused_computation.37 | custom fusion | flops 262144 | bytes 2494464 | tf_op jit(solution)/shard_map/scatter-add | solution.py:107
  252.9 2.7 %convert_element_type.152 = bf16[1024,512]{1,0:T(8,128)(2,1)} convert(f32[1024,512]{1,0:T(8,128)} %scatter_custom_fusion) | non-fusion elementwise | flops 524288 | bytes 3145728 | tf_op jit(solution)/shard_map/convert_element_type | solution.py:108
  (78 shorter events, 5.4 us)
Async XLA Ops:
  6.5 93.5 %copy-start = (bf16[1,192,8192]{2,1,0:T(8,128)(2,1)S(1)}, bf16[1,192,8192]{2,1,0:T(8,128)(2,1)}, u32[]{:S(2)}) copy-start(bf16[1,192,8192]{2,1,0:T(8,128)(2,1)} %param.16) | copy-start | bytes 9437188
  6.5 4.2 %collective-permute-start.1 = (s32[256,1]{0,1:T(1,128)}, s32[256,1]{0,1:T(1,128)S(1)}, u32[]{:S(2)}, u32[]{:S(2)}) collective-permute-start(s32[256,1]{0,1:T(1,128)} %param.11), channel_id=1, source_target_pairs={{16,0},{32,16},{48,32},{64,48},{80,64},{96,80},{112,96},{128,112},... | collective-permute-start | bytes 3080 | tf_op jit(solution)/shard_map/ppermute | solution.py:13
  8.6 3.1 %collective-permute-start.2 = (s32[1,256]{1,0:T(1,128)}, s32[1,256]{1,0:T(1,128)S(1)}, u32[]{:S(2)}, u32[]{:S(2)}) collective-permute-start(s32[1,256]{1,0:T(1,128)} %param.10), channel_id=1, source_target_pairs={{16,0},{32,16},{48,32},{64,48},{80,64},{96,80},{112,96},{128,112},... | collective-permute-start | bytes 3080 | tf_op jit(solution)/shard_map/ppermute | solution.py:13
  9.3 40.3 %collective-permute-start = (bf16[1024,512]{1,0:T(8,128)(2,1)}, bf16[1024,512]{1,0:T(8,128)(2,1)}, u32[]{:S(2)}, u32[]{:S(2)}) collective-permute-start(bf16[1024,512]{1,0:T(8,128)(2,1)} %param.9), channel_id=1, source_target_pairs={{240,0},{0,16},{16,32},{32,48},{48,64},{64,80},{80,96},{96,112},{1... | collective-permute-start | bytes 3145736 | tf_op jit(solution)/shard_map/ppermute | solution.py:13
  15.5 32.4 %all-to-all-start = ((bf16[16,33,512]{2,1,0:T(8,128)(2,1)}), bf16[16,33,512]{2,1,0:T(8,128)(2,1)}, u32[]{:S(2)}, u32[]{:S(2)}) async-start(bf16[16,33,512]{2,1,0:T(8,128)(2,1)} %pad_maximum_fusion), calls=%async_computation | async-start | bytes 1310720 | tf_op jit(solution)/shard_map/all_to_all | solution.py:63
  26.2 64.9 %all-gather.2.cloned.1.call-start = ((), (), s32[]{:S(2)}) async-start(), calls=%async_computation.2 | async-start | bytes 6684672 | tf_op jit(solution)/shard_map/all_gather | solution.py:81
  51.3 5.3 %collective-permute-start.3 = (f32[24]{0:T(128)S(1)}, f32[24]{0:T(128)S(1)}, u32[]{:S(2)}, u32[]{:S(2)}) collective-permute-start(f32[24]{0:T(128)S(1)} %get-tuple-element.32), channel_id=1, source_target_pairs={{240,0},{0,16},{16,32},{32,48},{48,64},{64,80},{80,96},{96,112},{1... | collective-permute-start | bytes 296 | tf_op jit(solution)/shard_map/ppermute | solution.py:13
  56.7 40.5 %copy-start.13 = (f32[24]{0:T(128)}, f32[24]{0:T(128)S(1)}, u32[]{:S(2)}) copy-start(f32[24]{0:T(128)S(1)} %collective-permute-done.3) | copy-start | bytes 292
  91.0 6.1 %copy-start.14 = (bf16[384,8192]{1,0:T(8,128)(2,1)S(1)}, bf16[384,8192]{1,0:T(8,128)(2,1)}, u32[]{:S(2)}) copy-start(bf16[384,8192]{1,0:T(8,128)(2,1)} %all-gather.2.cloned.1.call-done) | copy-start | bytes 18874372
  91.0 6.4 %copy-start.15 = (bf16[1,192,8192]{2,1,0:T(8,128)(2,1)S(1)}, bf16[1,192,8192]{2,1,0:T(8,128)(2,1)}, u32[]{:S(2)}) copy-start(bf16[1,192,8192]{2,1,0:T(8,128)(2,1)} %param.15) | copy-start | bytes 9437188
  101.9 3.1 %copy-start.1 = (bf16[384,8192]{1,0:T(8,128)(2,1)}, bf16[384,8192]{1,0:T(8,128)(2,1)S(1)}, u32[]{:S(2)}) copy-start(bf16[384,8192]{1,0:T(8,128)(2,1)S(1)} %convolution_convert_fusion) | copy-start | bytes 18874372
  101.9 82.8 %copy-start.12 = (s32[256,1]{0,1:T(1,128)S(1)}, s32[256,1]{0,1:T(1,128)}, u32[]{:S(2)}) copy-start(s32[256,1]{0,1:T(1,128)} %param.11) | copy-start | bytes 3076
  105.0 14.1 %collective-permute-start.10 = (bf16[24,8192]{1,0:T(8,128)(2,1)S(1)}, bf16[24,8192]{1,0:T(8,128)(2,1)S(1)}, u32[]{:S(2)}, u32[]{:S(2)}) collective-permute-start(bf16[24,8192]{1,0:T(8,128)(2,1)S(1)} %get-tuple-element.24), channel_id=1, source_target_pairs={{144,0},{160,16},{176,32},{192,48},{208,64},{224,80},{240,96},{0,1... | collective-permute-start | bytes 1179656 | tf_op jit(solution)/shard_map/ppermute | solution.py:13
  106.9 36.0 %collective-permute-start.11 = (bf16[24,8192]{1,0:T(8,128)(2,1)S(1)}, bf16[24,8192]{1,0:T(8,128)(2,1)S(1)}, u32[]{:S(2)}, u32[]{:S(2)}) collective-permute-start(bf16[24,8192]{1,0:T(8,128)(2,1)S(1)} %get-tuple-element.23), channel_id=1, source_target_pairs={{128,0},{144,16},{160,32},{176,48},{192,64},{208,80},{224,96},{240... | collective-permute-start | bytes 1179656 | tf_op jit(solution)/shard_map/ppermute | solution.py:13
  108.0 51.1 %collective-permute-start.12 = (bf16[24,8192]{1,0:T(8,128)(2,1)S(1)}, bf16[24,8192]{1,0:T(8,128)(2,1)S(1)}, u32[]{:S(2)}, u32[]{:S(2)}) collective-permute-start(bf16[24,8192]{1,0:T(8,128)(2,1)S(1)} %get-tuple-element.22), channel_id=1, source_target_pairs={{112,0},{128,16},{144,32},{160,48},{176,64},{192,80},{208,96},{224... | collective-permute-start | bytes 1179656 | tf_op jit(solution)/shard_map/ppermute | solution.py:13
  108.0 51.5 %collective-permute-start.13 = (bf16[24,8192]{1,0:T(8,128)(2,1)S(1)}, bf16[24,8192]{1,0:T(8,128)(2,1)S(1)}, u32[]{:S(2)}, u32[]{:S(2)}) collective-permute-start(bf16[24,8192]{1,0:T(8,128)(2,1)S(1)} %get-tuple-element.21), channel_id=1, source_target_pairs={{96,0},{112,16},{128,32},{144,48},{160,64},{176,80},{192,96},{208,... | collective-permute-start | bytes 1179656 | tf_op jit(solution)/shard_map/ppermute | solution.py:13
  109.4 51.8 %collective-permute-start.14 = (bf16[24,8192]{1,0:T(8,128)(2,1)S(1)}, bf16[24,8192]{1,0:T(8,128)(2,1)S(1)}, u32[]{:S(2)}, u32[]{:S(2)}) collective-permute-start(bf16[24,8192]{1,0:T(8,128)(2,1)S(1)} %get-tuple-element.20), channel_id=1, source_target_pairs={{80,0},{96,16},{112,32},{128,48},{144,64},{160,80},{176,96},{192,1... | collective-permute-start | bytes 1179656 | tf_op jit(solution)/shard_map/ppermute | solution.py:13
  119.1 61.3 %copy-start.2 = (bf16[24,8192]{1,0:T(8,128)(2,1)}, bf16[24,8192]{1,0:T(8,128)(2,1)S(1)}, u32[]{:S(2)}) copy-start(bf16[24,8192]{1,0:T(8,128)(2,1)S(1)} %collective-permute-done.10) | copy-start | bytes 1179652
  119.1 42.0 %collective-permute-start.15 = (bf16[24,8192]{1,0:T(8,128)(2,1)S(1)}, bf16[24,8192]{1,0:T(8,128)(2,1)S(1)}, u32[]{:S(2)}, u32[]{:S(2)}) collective-permute-start(bf16[24,8192]{1,0:T(8,128)(2,1)S(1)} %get-tuple-element.19), channel_id=1, source_target_pairs={{64,0},{80,16},{96,32},{112,48},{128,64},{144,80},{160,96},{176,11... | collective-permute-start | bytes 1179656 | tf_op jit(solution)/shard_map/ppermute | solution.py:13
  142.8 37.7 %copy-start.3 = (bf16[24,8192]{1,0:T(8,128)(2,1)}, bf16[24,8192]{1,0:T(8,128)(2,1)S(1)}, u32[]{:S(2)}) copy-start(bf16[24,8192]{1,0:T(8,128)(2,1)S(1)} %collective-permute-done.11) | copy-start | bytes 1179652
  142.8 23.1 %collective-permute-start.16 = (bf16[24,8192]{1,0:T(8,128)(2,1)S(1)}, bf16[24,8192]{1,0:T(8,128)(2,1)S(1)}, u32[]{:S(2)}, u32[]{:S(2)}) collective-permute-start(bf16[24,8192]{1,0:T(8,128)(2,1)S(1)} %get-tuple-element.18), channel_id=1, source_target_pairs={{48,0},{64,16},{80,32},{96,48},{112,64},{128,80},{144,96},{160,112... | collective-permute-start | bytes 1179656 | tf_op jit(solution)/shard_map/ppermute | solution.py:13
  159.1 21.4 %copy-start.4 = (bf16[24,8192]{1,0:T(8,128)(2,1)}, bf16[24,8192]{1,0:T(8,128)(2,1)S(1)}, u32[]{:S(2)}) copy-start(bf16[24,8192]{1,0:T(8,128)(2,1)S(1)} %collective-permute-done.12) | copy-start | bytes 1179652
  159.1 16.6 %collective-permute-start.17 = (bf16[24,8192]{1,0:T(8,128)(2,1)S(1)}, bf16[24,8192]{1,0:T(8,128)(2,1)S(1)}, u32[]{:S(2)}, u32[]{:S(2)}) collective-permute-start(bf16[24,8192]{1,0:T(8,128)(2,1)S(1)} %get-tuple-element.17), channel_id=1, source_target_pairs={{32,0},{48,16},{64,32},{80,48},{96,64},{112,80},{128,96},{144,112}... | collective-permute-start | bytes 1179656 | tf_op jit(solution)/shard_map/ppermute | solution.py:13
  159.6 20.9 %copy-start.5 = (bf16[24,8192]{1,0:T(8,128)(2,1)}, bf16[24,8192]{1,0:T(8,128)(2,1)S(1)}, u32[]{:S(2)}) copy-start(bf16[24,8192]{1,0:T(8,128)(2,1)S(1)} %collective-permute-done.13) | copy-start | bytes 1179652
  159.6 20.5 %collective-permute-start.18 = (bf16[24,8192]{1,0:T(8,128)(2,1)S(1)}, bf16[24,8192]{1,0:T(8,128)(2,1)S(1)}, u32[]{:S(2)}, u32[]{:S(2)}) collective-permute-start(bf16[24,8192]{1,0:T(8,128)(2,1)S(1)} %get-tuple-element.16), channel_id=1, source_target_pairs={{16,0},{32,16},{48,32},{64,48},{80,64},{96,80},{112,96},{128,112},... | collective-permute-start | bytes 1179656 | tf_op jit(solution)/shard_map/ppermute | solution.py:13
  161.2 19.3 %copy-start.6 = (bf16[24,8192]{1,0:T(8,128)(2,1)}, bf16[24,8192]{1,0:T(8,128)(2,1)S(1)}, u32[]{:S(2)}) copy-start(bf16[24,8192]{1,0:T(8,128)(2,1)S(1)} %collective-permute-done.14) | copy-start | bytes 1179652
  161.2 19.3 %collective-permute-start.4 = (bf16[24,8192]{1,0:T(8,128)(2,1)S(1)}, bf16[24,8192]{1,0:T(8,128)(2,1)S(1)}, u32[]{:S(2)}, u32[]{:S(2)}) collective-permute-start(bf16[24,8192]{1,0:T(8,128)(2,1)S(1)} %get-tuple-element.15), channel_id=1, source_target_pairs={{240,0},{0,16},{16,32},{32,48},{48,64},{64,80},{80,96},{96,112},{1... | collective-permute-start | bytes 1179656 | tf_op jit(solution)/shard_map/ppermute | solution.py:13
  161.2 19.3 %copy-start.7 = (bf16[24,8192]{1,0:T(8,128)(2,1)}, bf16[24,8192]{1,0:T(8,128)(2,1)S(1)}, u32[]{:S(2)}) copy-start(bf16[24,8192]{1,0:T(8,128)(2,1)S(1)} %collective-permute-done.15) | copy-start | bytes 1179652
  161.2 25.3 %collective-permute-start.5 = (bf16[24,8192]{1,0:T(8,128)(2,1)}, bf16[24,8192]{1,0:T(8,128)(2,1)}, u32[]{:S(2)}, u32[]{:S(2)}) collective-permute-start(bf16[24,8192]{1,0:T(8,128)(2,1)} %get-tuple-element.29), channel_id=1, source_target_pairs={{224,0},{240,16},{0,32},{16,48},{32,64},{48,80},{64,96},{80,112},{... | collective-permute-start | bytes 1179656 | tf_op jit(solution)/shard_map/ppermute | solution.py:13
  165.9 14.6 %copy-start.8 = (bf16[24,8192]{1,0:T(8,128)(2,1)}, bf16[24,8192]{1,0:T(8,128)(2,1)S(1)}, u32[]{:S(2)}) copy-start(bf16[24,8192]{1,0:T(8,128)(2,1)S(1)} %collective-permute-done.16) | copy-start | bytes 1179652
  165.9 22.9 %collective-permute-start.6 = (bf16[24,8192]{1,0:T(8,128)(2,1)}, bf16[24,8192]{1,0:T(8,128)(2,1)}, u32[]{:S(2)}, u32[]{:S(2)}) collective-permute-start(bf16[24,8192]{1,0:T(8,128)(2,1)} %get-tuple-element.28), channel_id=1, source_target_pairs={{208,0},{224,16},{240,32},{0,48},{16,64},{32,80},{48,96},{64,112},... | collective-permute-start | bytes 1179656 | tf_op jit(solution)/shard_map/ppermute | solution.py:13
  175.7 4.9 %copy-start.9 = (bf16[24,8192]{1,0:T(8,128)(2,1)}, bf16[24,8192]{1,0:T(8,128)(2,1)S(1)}, u32[]{:S(2)}) copy-start(bf16[24,8192]{1,0:T(8,128)(2,1)S(1)} %collective-permute-done.17) | copy-start | bytes 1179652
  175.7 15.6 %collective-permute-start.7 = (bf16[24,8192]{1,0:T(8,128)(2,1)}, bf16[24,8192]{1,0:T(8,128)(2,1)}, u32[]{:S(2)}, u32[]{:S(2)}) collective-permute-start(bf16[24,8192]{1,0:T(8,128)(2,1)} %get-tuple-element.27), channel_id=1, source_target_pairs={{192,0},{208,16},{224,32},{240,48},{0,64},{16,80},{32,96},{48,112}... | collective-permute-start | bytes 1179656 | tf_op jit(solution)/shard_map/ppermute | solution.py:13
  180.1 0.7 copy-start.10
  180.1 21.5 %collective-permute-start.8 = (bf16[24,8192]{1,0:T(8,128)(2,1)}, bf16[24,8192]{1,0:T(8,128)(2,1)}, u32[]{:S(2)}, u32[]{:S(2)}) collective-permute-start(bf16[24,8192]{1,0:T(8,128)(2,1)} %get-tuple-element.26), channel_id=1, source_target_pairs={{176,0},{192,16},{208,32},{224,48},{240,64},{0,80},{16,96},{32,112... | collective-permute-start | bytes 1179656 | tf_op jit(solution)/shard_map/ppermute | solution.py:13
  180.5 0.8 copy-start.11
  181.3 31.4 %collective-permute-start.9 = (bf16[24,8192]{1,0:T(8,128)(2,1)S(1)}, bf16[24,8192]{1,0:T(8,128)(2,1)}, u32[]{:S(2)}, u32[]{:S(2)}) collective-permute-start(bf16[24,8192]{1,0:T(8,128)(2,1)S(1)} %get-tuple-element.25), channel_id=1, source_target_pairs={{160,0},{176,16},{192,32},{208,48},{224,64},{240,80},{0,96},{16,11... | collective-permute-start | bytes 1179656 | tf_op jit(solution)/shard_map/ppermute | solution.py:13
  217.1 29.6 %all-to-all-start.1 = ((bf16[16,24,512]{2,1,0:T(8,128)(2,1)}), bf16[16,24,512]{2,1,0:T(8,128)(2,1)S(1)}, u32[]{:S(2)}, u32[]{:S(2)}) async-start(bf16[16,24,512]{2,1,0:T(8,128)(2,1)} %bitcast.127), calls=%async_computation.1 | async-start | bytes 786432 | tf_op jit(solution)/shard_map/all_to_all | solution.py:100
Sparse Core Ops, SparseCore 0:
  51.2 39.7 all-gather.1

commit v7 on v3

--- a/solution.py
+++ b/solution.py
@@ -19,14 +19,6 @@
     )
 
 
-def slots_of(experts, expert_count):
-    onehot = (experts[:, None] == jnp.arange(expert_count, dtype=jnp.int32)[None, :]).astype(
-        jnp.int32
-    )
-    ranks = jnp.cumsum(onehot, axis=0) - 1
-    return jnp.sum(ranks * onehot, axis=1)
-
-
 def body(activations, modality, selected, routes, norm_gain, router, gate_w, up_w, down_w):
     n_section = lax.axis_size("section")
     sel_count = selected.shape[1]
@@ -34,12 +26,17 @@
     capacity = max(2, 3 * sel_count // (2 * expert_count))
     groups = n_section
 
-    arrived = passed_along(activations, "section", 1)
-
     sel_next = passed_along(selected, "section", -1)[0]
     routes_next = passed_along(routes, "section", -1)[:, 0]
     rows = activations[sel_next]
-    target = routes_next * capacity + slots_of(routes_next, expert_count)
+    both = jnp.stack([routes_next, routes[:, 0]], axis=1)
+    onehot = (both[:, :, None] == jnp.arange(expert_count, dtype=jnp.int32)[None, None, :]).astype(
+        jnp.int32
+    )
+    slots = jnp.sum((jnp.cumsum(onehot, axis=0) - 1) * onehot, axis=2)
+    targets = both * capacity + slots
+    target = targets[:, 0]
+    position = targets[:, 1]
     placing = (
         target[None, :] == jnp.arange(expert_count * capacity, dtype=jnp.int32)[:, None]
     ).astype(jnp.bfloat16)
@@ -61,7 +58,6 @@
     )
     buffer = jnp.concatenate([buffer, extra], axis=1)
     mine = lax.all_to_all(buffer, "expert", split_axis=0, concat_axis=2, tiled=True)[0]
-    arrived, mine = lax.optimization_barrier((arrived, mine))
     coded = mine[capacity:].astype(jnp.float32).reshape(3, table_rows, mine.shape[1])
     tables = (coded[0] + coded[1]) + coded[2]
     mine = mine[:capacity]
@@ -79,7 +75,8 @@
     score_home = passed_along(score, "section", 1)
 
     block = lax.all_gather(normed, "section", axis=0, tiled=True)
-    block, score_home = lax.optimization_barrier((block, score_home))
+    block, score_home, leaving = lax.optimization_barrier((block, score_home, activations))
+    arrived = passed_along(leaving, "section", 1)
     gate = feature_product(block, gate_w[0])
     upper = feature_product(block, up_w[0])
     hidden = (jax.nn.silu(gate) * upper).astype(jnp.bfloat16)
@@ -102,11 +99,13 @@
     flat_back = back.reshape(expert_count * capacity, local_width)
 
     picks = selected[0]
-    experts = routes[:, 0]
-    position = experts * capacity + slots_of(experts, expert_count)
-    update = flat_back[position].astype(jnp.float32)
-    result = arrived.astype(jnp.float32).at[picks].add(update)
-    return result.astype(jnp.bfloat16)
+    token_count = arrived.shape[0]
+    source = jnp.full((token_count,), -1, jnp.int32).at[picks].set(position)
+    spread = (
+        source[:, None] == jnp.arange(expert_count * capacity, dtype=jnp.int32)[None, :]
+    ).astype(jnp.bfloat16)
+    update = jnp.dot(spread, flat_back, preferred_element_type=jnp.float32)
+    return (arrived.astype(jnp.float32) + update).astype(jnp.bfloat16)
 
 
 def solution(mesh):

time: 220 us -> 222 us (level)
  waiting for transfers between devices: 139 us -> 147 us
  other arithmetic: 21.3 us -> 14 us
    all_to_all x1, waiting for transfers between devices: 5.78 us -> 12 us  [body(): lax.all_to_all(outgoing, 'expert', split_axis=0, concat_axis=0, tiled=True)]
    scatter-add x1 -> x0, other arithmetic: 6.15 us -> none  [body(): result = arrived.astype(jnp.float32).at[picks].add(update)]
    convert_element_type x4 -> x2, other arithmetic: 5.57 us -> 2.56 us  [the longest x1 2.55 us: body(): return (arrived.astype(jnp.float32) + update).astype(jnp.bfloat16)]
  transfers between devices with their start and end apart: 8 -> 8, of which waited for: 5 -> 5; matrix products, arithmetic and copies ran while one was open for 7% -> 4% of each run, Pallas kernels for 0% -> 0%
where the time goes in v7:
time: 222 us; the launch traced here: 220 us
  waiting for transfers between devices  147 us (66%)
  starting transfers between devices  22.6 us (10%)
  other arithmetic  14 us (6%)
  matrix products  13.8 us (6%)
  between operations  13.7 us (6%)
  local copies, waits for them, and re-layouts  8.11 us (4%)
    reduce_scatter x1, waiting for transfers between devices, body(): lax.psum_scatter(lax.optimization_barrier(part.astype(jnp.bfloat16)).asty...  74.4 us
    all_gather x1, waiting for transfers between devices, body(): block = lax.all_gather(normed, 'section', axis=0, tiled=True)  34.2 us
    all_to_all x1, waiting for transfers between devices, body(): lax.all_to_all(buffer, 'expert', split_axis=0, concat_axis=2, tiled=True)[0]  21.7 us
    all_to_all x1, waiting for transfers between devices, body(): lax.all_to_all(outgoing, 'expert', split_axis=0, concat_axis=0, tiled=True)  12 us
    all_to_all x1, starting transfers between devices, body(): lax.all_to_all(buffer, 'expert', split_axis=0, concat_axis=2, tiled=True)[0]  10.6 us
    all_to_all x1, starting transfers between devices, body(): lax.all_to_all(outgoing, 'expert', split_axis=0, concat_axis=0, tiled=True)  8.75 us
    dot_general x2, matrix products, feature_product(): lax.dot_general(block, weight, (((1,), (1,)), ((), ())), preferred_elemen...  8.29 us
    ppermute x4, waiting for transfers between devices, passed_along(): return lax.ppermute(block, axis, route)  5.07 us
  transfers between devices with their start and end apart: 8, of which 5 were waited for; matrix products, arithmetic and copies ran while one was open for 4% of the time, Pallas kernels for 0%

profile of v7, /device:TPU:8, one launch (start us, length us, event | category | flops | bytes accessed | tf_op | source)
XLA Modules:
  0.0 219.5 jit_solution(2944080293633834807)
XLA Ops:
  6.5 2.1 collective-permute-start
  8.6 0.7 collective-permute-start.1
  9.3 0.7 fusion.12
  10.0 0.7 fusion.11
  10.7 0.0 collective-permute-done
  10.8 0.7 pad_add_fusion
  11.5 1.2 reduce-window.6
  12.6 0.1 slice.77
  12.7 0.1 copy.23
  12.8 0.1 fusion.9
  12.9 0.7 multiply_add_fusion
  13.7 2.6 %gather_fusion = bf16[256,512]{1,0:T(8,128)(2,1)S(1)} fusion(bf16[1024,512]{1,0:T(8,128)(2,1)} %param.9, s32[1024]{0:T(1024)S(1)} %pad_clamp_fusion), kind=kCustom, calls=%fused_computation | custom fusion | bytes 525312 | tf_op jit(solution)/shard_map/gather | solution.py:31
  16.3 0.3 convolution_convert_fusion.1
  16.6 0.9 pad_maximum_fusion
  17.5 10.6 %all-to-all-start = ((bf16[16,33,512]{2,1,0:T(8,128)(2,1)}), bf16[16,33,512]{2,1,0:T(8,128)(2,1)}, u32[]{:S(2)}, u32[]{:S(2)}) async-start(bf16[16,33,512]{2,1,0:T(8,128)(2,1)} %pad_maximum_fusion), calls=%async_computation | async-start | bytes 1310720 | tf_op jit(solution)/shard_map/all_to_all | solution.py:60
  28.1 0.0 all-gather.2.cloned.1.call-start
  28.2 21.7 %all-to-all-done = bf16[16,33,512]{2,1,0:T(8,128)(2,1)} async-done(((bf16[16,33,512]{2,1,0:T(8,128)(2,1)}), bf16[16,33,512]{2,1,0:T(8,128)(2,1)}, u32[]{:S(2)}, u32[]{:S(2)}) %all-to-all-start) | async-done | bytes 540704 | tf_op jit(solution)/shard_map/all_to_all | solution.py:60
  49.9 1.0 slice_convert_fusion.1
  50.9 0.1 slice_add_fusion
  51.0 2.0 fusion.18
  53.0 0.5 broadcast.113
  53.5 0.7 fusion.16
  54.3 1.2 copy.33
  55.5 1.3 multiply_reduce_fusion
  56.8 0.9 multiply_convert_fusion.1
  57.7 0.0 all-gather.2.cloned.1.call-update
  57.7 0.0 reduce-scatter.2.cloned.1.call-start
  57.8 0.1 collective-permute-start.2
  57.8 5.1 %collective-permute-done.2 = f32[24]{0:T(128)S(1)} collective-permute-done((f32[24]{0:T(128)S(1)}, f32[24]{0:T(128)S(1)}, u32[]{:S(2)}, u32[]{:S(2)}) %collective-permute-start.2) | collective-permute-done | bytes 128 | tf_op jit(solution)/shard_map/ppermute | solution.py:13
  62.9 34.2 %all-gather.2.cloned.1.call-done = bf16[384,8192]{1,0:T(8,128)(2,1)} async-done(((bf16[24,8192]{1,0:T(8,128)(2,1)}), bf16[384,8192]{1,0:T(8,128)(2,1)}) %all-gather.2.cloned.1.call-update) | async-done | bytes 6291472 | tf_op jit(solution)/shard_map/all_gather | solution.py:77
  97.1 6.1 %fusion.3 = f32[384,192]{0,1:T(8,128)S(1)} fusion(bf16[384,8192]{1,0:T(8,128)(2,1)} %all-gather.2.cloned.1.call-done, bf16[1,192,8192]{2,1,0:T(8,128)(2,1)} %param.14), kind=kOutput, calls=%fused_computation.6 | convolution fusion | flops 1207959552 | bytes 9732096 | tf_op jit(solution)/shard_map/dot_general | solution.py:17
  103.2 0.3 copy-done.3
  103.5 2.2 %multiply_convert_fusion.2 = bf16[384,192]{0,1:T(8,128)(2,1)S(1)} fusion(f32[384,192]{0,1:T(8,128)S(1)} %fusion.3, bf16[384,8192]{1,0:T(8,128)(2,1)S(1)} %copy-done.2, bf16[1,192,8192]{2,1,0:T(8,128)(2,1)S(1)} %copy-done.3), kind=kOutput, calls=%fused_computation.21 | convolution fusion | flops 1208401920 | bytes 9879552 | tf_op jit(solution)/shard_map/dot_general | solution.py:17
  105.8 0.1 slice_bitcast_fusion
  105.8 0.1 copy.27
  106.0 0.1 copy.28
  106.0 0.1 pad_maximum_fusion.1
  106.1 4.5 %convolution_convert_fusion = bf16[384,8192]{1,0:T(8,128)(2,1)} fusion(bf16[384,192]{1,0:T(8,128)(2,1)S(1)} %bitcast.77, bf16[1,192,8192]{2,1,0:T(8,128)(2,1)S(1)} %copy-done), kind=kOutput, calls=%fused_computation.2 | convolution fusion | flops 1211105280 | bytes 9584640 | tf_op jit(solution)/shard_map/dot_general | solution.py:87
  110.6 0.0 reduce-scatter.2.cloned.1.call-update
  110.6 0.3 collective-permute-start.3
  111.0 74.4 %reduce-scatter.2.cloned.1.call-done = bf16[24,8192]{1,0:T(8,128)(2,1)} async-done(((bf16[384,8192]{1,0:T(8,128)(2,1)}), bf16[24,8192]{1,0:T(8,128)(2,1)}) %reduce-scatter.2.cloned.1.call-update) | async-done | bytes 393232 | tf_op jit(solution)/shard_map/reduce_scatter | solution.py:88
  185.3 1.1 multiply_convert_fusion
  186.4 0.8 copy.38
  187.2 8.7 %all-to-all-start.1 = ((bf16[16,24,512]{2,1,0:T(8,128)(2,1)}), bf16[16,24,512]{2,1,0:T(8,128)(2,1)S(1)}, u32[]{:S(2)}, u32[]{:S(2)}) async-start(bf16[16,24,512]{2,1,0:T(8,128)(2,1)} %bitcast.74), calls=%async_computation.2 | async-start | bytes 786432 | tf_op jit(solution)/shard_map/all_to_all | solution.py:98
  196.0 1.4 scatter_custom_fusion
  197.4 12.0 %all-to-all-done.1 = bf16[16,24,512]{2,1,0:T(8,128)(2,1)S(1)} async-done(((bf16[16,24,512]{2,1,0:T(8,128)(2,1)}), bf16[16,24,512]{2,1,0:T(8,128)(2,1)S(1)}, u32[]{:S(2)}, u32[]{:S(2)}) %all-to-all-start.1) | async-done | bytes 393248 | tf_op jit(solution)/shard_map/all_to_all | solution.py:98
  209.4 0.8 fusion.5
  210.1 2.6 %add_convert_fusion = bf16[1024,512]{1,0:T(8,128)(2,1)} fusion(f32[1024,512]{1,0:T(8,128)S(1)} %fusion.5, bf16[1024,512]{1,0:T(8,128)(2,1)} %collective-permute-done.3), kind=kLoop, calls=%fused_computation.8 | loop fusion | flops 1572864 | bytes 4194304 | tf_op jit(solution)/shard_map/convert_element_type | solution.py:108
  (24 shorter events, 0.2 us)
Async XLA Ops:
  6.5 99.6 %copy-start = (bf16[1,192,8192]{2,1,0:T(8,128)(2,1)S(1)}, bf16[1,192,8192]{2,1,0:T(8,128)(2,1)}, u32[]{:S(2)}) copy-start(bf16[1,192,8192]{2,1,0:T(8,128)(2,1)} %param.16) | copy-start | bytes 9437188
  6.5 4.2 %collective-permute-start = (s32[256,1]{0,1:T(1,128)}, s32[256,1]{0,1:T(1,128)S(1)}, u32[]{:S(2)}, u32[]{:S(2)}) collective-permute-start(s32[256,1]{0,1:T(1,128)} %param.11), channel_id=1, source_target_pairs={{16,0},{32,16},{48,32},{64,48},{80,64},{96,80},{112,96},{128,112},... | collective-permute-start | bytes 3080 | tf_op jit(solution)/shard_map/ppermute | solution.py:13
  8.6 5.0 %collective-permute-start.1 = (s32[1,256]{1,0:T(1,128)}, s32[1,256]{1,0:T(1,128)S(1)}, u32[]{:S(2)}, u32[]{:S(2)}) collective-permute-start(s32[1,256]{1,0:T(1,128)} %param.10), channel_id=1, source_target_pairs={{16,0},{32,16},{48,32},{64,48},{80,64},{96,80},{112,96},{128,112},... | collective-permute-start | bytes 3080 | tf_op jit(solution)/shard_map/ppermute | solution.py:13
  17.5 32.4 %all-to-all-start = ((bf16[16,33,512]{2,1,0:T(8,128)(2,1)}), bf16[16,33,512]{2,1,0:T(8,128)(2,1)}, u32[]{:S(2)}, u32[]{:S(2)}) async-start(bf16[16,33,512]{2,1,0:T(8,128)(2,1)} %pad_maximum_fusion), calls=%async_computation | async-start | bytes 1310720 | tf_op jit(solution)/shard_map/all_to_all | solution.py:60
  28.1 69.0 %all-gather.2.cloned.1.call-start = ((), (), s32[]{:S(2)}) async-start(), calls=%async_computation.3 | async-start | bytes 6684672 | tf_op jit(solution)/shard_map/all_gather | solution.py:77
  57.7 127.6 %reduce-scatter.2.cloned.1.call-start = ((), (), s32[]{:S(2)}) async-start(), calls=%async_computation.4 | async-start | bytes 6684672 | tf_op jit(solution)/shard_map/reduce_scatter | solution.py:88
  57.8 5.2 %collective-permute-start.2 = (f32[24]{0:T(128)S(1)}, f32[24]{0:T(128)S(1)}, u32[]{:S(2)}, u32[]{:S(2)}) collective-permute-start(f32[24]{0:T(128)S(1)} %get-tuple-element.21), channel_id=1, source_target_pairs={{240,0},{0,16},{16,32},{32,48},{48,64},{64,80},{80,96},{96,112},{1... | collective-permute-start | bytes 296 | tf_op jit(solution)/shard_map/ppermute | solution.py:13
  97.1 6.1 %copy-start.2 = (bf16[384,8192]{1,0:T(8,128)(2,1)S(1)}, bf16[384,8192]{1,0:T(8,128)(2,1)}, u32[]{:S(2)}) copy-start(bf16[384,8192]{1,0:T(8,128)(2,1)} %all-gather.2.cloned.1.call-done) | copy-start | bytes 18874372
  97.1 6.4 %copy-start.3 = (bf16[1,192,8192]{2,1,0:T(8,128)(2,1)S(1)}, bf16[1,192,8192]{2,1,0:T(8,128)(2,1)}, u32[]{:S(2)}) copy-start(bf16[1,192,8192]{2,1,0:T(8,128)(2,1)} %param.15) | copy-start | bytes 9437188
  110.6 85.4 %copy-start.1 = (s32[1,256]{1,0:T(1,128)S(1)}, s32[1,256]{1,0:T(1,128)}, u32[]{:S(2)}) copy-start(s32[1,256]{1,0:T(1,128)} %param.10) | copy-start | bytes 3076
  110.6 99.5 %collective-permute-start.3 = (bf16[1024,512]{1,0:T(8,128)(2,1)}, bf16[1024,512]{1,0:T(8,128)(2,1)}, u32[]{:S(2)}, u32[]{:S(2)}) collective-permute-start(bf16[1024,512]{1,0:T(8,128)(2,1)} %param.9), channel_id=1, source_target_pairs={{240,0},{0,16},{16,32},{32,48},{48,64},{64,80},{80,96},{96,112},{1... | collective-permute-start | bytes 3145736 | tf_op jit(solution)/shard_map/ppermute | solution.py:13
  187.2 22.2 %all-to-all-start.1 = ((bf16[16,24,512]{2,1,0:T(8,128)(2,1)}), bf16[16,24,512]{2,1,0:T(8,128)(2,1)S(1)}, u32[]{:S(2)}, u32[]{:S(2)}) async-start(bf16[16,24,512]{2,1,0:T(8,128)(2,1)} %bitcast.74), calls=%async_computation.2 | async-start | bytes 786432 | tf_op jit(solution)/shard_map/all_to_all | solution.py:98
Sparse Core Ops, SparseCore 0:
  57.8 39.2 all-gather.1
  110.7 74.5 reduce-scatter.1

commit v8 on v7

--- a/solution.py
+++ b/solution.py
@@ -45,28 +45,29 @@
     buffer = buffer.reshape(expert_count, capacity, feature_width)
     n_exp_dev = lax.axis_size("expert")
     local_width = router.shape[0]
-    tables = jnp.concatenate([norm_gain, router[None, :]], axis=0)
+    kinds = (jnp.arange(expert_count, dtype=jnp.int32) >= expert_count // 2).astype(jnp.int32)
+    tables = jnp.stack(
+        [norm_gain[kinds], jnp.broadcast_to(router[None, :], (expert_count, local_width))], axis=1
+    )
     parts = []
     rest = tables
     for _ in range(3):
         piece = rest.astype(jnp.bfloat16)
         parts.append(piece)
         rest = rest - piece.astype(jnp.float32)
-    table_rows = tables.shape[0]
-    extra = jnp.broadcast_to(
-        jnp.concatenate(parts, axis=0)[None], (expert_count, 3 * table_rows, local_width)
-    )
-    buffer = jnp.concatenate([buffer, extra], axis=1)
+    table_rows = tables.shape[1]
+    coded_rows = 3 * table_rows
+    padded_rows = -(-coded_rows // 8) * 8
+    parts.append(jnp.zeros((expert_count, padded_rows - coded_rows, local_width), jnp.bfloat16))
+    buffer = jnp.concatenate([buffer] + parts, axis=1)
     mine = lax.all_to_all(buffer, "expert", split_axis=0, concat_axis=2, tiled=True)[0]
-    coded = mine[capacity:].astype(jnp.float32).reshape(3, table_rows, mine.shape[1])
+    coded = mine[capacity : capacity + coded_rows].astype(jnp.float32)
+    coded = coded.reshape(3, table_rows, mine.shape[1])
     tables = (coded[0] + coded[1]) + coded[2]
     mine = mine[:capacity]
 
-    gains_all = tables[:2]
-    router_all = tables[2]
-    expert_id = lax.axis_index("expert")
-    kind = (expert_id >= expert_count // 2).astype(jnp.int32)
-    gains = lax.dynamic_index_in_dim(gains_all, kind, axis=0, keepdims=False)
+    gains = tables[0]
+    router_all = tables[1]
     picked = mine.astype(jnp.float32)
     d = picked.shape[1]
     scale = lax.rsqrt(jnp.sum(picked * picked, axis=1) / d + EPS)

time: 222 us -> 218 us (0.982)
  blocking collectives: 0 us -> 29.3 us
  waiting for transfers between devices: 147 us -> 125 us
  starting transfers between devices: 22.6 us -> 12 us
  other arithmetic: 14 us -> 7.84 us
  local copies, waits for them, and re-layouts: 8.11 us -> 13.9 us
    all_to_all x0 -> x1, blocking collectives: none -> 29.3 us  [body(): lax.all_to_all(buffer, 'expert', split_axis=0, concat_axis=2, tiled=True)[0]]
    all_to_all x1 -> x0, waiting for transfers between devices: 21.7 us -> none  [body(): lax.all_to_all(buffer, 'expert', split_axis=0, concat_axis=2, tiled=True)[0]]
    all_to_all x1 -> x0, starting transfers between devices: 10.6 us -> none  [body(): lax.all_to_all(buffer, 'expert', split_axis=0, concat_axis=2, tiled=True)[0]]
    concatenate x0 -> x1, local copies, waits for them, and re-layouts: none -> 3 us  [body(): buffer = jnp.concatenate([buffer] + parts, axis=1)]
  transfers between devices with their start and end apart: 8 -> 7, of which waited for: 5 -> 4; matrix products, arithmetic and copies ran while one was open for 4% -> 5% of each run, Pallas kernels for 0% -> 0%
where the time goes in v8:
time: 218 us; the launch traced here: 216 us
  waiting for transfers between devices  125 us (57%)
  blocking collectives  29.3 us (13%)
  matrix products  14.7 us (7%)
  local copies, waits for them, and re-layouts  13.9 us (6%)
  between operations  13.6 us (6%)
  starting transfers between devices  12 us (6%)
  other arithmetic  7.84 us (4%)
    reduce_scatter x1, waiting for transfers between devices, body(): lax.psum_scatter(lax.optimization_barrier(part.astype(jnp.bfloat16)).asty...  74.4 us
    all_gather x1, waiting for transfers between devices, body(): block = lax.all_gather(normed, 'section', axis=0, tiled=True)  33.6 us
    all_to_all x1, blocking collectives, body(): lax.all_to_all(buffer, 'expert', split_axis=0, concat_axis=2, tiled=True)[0]  29.3 us
    all_to_all x1, waiting for transfers between devices, body(): lax.all_to_all(outgoing, 'expert', split_axis=0, concat_axis=0, tiled=True)  12 us
    all_to_all x1, starting transfers between devices, body(): lax.all_to_all(outgoing, 'expert', split_axis=0, concat_axis=0, tiled=True)  8.78 us
    dot_general x2, matrix products, feature_product(): lax.dot_general(block, weight, (((1,), (1,)), ((), ())), preferred_elemen...  8.29 us
    ppermute x4, waiting for transfers between devices, passed_along(): return lax.ppermute(block, axis, route)  5.07 us
    dot_general x1, matrix products, body(): part = jnp.dot(hidden, down_w[0], preferred_element_type=jnp.float32)  4.46 us
  transfers between devices with their start and end apart: 7, of which 4 were waited for; matrix products, arithmetic and copies ran while one was open for 5% of the time, Pallas kernels for 0%

profile of v8, /device:TPU:8, one launch (start us, length us, event | category | flops | bytes accessed | tf_op | source)
XLA Modules:
  0.0 216.3 jit_solution(8918394320817156904)
XLA Ops:
  6.5 2.1 collective-permute-start
  8.6 0.7 collective-permute-start.1
  9.3 1.3 gather_fusion.1
  10.6 0.7 stack_broadcast_in_dim.2
  11.3 0.6 copy.30
  12.0 0.6 copy.31
  12.6 0.6 copy.29
  13.2 0.0 collective-permute-done
  13.2 0.7 pad_add_fusion
  13.9 1.2 reduce-window.6
  15.1 0.1 slice.76
  15.2 0.1 copy.26
  15.3 0.1 fusion.12
  15.4 0.7 multiply_add_fusion
  16.1 3.3 %gather_fusion = bf16[256,512]{1,0:T(8,128)(2,1)} fusion(bf16[1024,512]{1,0:T(8,128)(2,1)} %param.9, s32[1024]{0:T(1024)S(1)} %pad_clamp_fusion.1), kind=kCustom, calls=%fused_computation | custom fusion | bytes 525312 | tf_op jit(solution)/shard_map/gather | solution.py:31
  19.4 1.2 convolution_convert_fusion.1
  20.6 0.6 broadcast_in_dim.4
  21.3 3.0 %concatenate.7 = bf16[16,32,512]{2,1,0:T(8,128)(2,1)} concatenate(bf16[16,24,512]{2,1,0:T(8,128)(2,1)S(1)} %bitcast.80, bf16[16,2,512]{2,1,0:T(2,128)(2,1)} %copy.29, bf16[16,2,512]{2,1,0:T(2,128)(2,1)} %copy.30, bf16[16,2,512]{2,1,0:T(2,128)(2,1)} %copy.31, bf16[16,2,512]{2,1,0:T(2,128)(2,1)} %broadcast_in_dim.4), dimensions={1} | concatenate | bytes 1048576 | tf_op jit(solution)/shard_map/concatenate | solution.py:62
  24.3 29.3 %all_to_all.20 = bf16[16,32,512]{2,1,0:T(8,128)(2,1)S(1)} all-to-all(bf16[16,32,512]{2,1,0:T(8,128)(2,1)} %concatenate.7), channel_id=1, replica_groups=mesh['section'=16,'expert'=16] {'expert'}, dimensions={0} | all-to-all | bytes 1048576 | tf_op jit(solution)/shard_map/all_to_all | solution.py:63
  53.6 0.1 fusion.20
  53.6 0.1 slice_add_fusion
  53.7 0.1 fusion.18
  53.8 0.1 copy.40
  53.8 0.3 multiply_reduce_fusion
  54.2 0.9 multiply_convert_fusion.1
  55.1 0.0 all-gather.2.cloned.1.call-update
  55.1 0.0 reduce-scatter.2.cloned.1.call-start
  55.1 0.1 collective-permute-start.2
  55.2 5.1 %collective-permute-done.2 = f32[24]{0:T(128)S(1)} collective-permute-done((f32[24]{0:T(128)S(1)}, f32[24]{0:T(128)S(1)}, u32[]{:S(2)}, u32[]{:S(2)}) %collective-permute-start.2) | collective-permute-done | bytes 128 | tf_op jit(solution)/shard_map/ppermute | solution.py:13
  60.3 33.6 %all-gather.2.cloned.1.call-done = bf16[384,8192]{1,0:T(8,128)(2,1)} async-done(((bf16[24,8192]{1,0:T(8,128)(2,1)}), bf16[384,8192]{1,0:T(8,128)(2,1)}) %all-gather.2.cloned.1.call-update) | async-done | bytes 6291472 | tf_op jit(solution)/shard_map/all_gather | solution.py:78
  93.9 6.1 %fusion.3 = f32[384,192]{0,1:T(8,128)S(1)} fusion(bf16[384,8192]{1,0:T(8,128)(2,1)} %all-gather.2.cloned.1.call-done, bf16[1,192,8192]{2,1,0:T(8,128)(2,1)} %param.14), kind=kOutput, calls=%fused_computation.7 | convolution fusion | flops 1207959552 | bytes 9732096 | tf_op jit(solution)/shard_map/dot_general | solution.py:17
  99.9 0.3 copy-done.3
  100.3 2.2 %multiply_convert_fusion.2 = bf16[384,192]{0,1:T(8,128)(2,1)S(1)} fusion(f32[384,192]{0,1:T(8,128)S(1)} %fusion.3, bf16[384,8192]{1,0:T(8,128)(2,1)S(1)} %copy-done.2, bf16[1,192,8192]{2,1,0:T(8,128)(2,1)S(1)} %copy-done.3), kind=kOutput, calls=%fused_computation.21 | convolution fusion | flops 1208401920 | bytes 9879552 | tf_op jit(solution)/shard_map/dot_general | solution.py:17
  102.5 0.1 slice_bitcast_fusion
  102.6 0.1 copy.33
  102.7 0.1 copy.34
  102.8 0.1 pad_maximum_fusion
  102.9 4.5 %convolution_convert_fusion = bf16[384,8192]{1,0:T(8,128)(2,1)} fusion(bf16[384,192]{1,0:T(8,128)(2,1)S(1)} %bitcast.82, bf16[1,192,8192]{2,1,0:T(8,128)(2,1)S(1)} %copy-done), kind=kOutput, calls=%fused_computation.3 | convolution fusion | flops 1211105280 | bytes 9584640 | tf_op jit(solution)/shard_map/dot_general | solution.py:88
  107.3 0.0 reduce-scatter.2.cloned.1.call-update
  107.4 0.3 collective-permute-start.3
  107.7 74.4 %reduce-scatter.2.cloned.1.call-done = bf16[24,8192]{1,0:T(8,128)(2,1)} async-done(((bf16[384,8192]{1,0:T(8,128)(2,1)}), bf16[24,8192]{1,0:T(8,128)(2,1)}) %reduce-scatter.2.cloned.1.call-update) | async-done | bytes 393232 | tf_op jit(solution)/shard_map/reduce_scatter | solution.py:89
  182.1 1.1 multiply_convert_fusion
  183.2 0.8 copy.46
  184.0 8.8 %all-to-all-start.1 = ((bf16[16,24,512]{2,1,0:T(8,128)(2,1)}), bf16[16,24,512]{2,1,0:T(8,128)(2,1)S(1)}, u32[]{:S(2)}, u32[]{:S(2)}) async-start(bf16[16,24,512]{2,1,0:T(8,128)(2,1)} %bitcast.79), calls=%async_computation.2 | async-start | bytes 786432 | tf_op jit(solution)/shard_map/all_to_all | solution.py:99
  192.8 1.4 scatter_custom_fusion
  194.2 12.0 %all-to-all-done.1 = bf16[16,24,512]{2,1,0:T(8,128)(2,1)S(1)} async-done(((bf16[16,24,512]{2,1,0:T(8,128)(2,1)}), bf16[16,24,512]{2,1,0:T(8,128)(2,1)S(1)}, u32[]{:S(2)}, u32[]{:S(2)}) %all-to-all-start.1) | async-done | bytes 393248 | tf_op jit(solution)/shard_map/all_to_all | solution.py:99
  206.1 0.8 fusion.5
  206.9 2.6 %add_convert_fusion = bf16[1024,512]{1,0:T(8,128)(2,1)} fusion(f32[1024,512]{1,0:T(8,128)S(1)} %fusion.5, bf16[1024,512]{1,0:T(8,128)(2,1)} %collective-permute-done.3), kind=kLoop, calls=%fused_computation.9 | loop fusion | flops 1572864 | bytes 4194304 | tf_op jit(solution)/shard_map/convert_element_type | solution.py:109
  (25 shorter events, 0.2 us)
Async XLA Ops:
  6.5 96.3 %copy-start = (bf16[1,192,8192]{2,1,0:T(8,128)(2,1)S(1)}, bf16[1,192,8192]{2,1,0:T(8,128)(2,1)}, u32[]{:S(2)}) copy-start(bf16[1,192,8192]{2,1,0:T(8,128)(2,1)} %param.16) | copy-start | bytes 9437188
  6.5 87.3 %all-gather.2.cloned.1.call-start = ((), (), s32[]{:S(2)}) async-start(), calls=%async_computation.3 | async-start | bytes 6684672 | tf_op jit(solution)/shard_map/all_gather | solution.py:78
  6.5 6.7 %collective-permute-start = (s32[256,1]{0,1:T(1,128)}, s32[256,1]{0,1:T(1,128)S(1)}, u32[]{:S(2)}, u32[]{:S(2)}) collective-permute-start(s32[256,1]{0,1:T(1,128)} %param.11), channel_id=1, source_target_pairs={{16,0},{32,16},{48,32},{64,48},{80,64},{96,80},{112,96},{128,112},... | collective-permute-start | bytes 3080 | tf_op jit(solution)/shard_map/ppermute | solution.py:13
  8.6 7.5 %collective-permute-start.1 = (s32[1,256]{1,0:T(1,128)}, s32[1,256]{1,0:T(1,128)S(1)}, u32[]{:S(2)}, u32[]{:S(2)}) collective-permute-start(s32[1,256]{1,0:T(1,128)} %param.10), channel_id=1, source_target_pairs={{16,0},{32,16},{48,32},{64,48},{80,64},{96,80},{112,96},{128,112},... | collective-permute-start | bytes 3080 | tf_op jit(solution)/shard_map/ppermute | solution.py:13
  55.1 127.0 %reduce-scatter.2.cloned.1.call-start = ((), (), s32[]{:S(2)}) async-start(), calls=%async_computation.4 | async-start | bytes 6684672 | tf_op jit(solution)/shard_map/reduce_scatter | solution.py:89
  55.1 5.2 %collective-permute-start.2 = (f32[24]{0:T(128)S(1)}, f32[24]{0:T(128)S(1)}, u32[]{:S(2)}, u32[]{:S(2)}) collective-permute-start(f32[24]{0:T(128)S(1)} %get-tuple-element.21), channel_id=1, source_target_pairs={{240,0},{0,16},{16,32},{32,48},{48,64},{64,80},{80,96},{96,112},{1... | collective-permute-start | bytes 296 | tf_op jit(solution)/shard_map/ppermute | solution.py:13
  93.9 6.1 %copy-start.2 = (bf16[384,8192]{1,0:T(8,128)(2,1)S(1)}, bf16[384,8192]{1,0:T(8,128)(2,1)}, u32[]{:S(2)}) copy-start(bf16[384,8192]{1,0:T(8,128)(2,1)} %all-gather.2.cloned.1.call-done) | copy-start | bytes 18874372
  93.9 6.4 %copy-start.3 = (bf16[1,192,8192]{2,1,0:T(8,128)(2,1)S(1)}, bf16[1,192,8192]{2,1,0:T(8,128)(2,1)}, u32[]{:S(2)}) copy-start(bf16[1,192,8192]{2,1,0:T(8,128)(2,1)} %param.15) | copy-start | bytes 9437188
  107.3 85.4 %copy-start.1 = (s32[1,256]{1,0:T(1,128)S(1)}, s32[1,256]{1,0:T(1,128)}, u32[]{:S(2)}) copy-start(s32[1,256]{1,0:T(1,128)} %param.10) | copy-start | bytes 3076
  107.4 99.6 %collective-permute-start.3 = (bf16[1024,512]{1,0:T(8,128)(2,1)}, bf16[1024,512]{1,0:T(8,128)(2,1)}, u32[]{:S(2)}, u32[]{:S(2)}) collective-permute-start(bf16[1024,512]{1,0:T(8,128)(2,1)} %param.9), channel_id=1, source_target_pairs={{240,0},{0,16},{16,32},{32,48},{48,64},{64,80},{80,96},{96,112},{1... | collective-permute-start | bytes 3145736 | tf_op jit(solution)/shard_map/ppermute | solution.py:13
  184.0 22.2 %all-to-all-start.1 = ((bf16[16,24,512]{2,1,0:T(8,128)(2,1)}), bf16[16,24,512]{2,1,0:T(8,128)(2,1)S(1)}, u32[]{:S(2)}, u32[]{:S(2)}) async-start(bf16[16,24,512]{2,1,0:T(8,128)(2,1)} %bitcast.79), calls=%async_computation.2 | async-start | bytes 786432 | tf_op jit(solution)/shard_map/all_to_all | solution.py:99
Sparse Core Ops, SparseCore 0:
  55.2 38.5 all-gather.1
  107.5 74.5 reduce-scatter.1

commit v9 on v8

--- a/solution.py
+++ b/solution.py
@@ -7,9 +7,15 @@
 EPS = 1e-05
 
 
+SECTION = ("chip", "core")
+
+
 def passed_along(block, axis, distance):
-    devices = range(lax.axis_size(axis))
-    route = [((i - distance) % len(devices), i) for i in devices]
+    names = axis if isinstance(axis, tuple) else (axis,)
+    count = 1
+    for name in names:
+        count *= lax.axis_size(name)
+    route = [((i - distance) % count, i) for i in range(count)]
     return lax.ppermute(block, axis, route)
 
 
@@ -20,14 +26,16 @@
 
 
 def body(activations, modality, selected, routes, norm_gain, router, gate_w, up_w, down_w):
-    n_section = lax.axis_size("section")
+    n_chip = lax.axis_size("chip")
+    n_core = lax.axis_size("core")
+    n_section = n_chip * n_core
     sel_count = selected.shape[1]
     expert_count = lax.axis_size("expert") * gate_w.shape[0]
     capacity = max(2, 3 * sel_count // (2 * expert_count))
     groups = n_section
 
-    sel_next = passed_along(selected, "section", -1)[0]
-    routes_next = passed_along(routes, "section", -1)[:, 0]
+    sel_next = passed_along(selected, SECTION, -1)[0]
+    routes_next = passed_along(routes, SECTION, -1)[:, 0]
     rows = activations[sel_next]
     both = jnp.stack([routes_next, routes[:, 0]], axis=1)
     onehot = (both[:, :, None] == jnp.arange(expert_count, dtype=jnp.int32)[None, None, :]).astype(
@@ -73,11 +81,11 @@
     scale = lax.rsqrt(jnp.sum(picked * picked, axis=1) / d + EPS)
     normed = (picked * scale[:, None] * gains[None, :]).astype(jnp.bfloat16)
     score = jax.nn.sigmoid(scale * jnp.sum(picked * gains[None, :] * router_all[None, :], axis=1))
-    score_home = passed_along(score, "section", 1)
+    score_home = passed_along(score, SECTION, 1)
 
-    block = lax.all_gather(normed, "section", axis=0, tiled=True)
+    block = lax.all_gather(normed, SECTION, axis=0, tiled=True)
     block, score_home, leaving = lax.optimization_barrier((block, score_home, activations))
-    arrived = passed_along(leaving, "section", 1)
+    arrived = passed_along(leaving, SECTION, 1)
     gate = feature_product(block, gate_w[0])
     upper = feature_product(block, up_w[0])
     hidden = (jax.nn.silu(gate) * upper).astype(jnp.bfloat16)
@@ -86,14 +94,19 @@
         groups * capacity, hidden_width
     )
     part = jnp.dot(hidden, down_w[0], preferred_element_type=jnp.float32)
-    summed = lax.psum_scatter(
+    pair = lax.psum_scatter(
         lax.optimization_barrier(part.astype(jnp.bfloat16))
         .astype(jnp.float32)
         .astype(jnp.bfloat16),
-        "section",
+        "chip",
         scatter_dimension=0,
         tiled=True,
-    )
+    ).reshape(n_core, capacity, part.shape[1])
+    core = lax.axis_index("core")
+    keep = lax.dynamic_index_in_dim(pair, core, axis=0, keepdims=False)
+    give = lax.dynamic_index_in_dim(pair, 1 - core, axis=0, keepdims=False)
+    taken = lax.ppermute(give, "core", [(0, 1), (1, 0)])
+    summed = (keep.astype(jnp.float32) + taken.astype(jnp.float32)).astype(jnp.bfloat16)
     update_rows = (score_home[:, None] * summed.astype(jnp.float32)).astype(jnp.bfloat16)
     outgoing = update_rows.reshape(capacity, n_exp_dev, local_width).transpose(1, 0, 2)
     back = lax.all_to_all(outgoing, "expert", split_axis=0, concat_axis=0, tiled=True)
@@ -110,17 +123,21 @@
 
 
 def solution(mesh):
+    n_section, n_expert = mesh.devices.shape
+    split = jax.sharding.Mesh(
+        mesh.devices.reshape(n_section // 2, 2, n_expert), ("chip", "core", "expert")
+    )
     placed = (
-        P("section", "expert"),
-        P("section"),
-        P("section", None),
-        P("section", None),
+        P(SECTION, "expert"),
+        P(SECTION),
+        P(SECTION, None),
+        P(SECTION, None),
         P(None, "expert"),
         P("expert"),
-        P("expert", "section", None),
-        P("expert", "section", None),
-        P("expert", "section", None),
+        P("expert", SECTION, None),
+        P("expert", SECTION, None),
+        P("expert", SECTION, None),
     )
     return jax.shard_map(
-        body, mesh=mesh, in_specs=placed, out_specs=P("section", "expert"), check_vma=False
+        body, mesh=split, in_specs=placed, out_specs=P(SECTION, "expert"), check_vma=False
     )

time: 218 us -> 226 us (1.037)
  waiting for transfers between devices: 125 us -> 131 us
    all_to_all x1, waiting for transfers between devices: 12 us -> 15 us  [body(): lax.all_to_all(outgoing, 'expert', split_axis=0, concat_axis=0, tiled=True)]
  transfers between devices with their start and end apart: 7 -> 8, of which waited for: 4 -> 5; matrix products, arithmetic and copies ran while one was open for 5% -> 5% of each run, Pallas kernels for 0% -> 0%
where the time goes in v9:
time: 226 us; the launch traced here: 224 us
  waiting for transfers between devices  131 us (58%)
  blocking collectives  29.3 us (13%)
  local copies, waits for them, and re-layouts  16 us (7%)
  matrix products  14.7 us (7%)
  between operations  13.6 us (6%)
  starting transfers between devices  12.3 us (5%)
  other arithmetic  7.83 us (3%)
    reduce_scatter x1, waiting for transfers between devices, body(): lax.psum_scatter(lax.optimization_barrier(part.astype(jnp.bfloat16)).asty...  75.5 us
    all_gather x1, waiting for transfers between devices, body(): block = lax.all_gather(normed, SECTION, axis=0, tiled=True)  33.5 us
    all_to_all x1, blocking collectives, body(): lax.all_to_all(buffer, 'expert', split_axis=0, concat_axis=2, tiled=True)[0]  29.3 us
    all_to_all x1, waiting for transfers between devices, body(): lax.all_to_all(outgoing, 'expert', split_axis=0, concat_axis=0, tiled=True)  15 us
    all_to_all x1, starting transfers between devices, body(): lax.all_to_all(outgoing, 'expert', split_axis=0, concat_axis=0, tiled=True)  8.95 us
    dot_general x2, matrix products, feature_product(): lax.dot_general(block, weight, (((1,), (1,)), ((), ())), preferred_elemen...  8.29 us
    ppermute x4, waiting for transfers between devices, passed_along(): return lax.ppermute(block, axis, route)  5.07 us
  transfers between devices with their start and end apart: 8, of which 5 were waited for; matrix products, arithmetic and copies ran while one was open for 5% of the time, Pallas kernels for 0%

profile of v9, /device:TPU:8, one launch (start us, length us, event | category | flops | bytes accessed | tf_op | source)
XLA Modules:
  0.0 224.4 jit_solution(9245096538287240673)
XLA Ops:
  6.5 2.1 collective-permute-start
  8.6 0.7 collective-permute-start.1
  9.3 1.3 gather_fusion.1
  10.6 0.7 stack_broadcast_in_dim.2
  11.3 0.6 copy.37
  12.0 0.6 copy.38
  12.6 0.6 copy.36
  13.2 0.7 pad_add_fusion
  13.9 1.2 reduce-window.6
  15.1 0.1 slice.76
  15.2 0.1 copy.33
  15.3 0.1 fusion.13
  15.4 0.7 multiply_add_fusion
  16.2 3.3 %gather_fusion = bf16[256,512]{1,0:T(8,128)(2,1)} fusion(bf16[1024,512]{1,0:T(8,128)(2,1)} %param.9, s32[1024]{0:T(1024)S(1)} %pad_clamp_fusion.1), kind=kCustom, calls=%fused_computation | custom fusion | bytes 525312 | tf_op jit(solution)/shard_map/gather | solution.py:39
  19.4 1.2 convolution_convert_fusion.1
  20.7 0.6 broadcast_in_dim.4
  21.3 3.0 %concatenate.7 = bf16[16,32,512]{2,1,0:T(8,128)(2,1)} concatenate(bf16[16,24,512]{2,1,0:T(8,128)(2,1)S(1)} %bitcast.83, bf16[16,2,512]{2,1,0:T(2,128)(2,1)} %copy.36, bf16[16,2,512]{2,1,0:T(2,128)(2,1)} %copy.37, bf16[16,2,512]{2,1,0:T(2,128)(2,1)} %copy.38, bf16[16,2,512]{2,1,0:T(2,128)(2,1)} %broadcast_in_dim.4), dimensions={1} | concatenate | bytes 1048576 | tf_op jit(solution)/shard_map/concatenate | solution.py:70
  24.3 29.3 %all_to_all.20 = bf16[16,32,512]{2,1,0:T(8,128)(2,1)S(1)} all-to-all(bf16[16,32,512]{2,1,0:T(8,128)(2,1)} %concatenate.7), channel_id=1, replica_groups=mesh['chip'=8,'core'=2,'expert'=16] {'expert'}, dimensions={0} | all-to-all | bytes 1048576 | tf_op jit(solution)/shard_map/all_to_all | solution.py:71
  53.6 0.1 fusion.21
  53.7 0.1 slice_add_fusion
  53.7 0.1 fusion.19
  53.8 0.1 copy.46
  53.9 0.3 multiply_reduce_fusion
  54.2 0.9 multiply_convert_fusion.1
  55.1 0.0 reduce-scatter.2.cloned.1.call-start
  55.2 0.1 collective-permute-start.2
  55.3 5.1 %collective-permute-done.2 = f32[24]{0:T(128)S(1)} collective-permute-done((f32[24]{0:T(128)S(1)}, f32[24]{0:T(128)S(1)}, u32[]{:S(2)}, u32[]{:S(2)}) %collective-permute-start.2) | collective-permute-done | bytes 128 | tf_op jit(solution)/shard_map/ppermute | solution.py:19
  60.3 33.5 %all-gather.2.cloned.1.call-done = bf16[384,8192]{1,0:T(8,128)(2,1)} async-done(((bf16[24,8192]{1,0:T(8,128)(2,1)}), bf16[384,8192]{1,0:T(8,128)(2,1)}) %all-gather.2.cloned.1.call-update) | async-done | bytes 6291472 | tf_op jit(solution)/shard_map/all_gather | solution.py:86
  93.9 6.1 %fusion.3 = f32[384,192]{0,1:T(8,128)S(1)} fusion(bf16[384,8192]{1,0:T(8,128)(2,1)} %all-gather.2.cloned.1.call-done, bf16[1,192,8192]{2,1,0:T(8,128)(2,1)} %param.14), kind=kOutput, calls=%fused_computation.7 | convolution fusion | flops 1207959552 | bytes 9732096 | tf_op jit(solution)/shard_map/dot_general | solution.py:23
  99.9 0.3 copy-done.3
  100.3 2.2 multiply_convert_fusion.2
  102.5 0.1 slice_bitcast_fusion
  102.6 0.1 copy.40
  102.7 0.1 copy.41
  102.8 0.1 pad_maximum_fusion
  102.9 4.5 %convolution_convert_fusion = bf16[384,8192]{1,0:T(8,128)(2,1)} fusion(bf16[384,192]{1,0:T(8,128)(2,1)S(1)} %bitcast.87, bf16[1,192,8192]{2,1,0:T(8,128)(2,1)S(1)} %copy-done), kind=kOutput, calls=%fused_computation.3 | convolution fusion | flops 1211105280 | bytes 9584640 | tf_op jit(solution)/shard_map/dot_general | solution.py:96
  107.4 75.5 %reduce-scatter.2.cloned.1.call-done = bf16[48,8192]{1,0:T(8,128)(2,1)} async-done(((bf16[384,8192]{1,0:T(8,128)(2,1)}), bf16[48,8192]{1,0:T(8,128)(2,1)}) %reduce-scatter.2.cloned.1.call-update) | async-done | bytes 786448 | tf_op jit(solution)/shard_map/reduce_scatter | solution.py:97
  182.9 1.8 dynamic-slice_bitcast_fusion
  184.7 0.5 collective-permute-start.3
  185.2 1.4 collective-permute-done.4
  186.6 1.1 multiply_convert_fusion
  187.8 0.1 copy.47
  187.9 1.0 copy.42
  188.9 8.9 %all-to-all-start.1 = ((bf16[16,24,512]{2,1,0:T(8,128)(2,1)}), bf16[16,24,512]{2,1,0:T(8,128)(2,1)S(1)}, u32[]{:S(2)}, u32[]{:S(2)}) async-start(bf16[16,24,512]{2,1,0:T(8,128)(2,1)} %copy.42), calls=%async_computation.2 | async-start | bytes 786432 | tf_op jit(solution)/shard_map/all_to_all | solution.py:112
  197.8 1.4 scatter_custom_fusion
  199.2 15.0 %all-to-all-done.1 = bf16[16,24,512]{2,1,0:T(8,128)(2,1)S(1)} async-done(((bf16[16,24,512]{2,1,0:T(8,128)(2,1)}), bf16[16,24,512]{2,1,0:T(8,128)(2,1)S(1)}, u32[]{:S(2)}, u32[]{:S(2)}) %all-to-all-start.1) | async-done | bytes 393248 | tf_op jit(solution)/shard_map/all_to_all | solution.py:112
  214.2 0.8 fusion.5
  215.0 2.6 %add_convert_fusion = bf16[1024,512]{1,0:T(8,128)(2,1)} fusion(f32[1024,512]{1,0:T(8,128)S(1)} %fusion.5, bf16[1024,512]{1,0:T(8,128)(2,1)} %collective-permute-done.3), kind=kLoop, calls=%fused_computation.9 | loop fusion | flops 1572864 | bytes 4194304 | tf_op jit(solution)/shard_map/convert_element_type | solution.py:122
  (29 shorter events, 0.2 us)
Async XLA Ops:
  6.5 96.3 %copy-start = (bf16[1,192,8192]{2,1,0:T(8,128)(2,1)S(1)}, bf16[1,192,8192]{2,1,0:T(8,128)(2,1)}, u32[]{:S(2)}) copy-start(bf16[1,192,8192]{2,1,0:T(8,128)(2,1)} %param.16) | copy-start | bytes 9437188
  6.5 87.3 %all-gather.2.cloned.1.call-start = ((), (), s32[]{:S(2)}) async-start(), calls=%async_computation.3 | async-start | bytes 6684672 | tf_op jit(solution)/shard_map/all_gather | solution.py:86
  6.5 6.7 %collective-permute-start = (s32[256,1]{0,1:T(1,128)}, s32[256,1]{0,1:T(1,128)S(1)}, u32[]{:S(2)}, u32[]{:S(2)}) collective-permute-start(s32[256,1]{0,1:T(1,128)} %param.11), channel_id=1, source_target_pairs={{16,0},{32,16},{48,32},{64,48},{80,64},{96,80},{112,96},{128,112},... | collective-permute-start | bytes 3080 | tf_op jit(solution)/shard_map/ppermute | solution.py:19
  8.6 7.5 %collective-permute-start.1 = (s32[1,256]{1,0:T(1,128)}, s32[1,256]{1,0:T(1,128)S(1)}, u32[]{:S(2)}, u32[]{:S(2)}) collective-permute-start(s32[1,256]{1,0:T(1,128)} %param.10), channel_id=1, source_target_pairs={{16,0},{32,16},{48,32},{64,48},{80,64},{96,80},{112,96},{128,112},... | collective-permute-start | bytes 3080 | tf_op jit(solution)/shard_map/ppermute | solution.py:19
  55.1 127.8 %reduce-scatter.2.cloned.1.call-start = ((), (), s32[]{:S(2)}) async-start(), calls=%async_computation.4 | async-start | bytes 7077888 | tf_op jit(solution)/shard_map/reduce_scatter | solution.py:97
  55.2 5.2 %collective-permute-start.2 = (f32[24]{0:T(128)S(1)}, f32[24]{0:T(128)S(1)}, u32[]{:S(2)}, u32[]{:S(2)}) collective-permute-start(f32[24]{0:T(128)S(1)} %get-tuple-element.21), channel_id=1, source_target_pairs={{240,0},{0,16},{16,32},{32,48},{48,64},{64,80},{80,96},{96,112},{1... | collective-permute-start | bytes 296 | tf_op jit(solution)/shard_map/ppermute | solution.py:19
  93.9 6.1 %copy-start.2 = (bf16[384,8192]{1,0:T(8,128)(2,1)S(1)}, bf16[384,8192]{1,0:T(8,128)(2,1)}, u32[]{:S(2)}) copy-start(bf16[384,8192]{1,0:T(8,128)(2,1)} %all-gather.2.cloned.1.call-done) | copy-start | bytes 18874372
  93.9 6.4 %copy-start.3 = (bf16[1,192,8192]{2,1,0:T(8,128)(2,1)S(1)}, bf16[1,192,8192]{2,1,0:T(8,128)(2,1)}, u32[]{:S(2)}) copy-start(bf16[1,192,8192]{2,1,0:T(8,128)(2,1)} %param.15) | copy-start | bytes 9437188
  107.4 90.4 %copy-start.1 = (s32[1,256]{1,0:T(1,128)S(1)}, s32[1,256]{1,0:T(1,128)}, u32[]{:S(2)}) copy-start(s32[1,256]{1,0:T(1,128)} %param.10) | copy-start | bytes 3076
  184.7 1.9 collective-permute-start.4
  184.7 30.3 %collective-permute-start.3 = (bf16[1024,512]{1,0:T(8,128)(2,1)}, bf16[1024,512]{1,0:T(8,128)(2,1)}, u32[]{:S(2)}, u32[]{:S(2)}) collective-permute-start(bf16[1024,512]{1,0:T(8,128)(2,1)} %param.9), channel_id=1, source_target_pairs={{240,0},{0,16},{16,32},{32,48},{48,64},{64,80},{80,96},{96,112},{1... | collective-permute-start | bytes 3145736 | tf_op jit(solution)/shard_map/ppermute | solution.py:19
  188.9 25.4 %all-to-all-start.1 = ((bf16[16,24,512]{2,1,0:T(8,128)(2,1)}), bf16[16,24,512]{2,1,0:T(8,128)(2,1)S(1)}, u32[]{:S(2)}, u32[]{:S(2)}) async-start(bf16[16,24,512]{2,1,0:T(8,128)(2,1)} %copy.42), calls=%async_computation.2 | async-start | bytes 786432 | tf_op jit(solution)/shard_map/all_to_all | solution.py:112
Sparse Core Ops, SparseCore 0:
  55.2 38.5 all-gather.1
  107.5 75.3 reduce-scatter.1

commit v10 on v9

--- a/solution.py
+++ b/solution.py
@@ -90,23 +90,24 @@
     upper = feature_product(block, up_w[0])
     hidden = (jax.nn.silu(gate) * upper).astype(jnp.bfloat16)
     hidden_width = hidden.shape[1]
-    hidden = jnp.roll(hidden.reshape(groups, capacity, hidden_width), 1, axis=0).reshape(
-        groups * capacity, hidden_width
+    order = []
+    for core in range(n_core):
+        for chip in range(n_chip):
+            order.append((chip * n_core + core - 1) % n_section)
+    hidden = jnp.take(
+        hidden.reshape(groups, capacity, hidden_width), jnp.array(order, jnp.int32), axis=0
+    ).reshape(groups * capacity, hidden_width)
+    part = jnp.dot(hidden, down_w[0], preferred_element_type=jnp.float32)
+    part = lax.optimization_barrier(part.astype(jnp.bfloat16)).astype(jnp.float32).astype(jnp.bfloat16)
+    part = part.reshape(n_core, n_chip, capacity, part.shape[1])
+    core = lax.axis_index("core")
+    keep = lax.dynamic_index_in_dim(part, core, axis=0, keepdims=False)
+    give = lax.dynamic_index_in_dim(part, 1 - core, axis=0, keepdims=False)
+    taken = lax.ppermute(give, "core", [(0, 1), (1, 0)])
+    pair = (keep.astype(jnp.float32) + taken.astype(jnp.float32)).astype(jnp.bfloat16)
+    summed = lax.psum_scatter(
+        pair.reshape(n_chip * capacity, part.shape[3]), "chip", scatter_dimension=0, tiled=True
     )
-    part = jnp.dot(hidden, down_w[0], preferred_element_type=jnp.float32)
-    pair = lax.psum_scatter(
-        lax.optimization_barrier(part.astype(jnp.bfloat16))
-        .astype(jnp.float32)
-        .astype(jnp.bfloat16),
-        "chip",
-        scatter_dimension=0,
-        tiled=True,
-    ).reshape(n_core, capacity, part.shape[1])
-    core = lax.axis_index("core")
-    keep = lax.dynamic_index_in_dim(pair, core, axis=0, keepdims=False)
-    give = lax.dynamic_index_in_dim(pair, 1 - core, axis=0, keepdims=False)
-    taken = lax.ppermute(give, "core", [(0, 1), (1, 0)])
-    summed = (keep.astype(jnp.float32) + taken.astype(jnp.float32)).astype(jnp.bfloat16)
     update_rows = (score_home[:, None] * summed.astype(jnp.float32)).astype(jnp.bfloat16)
     outgoing = update_rows.reshape(capacity, n_exp_dev, local_width).transpose(1, 0, 2)
     back = lax.all_to_all(outgoing, "expert", split_axis=0, concat_axis=0, tiled=True)

time: 226 us -> 205 us (0.907)
  waiting for transfers between devices: 131 us -> 106 us
  other arithmetic: 7.83 us -> 13.4 us
  matrix products: 14.7 us -> 12.1 us
  local copies, waits for them, and re-layouts: 16 us -> 18.4 us
    reduce_scatter x1, waiting for transfers between devices: 75.5 us -> 49.3 us  [body(): lax.psum_scatter(pair.reshape(n_chip * capacity, part.shape[3]), 'chip',...]
    convert_element_type x0 -> x1, other arithmetic: none -> 5.62 us  [body(): (keep.astype(jnp.float32) + taken.astype(jnp.float32)).astype(jnp.bfloat16)]
    ppermute x1, waiting for transfers between devices: 1.42 us -> 5.75 us  [body(): taken = lax.ppermute(give, 'core', [(0, 1), (1, 0)])]
    all_to_all x1, waiting for transfers between devices: 15 us -> 12 us  [body(): lax.all_to_all(outgoing, 'expert', split_axis=0, concat_axis=0, tiled=True)]
    dot_general x1, matrix products: 4.47 us -> 1.79 us  [body(): part = jnp.dot(hidden, down_w[0], preferred_element_type=jnp.float32)]
where the time goes in v10:
time: 205 us
  waiting for transfers between devices  106 us (52%)
  blocking collectives  29.3 us (14%)
  local copies, waits for them, and re-layouts  18.4 us (9%)
  between operations  13.7 us (7%)
  other arithmetic  13.4 us (7%)
  starting transfers between devices  12.2 us (6%)
  matrix products  12.1 us (6%)
    reduce_scatter x1, waiting for transfers between devices, body(): lax.psum_scatter(pair.reshape(n_chip * capacity, part.shape[3]), 'chip',...  49.3 us
    all_gather x1, waiting for transfers between devices, body(): block = lax.all_gather(normed, SECTION, axis=0, tiled=True)  33.5 us
    all_to_all x1, blocking collectives, body(): lax.all_to_all(buffer, 'expert', split_axis=0, concat_axis=2, tiled=True)[0]  29.3 us
    all_to_all x1, waiting for transfers between devices, body(): lax.all_to_all(outgoing, 'expert', split_axis=0, concat_axis=0, tiled=True)  12 us
    all_to_all x1, starting transfers between devices, body(): lax.all_to_all(outgoing, 'expert', split_axis=0, concat_axis=0, tiled=True)  8.69 us
    dot_general x2, matrix products, feature_product(): lax.dot_general(block, weight, (((1,), (1,)), ((), ())), preferred_elemen...  8.29 us
    ppermute x1, waiting for transfers between devices, body(): taken = lax.ppermute(give, 'core', [(0, 1), (1, 0)])  5.75 us
    convert_element_type x1, other arithmetic, body(): (keep.astype(jnp.float32) + taken.astype(jnp.float32)).astype(jnp.bfloat16)  5.62 us
  transfers between devices with their start and end apart: 8, of which 5 were waited for; matrix products, arithmetic and copies ran while one was open for 5% of the time, Pallas kernels for 0%

profile of v10, /device:TPU:8, one launch (start us, length us, event | category | flops | bytes accessed | tf_op | source)
XLA Modules:
  0.0 204.5 jit_solution(4019053144173746405)
XLA Ops:
  6.5 2.1 %collective-permute-start = (s32[256,1]{0,1:T(1,128)}, s32[256,1]{0,1:T(1,128)S(1)}, u32[]{:S(2)}, u32[]{:S(2)}) collective-permute-start(s32[256,1]{0,1:T(1,128)} %param.12), channel_id=1, source_target_pairs={{16,0},{32,16},{48,32},{64,48},{80,64},{96,80},{112,96},{128,112},... | collective-permute-start | bytes 3080 | tf_op jit(solution)/shard_map/ppermute | solution.py:19
  8.6 0.7 collective-permute-start.1
  9.3 1.3 gather_fusion.1
  10.6 0.7 stack_broadcast_in_dim.2
  11.3 0.6 copy.35
  12.0 0.7 copy.36
  12.6 0.6 copy.34
  13.3 0.7 pad_add_fusion
  14.0 1.2 reduce-window.6
  15.1 0.1 slice.60
  15.2 0.1 copy.31
  15.3 0.1 fusion.13
  15.4 0.7 multiply_add_fusion
  16.2 3.3 %gather_fusion = bf16[256,512]{1,0:T(8,128)(2,1)} fusion(bf16[1024,512]{1,0:T(8,128)(2,1)} %param.10, s32[1024]{0:T(1024)S(1)} %pad_clamp_fusion.2), kind=kCustom, calls=%fused_computation | custom fusion | bytes 525312 | tf_op jit(solution)/shard_map/gather | solution.py:39
  19.4 1.2 convolution_convert_fusion.1
  20.7 0.6 broadcast_in_dim.16
  21.3 3.0 %concatenate.3 = bf16[16,32,512]{2,1,0:T(8,128)(2,1)} concatenate(bf16[16,24,512]{2,1,0:T(8,128)(2,1)S(1)} %bitcast.84, bf16[16,2,512]{2,1,0:T(2,128)(2,1)} %copy.34, bf16[16,2,512]{2,1,0:T(2,128)(2,1)} %copy.35, bf16[16,2,512]{2,1,0:T(2,128)(2,1)} %copy.36, bf16[16,2,512]{2,1,0:T(2,128)(2,1)} %broadcast_in_dim.16), dimensions={1} | concatenate | bytes 1048576 | tf_op jit(solution)/shard_map/concatenate | solution.py:70
  24.3 29.3 %all_to_all.20 = bf16[16,32,512]{2,1,0:T(8,128)(2,1)S(1)} all-to-all(bf16[16,32,512]{2,1,0:T(8,128)(2,1)} %concatenate.3), channel_id=1, replica_groups=mesh['chip'=8,'core'=2,'expert'=16] {'expert'}, dimensions={0} | all-to-all | bytes 1048576 | tf_op jit(solution)/shard_map/all_to_all | solution.py:71
  53.6 0.1 fusion.21
  53.7 0.1 slice_add_fusion
  53.7 0.1 fusion.19
  53.8 0.1 copy.43
  53.9 0.3 multiply_reduce_fusion
  54.2 0.9 multiply_convert_fusion.1
  55.2 0.1 collective-permute-start.2
  55.3 5.1 %collective-permute-done.2 = f32[24]{0:T(128)S(1)} collective-permute-done((f32[24]{0:T(128)S(1)}, f32[24]{0:T(128)S(1)}, u32[]{:S(2)}, u32[]{:S(2)}) %collective-permute-start.2) | collective-permute-done | bytes 128 | tf_op jit(solution)/shard_map/ppermute | solution.py:19
  60.4 33.5 %all-gather.2.cloned.1.call-done = bf16[384,8192]{1,0:T(8,128)(2,1)} async-done(((bf16[24,8192]{1,0:T(8,128)(2,1)}), bf16[384,8192]{1,0:T(8,128)(2,1)}) %all-gather.2.cloned.1.call-update) | async-done | bytes 6291472 | tf_op jit(solution)/shard_map/all_gather | solution.py:86
  93.9 6.1 %fusion.4 = f32[384,192]{0,1:T(8,128)S(1)} fusion(bf16[384,8192]{1,0:T(8,128)(2,1)} %all-gather.2.cloned.1.call-done, bf16[1,192,8192]{2,1,0:T(8,128)(2,1)} %param.15), kind=kOutput, calls=%fused_computation.10 | convolution fusion | flops 1207959552 | bytes 9732096 | tf_op jit(solution)/shard_map/dot_general | solution.py:23
  99.9 0.3 copy-done.5
  100.3 2.2 %multiply_convert_fusion.2 = bf16[384,192]{0,1:T(8,128)(2,1)S(1)} fusion(f32[384,192]{0,1:T(8,128)S(1)} %fusion.4, bf16[384,8192]{1,0:T(8,128)(2,1)S(1)} %copy-done.4, bf16[1,192,8192]{2,1,0:T(8,128)(2,1)S(1)} %copy-done.5), kind=kOutput, calls=%fused_computation.24 | convolution fusion | flops 1208401920 | bytes 9879552 | tf_op jit(solution)/shard_map/dot_general | solution.py:23
  102.5 0.1 copy.38
  102.7 0.6 gather_fusion.2
  103.2 1.8 convolution_convert_fusion
  105.1 2.1 %dynamic-slice_bitcast_fusion = bf16[8,24,8192]{2,1,0:T(8,128)(2,1)} fusion(bf16[2,8,24,8192]{3,2,1,0:T(8,128)(2,1)S(1)} %bitcast.75, s32[]{:T(128)S(6)} %select_n.63), kind=kLoop, calls=%fused_computation.12 | loop fusion | bytes 6291460 | tf_op jit(solution)/shard_map/jit(dynamic_index_in_dim)/squeeze | solution.py:105
  107.1 1.6 copy-done.1
  108.7 0.2 collective-permute-start.4
  109.0 5.8 %collective-permute-done.4 = bf16[8,24,8192]{2,1,0:T(8,128)(2,1)} collective-permute-done((bf16[8,24,8192]{2,1,0:T(8,128)(2,1)}, bf16[8,24,8192]{2,1,0:T(8,128)(2,1)}, u32[]{:S(2)}, u32[]{:S(2)}) %collective-permute-start.4) | collective-permute-done | bytes 3145760 | tf_op jit(solution)/shard_map/ppermute | solution.py:106
  114.7 5.6 %fusion = bf16[8,24,8192]{2,1,0:T(8,128)(2,1)} fusion(bf16[8,24,8192]{2,1,0:T(8,128)(2,1)} %collective-permute-done.4, bf16[2,8,24,8192]{3,2,1,0:T(8,128)(2,1)} %bitcast.76, s32[]{:T(128)S(6)} %select_n.62), kind=kLoop, calls=%fused_computation.6 | loop fusion | flops 6291456 | bytes 9437188 | tf_op jit(solution)/shard_map/convert_element_type | solution.py:107
  120.4 0.3 collective-permute-start.3
  120.7 49.3 %reduce-scatter.2.cloned.1.call-done = bf16[24,8192]{1,0:T(8,128)(2,1)} async-done(((bf16[192,8192]{1,0:T(8,128)(2,1)}), bf16[24,8192]{1,0:T(8,128)(2,1)}) %reduce-scatter.2.cloned.1.call-update) | async-done | bytes 393232 | tf_op jit(solution)/shard_map/reduce_scatter | solution.py:108
  170.0 1.1 multiply_convert_fusion
  171.1 0.1 copy.44
  171.3 1.0 copy.39
  172.2 8.7 %all-to-all-start.1 = ((bf16[16,24,512]{2,1,0:T(8,128)(2,1)}), bf16[16,24,512]{2,1,0:T(8,128)(2,1)S(1)}, u32[]{:S(2)}, u32[]{:S(2)}) async-start(bf16[16,24,512]{2,1,0:T(8,128)(2,1)} %copy.39), calls=%async_computation.2 | async-start | bytes 786432 | tf_op jit(solution)/shard_map/all_to_all | solution.py:113
  181.0 1.4 scatter_custom_fusion
  182.4 12.0 %all-to-all-done.1 = bf16[16,24,512]{2,1,0:T(8,128)(2,1)S(1)} async-done(((bf16[16,24,512]{2,1,0:T(8,128)(2,1)}), bf16[16,24,512]{2,1,0:T(8,128)(2,1)S(1)}, u32[]{:S(2)}, u32[]{:S(2)}) %all-to-all-start.1) | async-done | bytes 393248 | tf_op jit(solution)/shard_map/all_to_all | solution.py:113
  194.4 0.8 fusion.6
  195.1 2.6 %add_convert_fusion = bf16[1024,512]{1,0:T(8,128)(2,1)} fusion(f32[1024,512]{1,0:T(8,128)S(1)} %fusion.6, bf16[1024,512]{1,0:T(8,128)(2,1)} %collective-permute-done.3), kind=kLoop, calls=%fused_computation.13 | loop fusion | flops 1572864 | bytes 4194304 | tf_op jit(solution)/shard_map/convert_element_type | solution.py:123
  (33 shorter events, 0.3 us)
Async XLA Ops:
  6.5 96.7 %copy-start = (bf16[1,192,8192]{2,1,0:T(8,128)(2,1)S(1)}, bf16[1,192,8192]{2,1,0:T(8,128)(2,1)}, u32[]{:S(2)}) copy-start(bf16[1,192,8192]{2,1,0:T(8,128)(2,1)} %param.17) | copy-start | bytes 9437188
  6.5 87.3 %all-gather.2.cloned.1.call-start = ((), (), s32[]{:S(2)}) async-start(), calls=%async_computation.3 | async-start | bytes 6684672 | tf_op jit(solution)/shard_map/all_gather | solution.py:86
  6.5 6.7 %collective-permute-start = (s32[256,1]{0,1:T(1,128)}, s32[256,1]{0,1:T(1,128)S(1)}, u32[]{:S(2)}, u32[]{:S(2)}) collective-permute-start(s32[256,1]{0,1:T(1,128)} %param.12), channel_id=1, source_target_pairs={{16,0},{32,16},{48,32},{64,48},{80,64},{96,80},{112,96},{128,112},... | collective-permute-start | bytes 3080 | tf_op jit(solution)/shard_map/ppermute | solution.py:19
  8.6 7.5 %collective-permute-start.1 = (s32[1,256]{1,0:T(1,128)}, s32[1,256]{1,0:T(1,128)S(1)}, u32[]{:S(2)}, u32[]{:S(2)}) collective-permute-start(s32[1,256]{1,0:T(1,128)} %param.11), channel_id=1, source_target_pairs={{16,0},{32,16},{48,32},{64,48},{80,64},{96,80},{112,96},{128,112},... | collective-permute-start | bytes 3080 | tf_op jit(solution)/shard_map/ppermute | solution.py:19
  53.6 1.6 copy-start.3
  55.1 114.9 %reduce-scatter.2.cloned.1.call-start = ((), (), s32[]{:S(2)}) async-start(), calls=%async_computation.4 | async-start | bytes 3538944 | tf_op jit(solution)/shard_map/reduce_scatter | solution.py:108
  55.2 5.2 %collective-permute-start.2 = (f32[24]{0:T(128)S(1)}, f32[24]{0:T(128)S(1)}, u32[]{:S(2)}, u32[]{:S(2)}) collective-permute-start(f32[24]{0:T(128)S(1)} %get-tuple-element.21), channel_id=1, source_target_pairs={{240,0},{0,16},{16,32},{32,48},{48,64},{64,80},{80,96},{96,112},{1... | collective-permute-start | bytes 296 | tf_op jit(solution)/shard_map/ppermute | solution.py:19
  93.9 6.1 %copy-start.4 = (bf16[384,8192]{1,0:T(8,128)(2,1)S(1)}, bf16[384,8192]{1,0:T(8,128)(2,1)}, u32[]{:S(2)}) copy-start(bf16[384,8192]{1,0:T(8,128)(2,1)} %all-gather.2.cloned.1.call-done) | copy-start | bytes 18874372
  93.9 6.4 %copy-start.5 = (bf16[1,192,8192]{2,1,0:T(8,128)(2,1)S(1)}, bf16[1,192,8192]{2,1,0:T(8,128)(2,1)}, u32[]{:S(2)}) copy-start(bf16[1,192,8192]{2,1,0:T(8,128)(2,1)} %param.16) | copy-start | bytes 9437188
  105.0 3.7 %copy-start.1 = (bf16[384,8192]{1,0:T(8,128)(2,1)}, bf16[384,8192]{1,0:T(8,128)(2,1)S(1)}, u32[]{:S(2)}) copy-start(bf16[384,8192]{1,0:T(8,128)(2,1)S(1)} %convolution_convert_fusion) | copy-start | bytes 18874372
  108.7 6.0 %collective-permute-start.4 = (bf16[8,24,8192]{2,1,0:T(8,128)(2,1)}, bf16[8,24,8192]{2,1,0:T(8,128)(2,1)}, u32[]{:S(2)}, u32[]{:S(2)}) collective-permute-start(bf16[8,24,8192]{2,1,0:T(8,128)(2,1)} %dynamic-slice_bitcast_fusion), channel_id=1, source_target_pairs={{0,16},{16,0},{1,17},{17,1},{2,18},{18,2},{3,19},{19,3},{4,20},{20... | collective-permute-start | bytes 9437192 | tf_op jit(solution)/shard_map/ppermute | solution.py:106
  120.4 60.6 %copy-start.2 = (s32[1,256]{1,0:T(1,128)S(1)}, s32[1,256]{1,0:T(1,128)}, u32[]{:S(2)}) copy-start(s32[1,256]{1,0:T(1,128)} %param.11) | copy-start | bytes 3076
  120.4 74.7 %collective-permute-start.3 = (bf16[1024,512]{1,0:T(8,128)(2,1)}, bf16[1024,512]{1,0:T(8,128)(2,1)}, u32[]{:S(2)}, u32[]{:S(2)}) collective-permute-start(bf16[1024,512]{1,0:T(8,128)(2,1)} %param.10), channel_id=1, source_target_pairs={{240,0},{0,16},{16,32},{32,48},{48,64},{64,80},{80,96},{96,112},{1... | collective-permute-start | bytes 3145736 | tf_op jit(solution)/shard_map/ppermute | solution.py:19
  172.2 22.1 %all-to-all-start.1 = ((bf16[16,24,512]{2,1,0:T(8,128)(2,1)}), bf16[16,24,512]{2,1,0:T(8,128)(2,1)S(1)}, u32[]{:S(2)}, u32[]{:S(2)}) async-start(bf16[16,24,512]{2,1,0:T(8,128)(2,1)} %copy.39), calls=%async_computation.2 | async-start | bytes 786432 | tf_op jit(solution)/shard_map/all_to_all | solution.py:113
Sparse Core Ops, SparseCore 0:
  55.2 38.5 all-gather.1
  120.5 49.4 reduce-scatter.1

commit v11 on v10

--- a/solution.py
+++ b/solution.py
@@ -97,17 +97,18 @@
     hidden = jnp.take(
         hidden.reshape(groups, capacity, hidden_width), jnp.array(order, jnp.int32), axis=0
     ).reshape(groups * capacity, hidden_width)
-    part = jnp.dot(hidden, down_w[0], preferred_element_type=jnp.float32)
-    part = lax.optimization_barrier(part.astype(jnp.bfloat16)).astype(jnp.float32).astype(jnp.bfloat16)
-    part = part.reshape(n_core, n_chip, capacity, part.shape[1])
+    hidden = hidden.reshape(n_core, n_chip * capacity, hidden_width)
     core = lax.axis_index("core")
-    keep = lax.dynamic_index_in_dim(part, core, axis=0, keepdims=False)
-    give = lax.dynamic_index_in_dim(part, 1 - core, axis=0, keepdims=False)
+
+    def down_part(rows):
+        part = jnp.dot(rows, down_w[0], preferred_element_type=jnp.float32)
+        return lax.optimization_barrier(part.astype(jnp.bfloat16)).astype(jnp.float32).astype(jnp.bfloat16)
+
+    give = down_part(lax.dynamic_index_in_dim(hidden, 1 - core, axis=0, keepdims=False))
     taken = lax.ppermute(give, "core", [(0, 1), (1, 0)])
+    keep = down_part(lax.dynamic_index_in_dim(hidden, core, axis=0, keepdims=False))
     pair = (keep.astype(jnp.float32) + taken.astype(jnp.float32)).astype(jnp.bfloat16)
-    summed = lax.psum_scatter(
-        pair.reshape(n_chip * capacity, part.shape[3]), "chip", scatter_dimension=0, tiled=True
-    )
+    summed = lax.psum_scatter(pair, "chip", scatter_dimension=0, tiled=True)
     update_rows = (score_home[:, None] * summed.astype(jnp.float32)).astype(jnp.bfloat16)
     outgoing = update_rows.reshape(capacity, n_exp_dev, local_width).transpose(1, 0, 2)
     back = lax.all_to_all(outgoing, "expert", split_axis=0, concat_axis=0, tiled=True)

time: 205 us -> 201 us (0.980)
  local copies, waits for them, and re-layouts: 18.4 us -> 14.3 us
    squeeze x1 -> x0, local copies, waits for them, and re-layouts: 2.06 us -> none  [body(): give = lax.dynamic_index_in_dim(part, 1 - core, axis=0, keepdims=False)]
  transfers between devices with their start and end apart: 8 -> 8, of which waited for: 5 -> 5; matrix products, arithmetic and copies ran while one was open for 5% -> 6% of each run, Pallas kernels for 0% -> 0%
where the time goes in v11:
time: 201 us; the launch traced here: 200 us
  waiting for transfers between devices  105 us (52%)
  blocking collectives  29.3 us (15%)
  local copies, waits for them, and re-layouts  14.3 us (7%)
  matrix products  13.9 us (7%)
  between operations  13.6 us (7%)
  other arithmetic  12.4 us (6%)
  starting transfers between devices  12.2 us (6%)
    reduce_scatter x1, waiting for transfers between devices, body(): summed = lax.psum_scatter(pair, 'chip', scatter_dimension=0, tiled=True)  49.3 us
    all_gather x1, waiting for transfers between devices, body(): block = lax.all_gather(normed, SECTION, axis=0, tiled=True)  33.5 us
    all_to_all x1, blocking collectives, body(): lax.all_to_all(buffer, 'expert', split_axis=0, concat_axis=2, tiled=True)[0]  29.3 us
    all_to_all x1, waiting for transfers between devices, body(): lax.all_to_all(outgoing, 'expert', split_axis=0, concat_axis=0, tiled=True)  12 us
    all_to_all x1, starting transfers between devices, body(): lax.all_to_all(outgoing, 'expert', split_axis=0, concat_axis=0, tiled=True)  8.78 us
    dot_general x2, matrix products, feature_product(): lax.dot_general(block, weight, (((1,), (1,)), ((), ())), preferred_elemen...  8.29 us
    ppermute x4, waiting for transfers between devices, passed_along(): return lax.ppermute(block, axis, route)  5.07 us
    ppermute x1, waiting for transfers between devices, body(): taken = lax.ppermute(give, 'core', [(0, 1), (1, 0)])  4.77 us
  transfers between devices with their start and end apart: 8, of which 5 were waited for; matrix products, arithmetic and copies ran while one was open for 6% of the time, Pallas kernels for 0%

profile of v11, /device:TPU:8, one launch (start us, length us, event | category | flops | bytes accessed | tf_op | source)
XLA Modules:
  0.0 200.4 jit_solution(6135563610206867511)
XLA Ops:
  6.5 2.1 %collective-permute-start = (s32[256,1]{0,1:T(1,128)}, s32[256,1]{0,1:T(1,128)S(1)}, u32[]{:S(2)}, u32[]{:S(2)}) collective-permute-start(s32[256,1]{0,1:T(1,128)} %param.12), channel_id=1, source_target_pairs={{16,0},{32,16},{48,32},{64,48},{80,64},{96,80},{112,96},{128,112},... | collective-permute-start | bytes 3080 | tf_op jit(solution)/shard_map/ppermute | solution.py:19
  8.6 0.7 collective-permute-start.1
  9.3 1.3 gather_fusion.1
  10.6 0.7 stack_broadcast_in_dim.2
  11.3 0.6 copy.29
  12.0 0.6 copy.30
  12.6 0.6 copy.28
  13.2 0.7 pad_add_fusion
  13.9 1.2 reduce-window.6
  15.1 0.1 slice.60
  15.2 0.1 copy.25
  15.3 0.1 fusion.17
  15.4 0.7 multiply_add_fusion
  16.2 3.3 %gather_fusion = bf16[256,512]{1,0:T(8,128)(2,1)} fusion(bf16[1024,512]{1,0:T(8,128)(2,1)} %param.10, s32[1024]{0:T(1024)S(1)} %pad_clamp_fusion.2), kind=kCustom, calls=%fused_computation | custom fusion | bytes 525312 | tf_op jit(solution)/shard_map/gather | solution.py:39
  19.4 1.2 convolution_convert_fusion.2
  20.7 0.6 broadcast_in_dim.35
  21.3 3.0 %concatenate.3 = bf16[16,32,512]{2,1,0:T(8,128)(2,1)} concatenate(bf16[16,24,512]{2,1,0:T(8,128)(2,1)S(1)} %bitcast.84, bf16[16,2,512]{2,1,0:T(2,128)(2,1)} %copy.28, bf16[16,2,512]{2,1,0:T(2,128)(2,1)} %copy.29, bf16[16,2,512]{2,1,0:T(2,128)(2,1)} %copy.30, bf16[16,2,512]{2,1,0:T(2,128)(2,1)} %broadcast_in_dim.35), dimensions={1} | concatenate | bytes 1048576 | tf_op jit(solution)/shard_map/concatenate | solution.py:70
  24.3 29.3 %all_to_all.20 = bf16[16,32,512]{2,1,0:T(8,128)(2,1)S(1)} all-to-all(bf16[16,32,512]{2,1,0:T(8,128)(2,1)} %concatenate.3), channel_id=1, replica_groups=mesh['chip'=8,'core'=2,'expert'=16] {'expert'}, dimensions={0} | all-to-all | bytes 1048576 | tf_op jit(solution)/shard_map/all_to_all | solution.py:71
  53.6 0.1 fusion.27
  53.7 0.1 slice_add_fusion
  53.7 0.1 fusion.25
  53.8 0.1 copy.38
  53.9 0.3 multiply_reduce_fusion
  54.2 0.9 multiply_convert_fusion.1
  55.1 0.0 reduce-scatter.2.cloned.1.call-start
  55.2 0.1 collective-permute-start.2
  55.3 5.1 %collective-permute-done.2 = f32[24]{0:T(128)S(1)} collective-permute-done((f32[24]{0:T(128)S(1)}, f32[24]{0:T(128)S(1)}, u32[]{:S(2)}, u32[]{:S(2)}) %collective-permute-start.2) | collective-permute-done | bytes 128 | tf_op jit(solution)/shard_map/ppermute | solution.py:19
  60.3 33.5 %all-gather.2.cloned.1.call-done = bf16[384,8192]{1,0:T(8,128)(2,1)} async-done(((bf16[24,8192]{1,0:T(8,128)(2,1)}), bf16[384,8192]{1,0:T(8,128)(2,1)}) %all-gather.2.cloned.1.call-update) | async-done | bytes 6291472 | tf_op jit(solution)/shard_map/all_gather | solution.py:86
  93.9 6.1 %fusion.4 = f32[384,192]{0,1:T(8,128)S(1)} fusion(bf16[384,8192]{1,0:T(8,128)(2,1)} %all-gather.2.cloned.1.call-done, bf16[1,192,8192]{2,1,0:T(8,128)(2,1)} %param.15), kind=kOutput, calls=%fused_computation.11 | convolution fusion | flops 1207959552 | bytes 9732096 | tf_op jit(solution)/shard_map/dot_general | solution.py:23
  99.9 0.3 copy-done.4
  100.3 2.2 %multiply_convert_fusion.2 = bf16[384,192]{0,1:T(8,128)(2,1)S(1)} fusion(f32[384,192]{0,1:T(8,128)S(1)} %fusion.4, bf16[384,8192]{1,0:T(8,128)(2,1)S(1)} %copy-done.3, bf16[1,192,8192]{2,1,0:T(8,128)(2,1)S(1)} %copy-done.4), kind=kOutput, calls=%fused_computation.25 | convolution fusion | flops 1208401920 | bytes 9879552 | tf_op jit(solution)/shard_map/dot_general | solution.py:23
  102.5 0.1 copy.32
  102.6 0.6 gather_fusion.2
  103.2 2.6 %convolution_convert_fusion = bf16[192,8192]{1,0:T(8,128)(2,1)} fusion(bf16[1,192,8192]{2,1,0:T(8,128)(2,1)S(1)} %copy-done, bf16[2,192,192]{2,1,0:T(8,128)(2,1)S(1)} %bitcast.86, s32[]{:T(128)S(6)} %select_n.53), kind=kOutput, calls=%fused_computation.4 | convolution fusion | flops 605552640 | bytes 6389764 | tf_op jit(solution)/shard_map/dot_general | solution.py:104
  105.9 0.3 collective-permute-start.4
  106.1 1.0 convolution_convert_fusion.1
  107.1 4.8 %collective-permute-done.4 = bf16[192,8192]{1,0:T(8,128)(2,1)} collective-permute-done((bf16[192,8192]{1,0:T(8,128)(2,1)}, bf16[192,8192]{1,0:T(8,128)(2,1)}, u32[]{:S(2)}, u32[]{:S(2)}) %collective-permute-start.4) | collective-permute-done | bytes 3145760 | tf_op jit(solution)/shard_map/ppermute | solution.py:108
  111.9 4.6 %add_convert_fusion = bf16[192,8192]{1,0:T(8,128)(2,1)} fusion(bf16[192,8192]{1,0:T(8,128)(2,1)} %collective-permute-done.4, bf16[192,8192]{1,0:T(8,128)(2,1)S(1)} %convolution_convert_fusion.1), kind=kLoop, calls=%fused_computation.6 | loop fusion | flops 6291456 | bytes 9437184 | tf_op jit(solution)/shard_map/convert_element_type | solution.py:110
  116.5 0.0 reduce-scatter.2.cloned.1.call-update
  116.5 0.3 collective-permute-start.3
  116.8 49.3 %reduce-scatter.2.cloned.1.call-done = bf16[24,8192]{1,0:T(8,128)(2,1)} async-done(((bf16[192,8192]{1,0:T(8,128)(2,1)}), bf16[24,8192]{1,0:T(8,128)(2,1)}) %reduce-scatter.2.cloned.1.call-update) | async-done | bytes 393232 | tf_op jit(solution)/shard_map/reduce_scatter | solution.py:111
  166.1 1.1 multiply_convert_fusion
  167.2 0.8 copy.44
  168.0 8.8 %all-to-all-start.1 = ((bf16[16,24,512]{2,1,0:T(8,128)(2,1)}), bf16[16,24,512]{2,1,0:T(8,128)(2,1)S(1)}, u32[]{:S(2)}, u32[]{:S(2)}) async-start(bf16[16,24,512]{2,1,0:T(8,128)(2,1)} %bitcast.83), calls=%async_computation.2 | async-start | bytes 786432 | tf_op jit(solution)/shard_map/all_to_all | solution.py:114
  176.8 1.4 scatter_custom_fusion
  178.2 12.0 %all-to-all-done.1 = bf16[16,24,512]{2,1,0:T(8,128)(2,1)S(1)} async-done(((bf16[16,24,512]{2,1,0:T(8,128)(2,1)}), bf16[16,24,512]{2,1,0:T(8,128)(2,1)S(1)}, u32[]{:S(2)}, u32[]{:S(2)}) %all-to-all-start.1) | async-done | bytes 393248 | tf_op jit(solution)/shard_map/all_to_all | solution.py:114
  190.2 0.8 fusion.6
  191.0 2.6 %add_convert_fusion.1 = bf16[1024,512]{1,0:T(8,128)(2,1)} fusion(f32[1024,512]{1,0:T(8,128)S(1)} %fusion.6, bf16[1024,512]{1,0:T(8,128)(2,1)} %collective-permute-done.3), kind=kLoop, calls=%fused_computation.13 | loop fusion | flops 1572864 | bytes 4194304 | tf_op jit(solution)/shard_map/convert_element_type | solution.py:124
  (30 shorter events, 0.2 us)
Async XLA Ops:
  6.5 96.7 %copy-start = (bf16[1,192,8192]{2,1,0:T(8,128)(2,1)S(1)}, bf16[1,192,8192]{2,1,0:T(8,128)(2,1)}, u32[]{:S(2)}) copy-start(bf16[1,192,8192]{2,1,0:T(8,128)(2,1)} %param.17) | copy-start | bytes 9437188
  6.5 87.3 %all-gather.2.cloned.1.call-start = ((), (), s32[]{:S(2)}) async-start(), calls=%async_computation.3 | async-start | bytes 6684672 | tf_op jit(solution)/shard_map/all_gather | solution.py:86
  6.5 6.7 %collective-permute-start = (s32[256,1]{0,1:T(1,128)}, s32[256,1]{0,1:T(1,128)S(1)}, u32[]{:S(2)}, u32[]{:S(2)}) collective-permute-start(s32[256,1]{0,1:T(1,128)} %param.12), channel_id=1, source_target_pairs={{16,0},{32,16},{48,32},{64,48},{80,64},{96,80},{112,96},{128,112},... | collective-permute-start | bytes 3080 | tf_op jit(solution)/shard_map/ppermute | solution.py:19
  8.6 7.5 %collective-permute-start.1 = (s32[1,256]{1,0:T(1,128)}, s32[1,256]{1,0:T(1,128)S(1)}, u32[]{:S(2)}, u32[]{:S(2)}) collective-permute-start(s32[1,256]{1,0:T(1,128)} %param.11), channel_id=1, source_target_pairs={{16,0},{32,16},{48,32},{64,48},{80,64},{96,80},{112,96},{128,112},... | collective-permute-start | bytes 3080 | tf_op jit(solution)/shard_map/ppermute | solution.py:19
  53.5 1.6 copy-start.2
  55.1 111.0 %reduce-scatter.2.cloned.1.call-start = ((), (), s32[]{:S(2)}) async-start(), calls=%async_computation.4 | async-start | bytes 3538944 | tf_op jit(solution)/shard_map/reduce_scatter | solution.py:111
  55.2 5.2 %collective-permute-start.2 = (f32[24]{0:T(128)S(1)}, f32[24]{0:T(128)S(1)}, u32[]{:S(2)}, u32[]{:S(2)}) collective-permute-start(f32[24]{0:T(128)S(1)} %get-tuple-element.21), channel_id=1, source_target_pairs={{240,0},{0,16},{16,32},{32,48},{48,64},{64,80},{80,96},{96,112},{1... | collective-permute-start | bytes 296 | tf_op jit(solution)/shard_map/ppermute | solution.py:19
  93.8 6.1 %copy-start.3 = (bf16[384,8192]{1,0:T(8,128)(2,1)S(1)}, bf16[384,8192]{1,0:T(8,128)(2,1)}, u32[]{:S(2)}) copy-start(bf16[384,8192]{1,0:T(8,128)(2,1)} %all-gather.2.cloned.1.call-done) | copy-start | bytes 18874372
  93.9 6.4 %copy-start.4 = (bf16[1,192,8192]{2,1,0:T(8,128)(2,1)S(1)}, bf16[1,192,8192]{2,1,0:T(8,128)(2,1)}, u32[]{:S(2)}) copy-start(bf16[1,192,8192]{2,1,0:T(8,128)(2,1)} %param.16) | copy-start | bytes 9437188
  105.9 6.0 %collective-permute-start.4 = (bf16[192,8192]{1,0:T(8,128)(2,1)}, bf16[192,8192]{1,0:T(8,128)(2,1)}, u32[]{:S(2)}, u32[]{:S(2)}) collective-permute-start(bf16[192,8192]{1,0:T(8,128)(2,1)} %convolution_convert_fusion), channel_id=1, source_target_pairs={{0,16},{16,0},{1,17},{17,1},{2,18},{18,2},{3,19},{19,3},{4,20},{20... | collective-permute-start | bytes 9437192 | tf_op jit(solution)/shard_map/ppermute | solution.py:108
  116.5 60.3 %copy-start.1 = (s32[1,256]{1,0:T(1,128)S(1)}, s32[1,256]{1,0:T(1,128)}, u32[]{:S(2)}) copy-start(s32[1,256]{1,0:T(1,128)} %param.11) | copy-start | bytes 3076
  116.5 74.4 %collective-permute-start.3 = (bf16[1024,512]{1,0:T(8,128)(2,1)}, bf16[1024,512]{1,0:T(8,128)(2,1)}, u32[]{:S(2)}, u32[]{:S(2)}) collective-permute-start(bf16[1024,512]{1,0:T(8,128)(2,1)} %param.10), channel_id=1, source_target_pairs={{240,0},{0,16},{16,32},{32,48},{48,64},{64,80},{80,96},{96,112},{1... | collective-permute-start | bytes 3145736 | tf_op jit(solution)/shard_map/ppermute | solution.py:19
  168.0 22.2 %all-to-all-start.1 = ((bf16[16,24,512]{2,1,0:T(8,128)(2,1)}), bf16[16,24,512]{2,1,0:T(8,128)(2,1)S(1)}, u32[]{:S(2)}, u32[]{:S(2)}) async-start(bf16[16,24,512]{2,1,0:T(8,128)(2,1)} %bitcast.83), calls=%async_computation.2 | async-start | bytes 786432 | tf_op jit(solution)/shard_map/all_to_all | solution.py:114
Sparse Core Ops, SparseCore 0:
  55.2 38.5 all-gather.1
  116.6 49.4 reduce-scatter.1

commit v12 on v11

--- a/solution.py
+++ b/solution.py
@@ -45,29 +45,37 @@
     targets = both * capacity + slots
     target = targets[:, 0]
     position = targets[:, 1]
-    placing = (
-        target[None, :] == jnp.arange(expert_count * capacity, dtype=jnp.int32)[:, None]
-    ).astype(jnp.bfloat16)
     feature_width = rows.shape[1]
-    buffer = jnp.dot(placing, rows, preferred_element_type=jnp.float32).astype(jnp.bfloat16)
-    buffer = buffer.reshape(expert_count, capacity, feature_width)
     n_exp_dev = lax.axis_size("expert")
     local_width = router.shape[0]
-    kinds = (jnp.arange(expert_count, dtype=jnp.int32) >= expert_count // 2).astype(jnp.int32)
-    tables = jnp.stack(
-        [norm_gain[kinds], jnp.broadcast_to(router[None, :], (expert_count, local_width))], axis=1
-    )
+    tables = jnp.concatenate([norm_gain, router[None, :]], axis=0)
+    table_count = tables.shape[0]
     parts = []
     rest = tables
     for _ in range(3):
         piece = rest.astype(jnp.bfloat16)
         parts.append(piece)
         rest = rest - piece.astype(jnp.float32)
-    table_rows = tables.shape[1]
+    sources = jnp.concatenate([rows] + parts, axis=0)
+    table_rows = 2
     coded_rows = 3 * table_rows
-    padded_rows = -(-coded_rows // 8) * 8
-    parts.append(jnp.zeros((expert_count, padded_rows - coded_rows, local_width), jnp.bfloat16))
-    buffer = jnp.concatenate([buffer] + parts, axis=1)
+    span = capacity + -(-coded_rows // 8) * 8
+    slot_of_row = jnp.arange(expert_count * span, dtype=jnp.int32)
+    row_expert = slot_of_row // span
+    row_slot = slot_of_row % span
+    row_kind = (row_expert >= expert_count // 2).astype(jnp.int32)
+    coded_index = row_slot - capacity
+    part_index = coded_index // table_rows
+    table_index = jnp.where(coded_index % table_rows == 0, row_kind, table_count - 1)
+    wanted = jnp.where(row_slot < capacity, row_expert * capacity + row_slot, -1)
+    token_hit = target[None, :] == wanted[:, None]
+    table_source = jnp.where(
+        (coded_index >= 0) & (coded_index < coded_rows), part_index * table_count + table_index, -1
+    )
+    table_hit = table_source[:, None] == jnp.arange(3 * table_count, dtype=jnp.int32)[None, :]
+    placing = jnp.concatenate([token_hit, table_hit], axis=1).astype(jnp.bfloat16)
+    buffer = jnp.dot(placing, sources, preferred_element_type=jnp.float32).astype(jnp.bfloat16)
+    buffer = buffer.reshape(expert_count, span, feature_width)
     mine = lax.all_to_all(buffer, "expert", split_axis=0, concat_axis=2, tiled=True)[0]
     coded = mine[capacity : capacity + coded_rows].astype(jnp.float32)
     coded = coded.reshape(3, table_rows, mine.shape[1])

time: 201 us -> 196 us (0.975)
  local copies, waits for them, and re-layouts: 14.3 us -> 6.83 us
  other arithmetic: 12.4 us -> 14.7 us
    concatenate x1 -> x0, local copies, waits for them, and re-layouts: 3 us -> none  [body(): buffer = jnp.concatenate([buffer] + parts, axis=1)]
where the time goes in v12:
time: 196 us
  waiting for transfers between devices  105 us (54%)
  blocking collectives  29.1 us (15%)
  other arithmetic  14.7 us (8%)
  matrix products  13.9 us (7%)
  between operations  13.6 us (7%)
  starting transfers between devices  12.1 us (6%)
  local copies, waits for them, and re-layouts  6.83 us (3%)
    reduce_scatter x1, waiting for transfers between devices, body(): summed = lax.psum_scatter(pair, 'chip', scatter_dimension=0, tiled=True)  49.3 us
    all_gather x1, waiting for transfers between devices, body(): block = lax.all_gather(normed, SECTION, axis=0, tiled=True)  34.4 us
    all_to_all x1, blocking collectives, body(): lax.all_to_all(buffer, 'expert', split_axis=0, concat_axis=2, tiled=True)[0]  29.1 us
    all_to_all x1, waiting for transfers between devices, body(): lax.all_to_all(outgoing, 'expert', split_axis=0, concat_axis=0, tiled=True)  11.9 us
    all_to_all x1, starting transfers between devices, body(): lax.all_to_all(outgoing, 'expert', split_axis=0, concat_axis=0, tiled=True)  8.69 us
    dot_general x2, matrix products, feature_product(): lax.dot_general(block, weight, (((1,), (1,)), ((), ())), preferred_elemen...  8.29 us
    ppermute x4, waiting for transfers between devices, passed_along(): return lax.ppermute(block, axis, route)  5.07 us
    ppermute x1, waiting for transfers between devices, body(): taken = lax.ppermute(give, 'core', [(0, 1), (1, 0)])  4.78 us
  transfers between devices with their start and end apart: 8, of which 5 were waited for; matrix products, arithmetic and copies ran while one was open for 6% of the time, Pallas kernels for 0%

profile of v12, /device:TPU:8, one launch (start us, length us, event | category | flops | bytes accessed | tf_op | source)
XLA Modules:
  0.0 195.8 jit_solution(11935479390198450504)
XLA Ops:
  6.5 2.1 %collective-permute-start = (s32[256,1]{0,1:T(1,128)}, s32[256,1]{0,1:T(1,128)S(1)}, u32[]{:S(2)}, u32[]{:S(2)}) collective-permute-start(s32[256,1]{0,1:T(1,128)} %param.12), channel_id=1, source_target_pairs={{16,0},{32,16},{48,32},{64,48},{80,64},{96,80},{112,96},{128,112},... | collective-permute-start | bytes 3080 | tf_op jit(solution)/shard_map/ppermute | solution.py:19
  8.6 0.7 collective-permute-start.1
  9.3 0.7 fusion.30
  10.0 0.7 fusion.25
  10.7 0.8 iota_compare_fusion.2
  11.5 0.0 collective-permute-done
  11.5 0.7 pad_add_fusion
  12.2 1.2 reduce-window.6
  13.4 0.1 slice.58
  13.5 0.1 copy.22
  13.6 0.1 fusion.23
  13.7 0.7 multiply_add_fusion
  14.4 0.6 fusion.52
  15.0 0.1 broadcast_compare_fusion
  15.1 2.6 %gather_fusion = bf16[256,512]{1,0:T(8,128)(2,1)S(1)} fusion(bf16[1024,512]{1,0:T(8,128)(2,1)} %param.10, s32[1024]{0:T(1024)S(1)} %pad_clamp_fusion.1), kind=kCustom, calls=%fused_computation | custom fusion | bytes 525312 | tf_op jit(solution)/shard_map/gather | solution.py:39
  17.7 1.3 convolution_convert_fusion.2
  19.0 29.1 %all_to_all.20 = bf16[16,32,512]{2,1,0:T(8,128)(2,1)S(1)} all-to-all(bf16[16,32,512]{2,1,0:T(8,128)(2,1)S(1)} %bitcast.85), channel_id=1, replica_groups=mesh['chip'=8,'core'=2,'expert'=16] {'expert'}, dimensions={0} | all-to-all | bytes 1048576 | tf_op jit(solution)/shard_map/all_to_all | solution.py:79
  48.1 0.1 fusion.53
  48.2 0.1 slice_add_fusion
  48.3 0.1 fusion.51
  48.3 0.1 copy.32
  48.4 0.3 multiply_reduce_fusion
  48.7 0.9 multiply_convert_fusion.1
  49.6 0.0 all-gather.2.cloned.1.call-update
  49.6 0.0 reduce-scatter.2.cloned.1.call-start
  49.7 0.1 collective-permute-start.2
  49.8 5.1 %collective-permute-done.2 = f32[24]{0:T(128)S(1)} collective-permute-done((f32[24]{0:T(128)S(1)}, f32[24]{0:T(128)S(1)}, u32[]{:S(2)}, u32[]{:S(2)}) %collective-permute-start.2) | collective-permute-done | bytes 128 | tf_op jit(solution)/shard_map/ppermute | solution.py:19
  54.9 34.4 %all-gather.2.cloned.1.call-done = bf16[384,8192]{1,0:T(8,128)(2,1)} async-done(((bf16[24,8192]{1,0:T(8,128)(2,1)}), bf16[384,8192]{1,0:T(8,128)(2,1)}) %all-gather.2.cloned.1.call-update) | async-done | bytes 6291472 | tf_op jit(solution)/shard_map/all_gather | solution.py:94
  89.3 6.1 %fusion.4 = f32[384,192]{0,1:T(8,128)S(1)} fusion(bf16[384,8192]{1,0:T(8,128)(2,1)} %all-gather.2.cloned.1.call-done, bf16[1,192,8192]{2,1,0:T(8,128)(2,1)} %param.15), kind=kOutput, calls=%fused_computation.10 | convolution fusion | flops 1207959552 | bytes 9732096 | tf_op jit(solution)/shard_map/dot_general | solution.py:23
  95.3 0.3 copy-done.4
  95.7 2.2 %multiply_convert_fusion.2 = bf16[384,192]{0,1:T(8,128)(2,1)S(1)} fusion(f32[384,192]{0,1:T(8,128)S(1)} %fusion.4, bf16[384,8192]{1,0:T(8,128)(2,1)S(1)} %copy-done.3, bf16[1,192,8192]{2,1,0:T(8,128)(2,1)S(1)} %copy-done.4), kind=kOutput, calls=%fused_computation.26 | convolution fusion | flops 1208401920 | bytes 9879552 | tf_op jit(solution)/shard_map/dot_general | solution.py:23
  97.9 0.1 copy.26
  98.1 0.6 gather_fusion.1
  98.6 2.6 %convolution_convert_fusion = bf16[192,8192]{1,0:T(8,128)(2,1)} fusion(bf16[1,192,8192]{2,1,0:T(8,128)(2,1)S(1)} %copy-done, bf16[2,192,192]{2,1,0:T(8,128)(2,1)S(1)} %bitcast.82, s32[]{:T(128)S(6)} %select_n.116), kind=kOutput, calls=%fused_computation.3 | convolution fusion | flops 605552640 | bytes 6389764 | tf_op jit(solution)/shard_map/dot_general | solution.py:112
  101.3 0.2 collective-permute-start.4
  101.5 1.0 convolution_convert_fusion.1
  102.5 4.8 %collective-permute-done.4 = bf16[192,8192]{1,0:T(8,128)(2,1)} collective-permute-done((bf16[192,8192]{1,0:T(8,128)(2,1)}, bf16[192,8192]{1,0:T(8,128)(2,1)}, u32[]{:S(2)}, u32[]{:S(2)}) %collective-permute-start.4) | collective-permute-done | bytes 3145760 | tf_op jit(solution)/shard_map/ppermute | solution.py:116
  107.3 4.6 %add_convert_fusion = bf16[192,8192]{1,0:T(8,128)(2,1)} fusion(bf16[192,8192]{1,0:T(8,128)(2,1)} %collective-permute-done.4, bf16[192,8192]{1,0:T(8,128)(2,1)S(1)} %convolution_convert_fusion.1), kind=kLoop, calls=%fused_computation.5 | loop fusion | flops 6291456 | bytes 9437184 | tf_op jit(solution)/shard_map/convert_element_type | solution.py:118
  111.9 0.0 reduce-scatter.2.cloned.1.call-update
  111.9 0.3 collective-permute-start.3
  112.3 49.3 %reduce-scatter.2.cloned.1.call-done = bf16[24,8192]{1,0:T(8,128)(2,1)} async-done(((bf16[192,8192]{1,0:T(8,128)(2,1)}), bf16[24,8192]{1,0:T(8,128)(2,1)}) %reduce-scatter.2.cloned.1.call-update) | async-done | bytes 393232 | tf_op jit(solution)/shard_map/reduce_scatter | solution.py:119
  161.5 1.1 multiply_convert_fusion
  162.7 0.8 copy.38
  163.4 8.7 %all-to-all-start.1 = ((bf16[16,24,512]{2,1,0:T(8,128)(2,1)}), bf16[16,24,512]{2,1,0:T(8,128)(2,1)S(1)}, u32[]{:S(2)}, u32[]{:S(2)}) async-start(bf16[16,24,512]{2,1,0:T(8,128)(2,1)} %bitcast.80), calls=%async_computation.2 | async-start | bytes 786432 | tf_op jit(solution)/shard_map/all_to_all | solution.py:122
  172.2 1.6 scatter_custom_fusion
  173.7 11.9 %all-to-all-done.1 = bf16[16,24,512]{2,1,0:T(8,128)(2,1)S(1)} async-done(((bf16[16,24,512]{2,1,0:T(8,128)(2,1)}), bf16[16,24,512]{2,1,0:T(8,128)(2,1)S(1)}, u32[]{:S(2)}, u32[]{:S(2)}) %all-to-all-start.1) | async-done | bytes 393248 | tf_op jit(solution)/shard_map/all_to_all | solution.py:122
  185.6 0.7 fusion.6
  186.4 2.6 %add_convert_fusion.1 = bf16[1024,512]{1,0:T(8,128)(2,1)} fusion(f32[1024,512]{1,0:T(8,128)S(1)} %fusion.6, bf16[1024,512]{1,0:T(8,128)(2,1)} %collective-permute-done.3), kind=kLoop, calls=%fused_computation.12 | loop fusion | flops 1572864 | bytes 4194304 | tf_op jit(solution)/shard_map/convert_element_type | solution.py:132
  (25 shorter events, 0.2 us)
Async XLA Ops:
  6.5 92.1 %copy-start = (bf16[1,192,8192]{2,1,0:T(8,128)(2,1)S(1)}, bf16[1,192,8192]{2,1,0:T(8,128)(2,1)}, u32[]{:S(2)}) copy-start(bf16[1,192,8192]{2,1,0:T(8,128)(2,1)} %param.17) | copy-start | bytes 9437188
  6.5 82.7 %all-gather.2.cloned.1.call-start = ((), (), s32[]{:S(2)}) async-start(), calls=%async_computation.3 | async-start | bytes 6684672 | tf_op jit(solution)/shard_map/all_gather | solution.py:94
  6.5 5.0 %collective-permute-start = (s32[256,1]{0,1:T(1,128)}, s32[256,1]{0,1:T(1,128)S(1)}, u32[]{:S(2)}, u32[]{:S(2)}) collective-permute-start(s32[256,1]{0,1:T(1,128)} %param.12), channel_id=1, source_target_pairs={{16,0},{32,16},{48,32},{64,48},{80,64},{96,80},{112,96},{128,112},... | collective-permute-start | bytes 3080 | tf_op jit(solution)/shard_map/ppermute | solution.py:19
  8.6 6.4 %collective-permute-start.1 = (s32[1,256]{1,0:T(1,128)}, s32[1,256]{1,0:T(1,128)S(1)}, u32[]{:S(2)}, u32[]{:S(2)}) collective-permute-start(s32[1,256]{1,0:T(1,128)} %param.11), channel_id=1, source_target_pairs={{16,0},{32,16},{48,32},{64,48},{80,64},{96,80},{112,96},{128,112},... | collective-permute-start | bytes 3080 | tf_op jit(solution)/shard_map/ppermute | solution.py:19
  48.1 1.6 copy-start.2
  49.6 111.9 %reduce-scatter.2.cloned.1.call-start = ((), (), s32[]{:S(2)}) async-start(), calls=%async_computation.4 | async-start | bytes 3538944 | tf_op jit(solution)/shard_map/reduce_scatter | solution.py:119
  49.7 5.2 %collective-permute-start.2 = (f32[24]{0:T(128)S(1)}, f32[24]{0:T(128)S(1)}, u32[]{:S(2)}, u32[]{:S(2)}) collective-permute-start(f32[24]{0:T(128)S(1)} %get-tuple-element.21), channel_id=1, source_target_pairs={{240,0},{0,16},{16,32},{32,48},{48,64},{64,80},{80,96},{96,112},{1... | collective-permute-start | bytes 296 | tf_op jit(solution)/shard_map/ppermute | solution.py:19
  89.3 6.1 %copy-start.3 = (bf16[384,8192]{1,0:T(8,128)(2,1)S(1)}, bf16[384,8192]{1,0:T(8,128)(2,1)}, u32[]{:S(2)}) copy-start(bf16[384,8192]{1,0:T(8,128)(2,1)} %all-gather.2.cloned.1.call-done) | copy-start | bytes 18874372
  89.3 6.4 %copy-start.4 = (bf16[1,192,8192]{2,1,0:T(8,128)(2,1)S(1)}, bf16[1,192,8192]{2,1,0:T(8,128)(2,1)}, u32[]{:S(2)}) copy-start(bf16[1,192,8192]{2,1,0:T(8,128)(2,1)} %param.16) | copy-start | bytes 9437188
  101.3 6.0 %collective-permute-start.4 = (bf16[192,8192]{1,0:T(8,128)(2,1)}, bf16[192,8192]{1,0:T(8,128)(2,1)}, u32[]{:S(2)}, u32[]{:S(2)}) collective-permute-start(bf16[192,8192]{1,0:T(8,128)(2,1)} %convolution_convert_fusion), channel_id=1, source_target_pairs={{0,16},{16,0},{1,17},{17,1},{2,18},{18,2},{3,19},{19,3},{4,20},{20... | collective-permute-start | bytes 9437192 | tf_op jit(solution)/shard_map/ppermute | solution.py:116
  111.9 60.2 %copy-start.1 = (s32[1,256]{1,0:T(1,128)S(1)}, s32[1,256]{1,0:T(1,128)}, u32[]{:S(2)}) copy-start(s32[1,256]{1,0:T(1,128)} %param.11) | copy-start | bytes 3076
  111.9 74.5 %collective-permute-start.3 = (bf16[1024,512]{1,0:T(8,128)(2,1)}, bf16[1024,512]{1,0:T(8,128)(2,1)}, u32[]{:S(2)}, u32[]{:S(2)}) collective-permute-start(bf16[1024,512]{1,0:T(8,128)(2,1)} %param.10), channel_id=1, source_target_pairs={{240,0},{0,16},{16,32},{32,48},{48,64},{64,80},{80,96},{96,112},{1... | collective-permute-start | bytes 3145736 | tf_op jit(solution)/shard_map/ppermute | solution.py:19
  163.4 22.2 %all-to-all-start.1 = ((bf16[16,24,512]{2,1,0:T(8,128)(2,1)}), bf16[16,24,512]{2,1,0:T(8,128)(2,1)S(1)}, u32[]{:S(2)}, u32[]{:S(2)}) async-start(bf16[16,24,512]{2,1,0:T(8,128)(2,1)} %bitcast.80), calls=%async_computation.2 | async-start | bytes 786432 | tf_op jit(solution)/shard_map/all_to_all | solution.py:122
Sparse Core Ops, SparseCore 0:
  49.8 39.4 all-gather.1
  112.1 49.4 reduce-scatter.1

commit v13 on v12

--- a/solution.py
+++ b/solution.py
@@ -114,8 +114,12 @@
 
     give = down_part(lax.dynamic_index_in_dim(hidden, 1 - core, axis=0, keepdims=False))
     taken = lax.ppermute(give, "core", [(0, 1), (1, 0)])
-    keep = down_part(lax.dynamic_index_in_dim(hidden, core, axis=0, keepdims=False))
-    pair = (keep.astype(jnp.float32) + taken.astype(jnp.float32)).astype(jnp.bfloat16)
+    keep = jnp.dot(
+        lax.dynamic_index_in_dim(hidden, core, axis=0, keepdims=False),
+        down_w[0],
+        preferred_element_type=jnp.float32,
+    )
+    pair = (keep + taken.astype(jnp.float32)).astype(jnp.bfloat16)
     summed = lax.psum_scatter(pair, "chip", scatter_dimension=0, tiled=True)
     update_rows = (score_home[:, None] * summed.astype(jnp.float32)).astype(jnp.bfloat16)
     outgoing = update_rows.reshape(capacity, n_exp_dev, local_width).transpose(1, 0, 2)

time: 196 us -> 197 us (level)
  other arithmetic: 14.7 us -> 10.1 us
  matrix products: 13.9 us -> 17.5 us
    convert_element_type x1 -> x0, other arithmetic: 4.62 us -> none  [body(): (keep.astype(jnp.float32) + taken.astype(jnp.float32)).astype(jnp.bfloat16)]
    dot_general x0 -> x1, matrix products: none -> 4.52 us  [body(): jnp.dot(lax.dynamic_index_in_dim(hidden, core, axis=0, keepdims=False), d...]
  transfers between devices with their start and end apart: 8 -> 8, of which waited for: 5 -> 5; matrix products, arithmetic and copies ran while one was open for 6% -> 5% of each run, Pallas kernels for 0% -> 0%
where the time goes in v13:
time: 197 us; the launch traced here: 196 us
  waiting for transfers between devices  106 us (54%)
  blocking collectives  29.1 us (15%)
  matrix products  17.5 us (9%)
  between operations  13.6 us (7%)
  starting transfers between devices  12.4 us (6%)
  other arithmetic  10.1 us (5%)
  local copies, waits for them, and re-layouts  6.83 us (3%)
    reduce_scatter x1, waiting for transfers between devices, body(): summed = lax.psum_scatter(pair, 'chip', scatter_dimension=0, tiled=True)  49.3 us
    all_gather x1, waiting for transfers between devices, body(): block = lax.all_gather(normed, SECTION, axis=0, tiled=True)  34.4 us
    all_to_all x1, blocking collectives, body(): lax.all_to_all(buffer, 'expert', split_axis=0, concat_axis=2, tiled=True)[0]  29.1 us
    all_to_all x1, waiting for transfers between devices, body(): lax.all_to_all(outgoing, 'expert', split_axis=0, concat_axis=0, tiled=True)  11.8 us
    all_to_all x1, starting transfers between devices, body(): lax.all_to_all(outgoing, 'expert', split_axis=0, concat_axis=0, tiled=True)  8.81 us
    dot_general x2, matrix products, feature_product(): lax.dot_general(block, weight, (((1,), (1,)), ((), ())), preferred_elemen...  8.29 us
    ppermute x1, waiting for transfers between devices, body(): taken = lax.ppermute(give, 'core', [(0, 1), (1, 0)])  5.76 us
    ppermute x4, waiting for transfers between devices, passed_along(): return lax.ppermute(block, axis, route)  5.07 us
  transfers between devices with their start and end apart: 8, of which 5 were waited for; matrix products, arithmetic and copies ran while one was open for 5% of the time, Pallas kernels for 0%

profile of v13, /device:TPU:8, one launch (start us, length us, event | category | flops | bytes accessed | tf_op | source)
XLA Modules:
  0.0 195.9 jit_solution(5591012348736804551)
XLA Ops:
  6.5 2.1 %collective-permute-start = (s32[256,1]{0,1:T(1,128)}, s32[256,1]{0,1:T(1,128)S(1)}, u32[]{:S(2)}, u32[]{:S(2)}) collective-permute-start(s32[256,1]{0,1:T(1,128)} %param.12), channel_id=1, source_target_pairs={{16,0},{32,16},{48,32},{64,48},{80,64},{96,80},{112,96},{128,112},... | collective-permute-start | bytes 3080 | tf_op jit(solution)/shard_map/ppermute | solution.py:19
  8.6 0.7 collective-permute-start.1
  9.3 0.7 fusion.33
  10.0 0.7 fusion.28
  10.7 0.8 iota_compare_fusion.2
  11.5 0.0 collective-permute-done
  11.5 0.7 pad_add_fusion
  12.2 1.2 reduce-window.6
  13.4 0.1 slice.58
  13.5 0.1 copy.22
  13.6 0.1 fusion.26
  13.7 0.7 multiply_add_fusion
  14.4 0.6 fusion.55
  15.0 0.0 collective-permute-done.1
  15.0 0.1 broadcast_compare_fusion
  15.1 2.6 %gather_fusion = bf16[256,512]{1,0:T(8,128)(2,1)S(1)} fusion(bf16[1024,512]{1,0:T(8,128)(2,1)} %param.10, s32[1024]{0:T(1024)S(1)} %pad_clamp_fusion.1), kind=kCustom, calls=%fused_computation | custom fusion | bytes 525312 | tf_op jit(solution)/shard_map/gather | solution.py:39
  17.7 1.3 convolution_convert_fusion.1
  19.0 29.1 %all_to_all.20 = bf16[16,32,512]{2,1,0:T(8,128)(2,1)S(1)} all-to-all(bf16[16,32,512]{2,1,0:T(8,128)(2,1)S(1)} %bitcast.87), channel_id=1, replica_groups=mesh['chip'=8,'core'=2,'expert'=16] {'expert'}, dimensions={0} | all-to-all | bytes 1048576 | tf_op jit(solution)/shard_map/all_to_all | solution.py:79
  48.1 0.1 fusion.56
  48.2 0.1 slice_add_fusion
  48.3 0.1 fusion.54
  48.3 0.1 copy.32
  48.4 0.3 multiply_reduce_fusion
  48.7 0.9 multiply_convert_fusion.1
  49.6 0.0 all-gather.2.cloned.1.call-update
  49.6 0.0 reduce-scatter.2.cloned.1.call-start
  49.7 0.1 collective-permute-start.2
  49.8 5.1 %collective-permute-done.2 = f32[24]{0:T(128)S(1)} collective-permute-done((f32[24]{0:T(128)S(1)}, f32[24]{0:T(128)S(1)}, u32[]{:S(2)}, u32[]{:S(2)}) %collective-permute-start.2) | collective-permute-done | bytes 128 | tf_op jit(solution)/shard_map/ppermute | solution.py:19
  54.9 34.4 %all-gather.2.cloned.1.call-done = bf16[384,8192]{1,0:T(8,128)(2,1)} async-done(((bf16[24,8192]{1,0:T(8,128)(2,1)}), bf16[384,8192]{1,0:T(8,128)(2,1)}) %all-gather.2.cloned.1.call-update) | async-done | bytes 6291472 | tf_op jit(solution)/shard_map/all_gather | solution.py:94
  89.3 6.1 %fusion.7 = f32[384,192]{0,1:T(8,128)S(1)} fusion(bf16[384,8192]{1,0:T(8,128)(2,1)} %all-gather.2.cloned.1.call-done, bf16[1,192,8192]{2,1,0:T(8,128)(2,1)} %param.15), kind=kOutput, calls=%fused_computation.10 | convolution fusion | flops 1207959552 | bytes 9732096 | tf_op jit(solution)/shard_map/dot_general | solution.py:23
  95.3 0.3 copy-done.4
  95.7 2.2 %multiply_convert_fusion.2 = bf16[384,192]{0,1:T(8,128)(2,1)S(1)} fusion(f32[384,192]{0,1:T(8,128)S(1)} %fusion.7, bf16[384,8192]{1,0:T(8,128)(2,1)S(1)} %copy-done.3, bf16[1,192,8192]{2,1,0:T(8,128)(2,1)S(1)} %copy-done.4), kind=kOutput, calls=%fused_computation.26 | convolution fusion | flops 1208401920 | bytes 9879552 | tf_op jit(solution)/shard_map/dot_general | solution.py:23
  97.9 0.1 copy.26
  98.1 0.6 gather_fusion.1
  98.6 2.6 %convolution_convert_fusion = bf16[192,8192]{1,0:T(8,128)(2,1)} fusion(bf16[1,192,8192]{2,1,0:T(8,128)(2,1)S(1)} %copy-done, bf16[2,192,192]{2,1,0:T(8,128)(2,1)S(1)} %bitcast.84, s32[]{:T(128)S(6)} %select_n.116), kind=kOutput, calls=%fused_computation.3 | convolution fusion | flops 605552640 | bytes 6389764 | tf_op jit(solution)/shard_map/dot_general | solution.py:112
  101.3 0.2 collective-permute-start.4
  101.5 5.8 %collective-permute-done.4 = bf16[192,8192]{1,0:T(8,128)(2,1)} collective-permute-done((bf16[192,8192]{1,0:T(8,128)(2,1)}, bf16[192,8192]{1,0:T(8,128)(2,1)}, u32[]{:S(2)}, u32[]{:S(2)}) %collective-permute-start.4) | collective-permute-done | bytes 3145760 | tf_op jit(solution)/shard_map/ppermute | solution.py:116
  107.3 4.5 %add_convert_fusion = bf16[192,8192]{1,0:T(8,128)(2,1)} fusion(bf16[192,8192]{1,0:T(8,128)(2,1)} %collective-permute-done.4, bf16[1,192,8192]{2,1,0:T(8,128)(2,1)S(1)} %copy-done, bf16[2,192,192]{2,1,0:T(8,128)(2,1)S(1)} %bitcast.85, s32[]{:T(128)S(6)} %select_n.115), kind=kOutput, calls=%fused_computation.4 | convolution fusion | flops 608698368 | bytes 9535492 | tf_op jit(solution)/shard_map/dot_general | solution.py:117
  111.8 0.0 reduce-scatter.2.cloned.1.call-update
  111.8 0.5 collective-permute-start.3
  112.3 49.3 %reduce-scatter.2.cloned.1.call-done = bf16[24,8192]{1,0:T(8,128)(2,1)} async-done(((bf16[192,8192]{1,0:T(8,128)(2,1)}), bf16[24,8192]{1,0:T(8,128)(2,1)}) %reduce-scatter.2.cloned.1.call-update) | async-done | bytes 393232 | tf_op jit(solution)/shard_map/reduce_scatter | solution.py:123
  161.6 1.1 multiply_convert_fusion
  162.8 0.8 copy.38
  163.5 8.8 %all-to-all-start.1 = ((bf16[16,24,512]{2,1,0:T(8,128)(2,1)}), bf16[16,24,512]{2,1,0:T(8,128)(2,1)S(1)}, u32[]{:S(2)}, u32[]{:S(2)}) async-start(bf16[16,24,512]{2,1,0:T(8,128)(2,1)} %bitcast.82), calls=%async_computation.2 | async-start | bytes 786432 | tf_op jit(solution)/shard_map/all_to_all | solution.py:126
  172.4 1.6 scatter_custom_fusion
  173.9 11.8 %all-to-all-done.1 = bf16[16,24,512]{2,1,0:T(8,128)(2,1)S(1)} async-done(((bf16[16,24,512]{2,1,0:T(8,128)(2,1)}), bf16[16,24,512]{2,1,0:T(8,128)(2,1)S(1)}, u32[]{:S(2)}, u32[]{:S(2)}) %all-to-all-start.1) | async-done | bytes 393248 | tf_op jit(solution)/shard_map/all_to_all | solution.py:126
  185.7 0.8 fusion.9
  186.5 2.6 %add_convert_fusion.1 = bf16[1024,512]{1,0:T(8,128)(2,1)} fusion(f32[1024,512]{1,0:T(8,128)S(1)} %fusion.9, bf16[1024,512]{1,0:T(8,128)(2,1)} %collective-permute-done.3), kind=kLoop, calls=%fused_computation.12 | loop fusion | flops 1572864 | bytes 4194304 | tf_op jit(solution)/shard_map/convert_element_type | solution.py:136
  (24 shorter events, 0.2 us)
Async XLA Ops:
  6.5 92.1 %copy-start = (bf16[1,192,8192]{2,1,0:T(8,128)(2,1)S(1)}, bf16[1,192,8192]{2,1,0:T(8,128)(2,1)}, u32[]{:S(2)}) copy-start(bf16[1,192,8192]{2,1,0:T(8,128)(2,1)} %param.17) | copy-start | bytes 9437188
  6.5 82.7 %all-gather.2.cloned.1.call-start = ((), (), s32[]{:S(2)}) async-start(), calls=%async_computation.3 | async-start | bytes 6684672 | tf_op jit(solution)/shard_map/all_gather | solution.py:94
  6.5 5.0 %collective-permute-start = (s32[256,1]{0,1:T(1,128)}, s32[256,1]{0,1:T(1,128)S(1)}, u32[]{:S(2)}, u32[]{:S(2)}) collective-permute-start(s32[256,1]{0,1:T(1,128)} %param.12), channel_id=1, source_target_pairs={{16,0},{32,16},{48,32},{64,48},{80,64},{96,80},{112,96},{128,112},... | collective-permute-start | bytes 3080 | tf_op jit(solution)/shard_map/ppermute | solution.py:19
  8.6 6.4 %collective-permute-start.1 = (s32[1,256]{1,0:T(1,128)}, s32[1,256]{1,0:T(1,128)S(1)}, u32[]{:S(2)}, u32[]{:S(2)}) collective-permute-start(s32[1,256]{1,0:T(1,128)} %param.11), channel_id=1, source_target_pairs={{16,0},{32,16},{48,32},{64,48},{80,64},{96,80},{112,96},{128,112},... | collective-permute-start | bytes 3080 | tf_op jit(solution)/shard_map/ppermute | solution.py:19
  48.1 1.6 copy-start.2
  49.6 112.0 %reduce-scatter.2.cloned.1.call-start = ((), (), s32[]{:S(2)}) async-start(), calls=%async_computation.4 | async-start | bytes 3538944 | tf_op jit(solution)/shard_map/reduce_scatter | solution.py:123
  49.7 5.2 %collective-permute-start.2 = (f32[24]{0:T(128)S(1)}, f32[24]{0:T(128)S(1)}, u32[]{:S(2)}, u32[]{:S(2)}) collective-permute-start(f32[24]{0:T(128)S(1)} %get-tuple-element.21), channel_id=1, source_target_pairs={{240,0},{0,16},{16,32},{32,48},{48,64},{64,80},{80,96},{96,112},{1... | collective-permute-start | bytes 296 | tf_op jit(solution)/shard_map/ppermute | solution.py:19
  89.3 6.1 %copy-start.3 = (bf16[384,8192]{1,0:T(8,128)(2,1)S(1)}, bf16[384,8192]{1,0:T(8,128)(2,1)}, u32[]{:S(2)}) copy-start(bf16[384,8192]{1,0:T(8,128)(2,1)} %all-gather.2.cloned.1.call-done) | copy-start | bytes 18874372
  89.3 6.4 %copy-start.4 = (bf16[1,192,8192]{2,1,0:T(8,128)(2,1)S(1)}, bf16[1,192,8192]{2,1,0:T(8,128)(2,1)}, u32[]{:S(2)}) copy-start(bf16[1,192,8192]{2,1,0:T(8,128)(2,1)} %param.16) | copy-start | bytes 9437188
  101.3 6.0 %collective-permute-start.4 = (bf16[192,8192]{1,0:T(8,128)(2,1)}, bf16[192,8192]{1,0:T(8,128)(2,1)}, u32[]{:S(2)}, u32[]{:S(2)}) collective-permute-start(bf16[192,8192]{1,0:T(8,128)(2,1)} %convolution_convert_fusion), channel_id=1, source_target_pairs={{0,16},{16,0},{1,17},{17,1},{2,18},{18,2},{3,19},{19,3},{4,20},{20... | collective-permute-start | bytes 9437192 | tf_op jit(solution)/shard_map/ppermute | solution.py:116
  111.8 60.5 %copy-start.1 = (s32[1,256]{1,0:T(1,128)S(1)}, s32[1,256]{1,0:T(1,128)}, u32[]{:S(2)}) copy-start(s32[1,256]{1,0:T(1,128)} %param.11) | copy-start | bytes 3076
  111.8 74.7 %collective-permute-start.3 = (bf16[1024,512]{1,0:T(8,128)(2,1)}, bf16[1024,512]{1,0:T(8,128)(2,1)}, u32[]{:S(2)}, u32[]{:S(2)}) collective-permute-start(bf16[1024,512]{1,0:T(8,128)(2,1)} %param.10), channel_id=1, source_target_pairs={{240,0},{0,16},{16,32},{32,48},{48,64},{64,80},{80,96},{96,112},{1... | collective-permute-start | bytes 3145736 | tf_op jit(solution)/shard_map/ppermute | solution.py:19
  163.5 22.2 %all-to-all-start.1 = ((bf16[16,24,512]{2,1,0:T(8,128)(2,1)}), bf16[16,24,512]{2,1,0:T(8,128)(2,1)S(1)}, u32[]{:S(2)}, u32[]{:S(2)}) async-start(bf16[16,24,512]{2,1,0:T(8,128)(2,1)} %bitcast.82), calls=%async_computation.2 | async-start | bytes 786432 | tf_op jit(solution)/shard_map/all_to_all | solution.py:126
Sparse Core Ops, SparseCore 0:
  49.8 39.4 all-gather.1
  112.0 49.6 reduce-scatter.1

commit v14 on v12

--- a/solution.py
+++ b/solution.py
@@ -91,30 +91,28 @@
     score = jax.nn.sigmoid(scale * jnp.sum(picked * gains[None, :] * router_all[None, :], axis=1))
     score_home = passed_along(score, SECTION, 1)
 
-    block = lax.all_gather(normed, SECTION, axis=0, tiled=True)
+    block = lax.all_gather(normed, ("core", "chip"), axis=0, tiled=True)
     block, score_home, leaving = lax.optimization_barrier((block, score_home, activations))
     arrived = passed_along(leaving, SECTION, 1)
-    gate = feature_product(block, gate_w[0])
-    upper = feature_product(block, up_w[0])
-    hidden = (jax.nn.silu(gate) * upper).astype(jnp.bfloat16)
-    hidden_width = hidden.shape[1]
-    order = []
-    for core in range(n_core):
-        for chip in range(n_chip):
-            order.append((chip * n_core + core - 1) % n_section)
-    hidden = jnp.take(
-        hidden.reshape(groups, capacity, hidden_width), jnp.array(order, jnp.int32), axis=0
-    ).reshape(groups * capacity, hidden_width)
-    hidden = hidden.reshape(n_core, n_chip * capacity, hidden_width)
+    block = block.reshape(n_core, n_chip * capacity, block.shape[1])
     core = lax.axis_index("core")
 
-    def down_part(rows):
-        part = jnp.dot(rows, down_w[0], preferred_element_type=jnp.float32)
-        return lax.optimization_barrier(part.astype(jnp.bfloat16)).astype(jnp.float32).astype(jnp.bfloat16)
+    def partial_rows(half):
+        rows = lax.dynamic_index_in_dim(block, half, axis=0, keepdims=False)
+        gate = feature_product(rows, gate_w[0])
+        upper = feature_product(rows, up_w[0])
+        hidden = (jax.nn.silu(gate) * upper).astype(jnp.bfloat16)
+        hidden = hidden.reshape(n_chip, capacity, hidden.shape[1])
+        doubled = jnp.concatenate([hidden, hidden], axis=0)
+        hidden = lax.dynamic_slice_in_dim(doubled, n_chip - half, n_chip, axis=0)
+        hidden = hidden.reshape(n_chip * capacity, hidden.shape[2])
+        return jnp.dot(hidden, down_w[0], preferred_element_type=jnp.float32)
 
-    give = down_part(lax.dynamic_index_in_dim(hidden, 1 - core, axis=0, keepdims=False))
+    give = partial_rows(core)
+    give = lax.optimization_barrier(give.astype(jnp.bfloat16)).astype(jnp.float32).astype(jnp.bfloat16)
     taken = lax.ppermute(give, "core", [(0, 1), (1, 0)])
-    keep = down_part(lax.dynamic_index_in_dim(hidden, core, axis=0, keepdims=False))
+    keep = partial_rows(1 - core)
+    keep = lax.optimization_barrier(keep.astype(jnp.bfloat16)).astype(jnp.float32).astype(jnp.bfloat16)
     pair = (keep.astype(jnp.float32) + taken.astype(jnp.float32)).astype(jnp.bfloat16)
     summed = lax.psum_scatter(pair, "chip", scatter_dimension=0, tiled=True)
     update_rows = (score_home[:, None] * summed.astype(jnp.float32)).astype(jnp.bfloat16)

time: 196 us -> 197 us (level)
  matrix products: 13.9 us -> 19.4 us
  waiting for transfers between devices: 105 us -> 101 us
    dot_general x2 -> x4, matrix products: 8.29 us -> 13.7 us  [feature_product(): lax.dot_general(block, weight, (((1,), (1,)), ((), ())), preferred_elemen...]
    ppermute x1, waiting for transfers between devices: 4.78 us -> 0.01 us  [body(): taken = lax.ppermute(give, 'core', [(0, 1), (1, 0)])]
  transfers between devices with their start and end apart: 8 -> 8, of which waited for: 5 -> 4; matrix products, arithmetic and copies ran while one was open for 6% -> 9% of each run, Pallas kernels for 0% -> 0%
where the time goes in v14:
time: 197 us; the launch traced here: 196 us
  waiting for transfers between devices  101 us (51%)
  blocking collectives  29.1 us (15%)
  matrix products  19.4 us (10%)
  other arithmetic  14.9 us (8%)
  between operations  13.6 us (7%)
  starting transfers between devices  11.8 us (6%)
  local copies, waits for them, and re-layouts  6.41 us (3%)
    reduce_scatter x1, waiting for transfers between devices, body(): summed = lax.psum_scatter(pair, 'chip', scatter_dimension=0, tiled=True)  49.2 us
    all_gather x1, waiting for transfers between devices, body(): block = lax.all_gather(normed, ('core', 'chip'), axis=0, tiled=True)  34.4 us
    all_to_all x1, blocking collectives, body(): lax.all_to_all(buffer, 'expert', split_axis=0, concat_axis=2, tiled=True)[0]  29.1 us
    dot_general x4, matrix products, feature_product(): lax.dot_general(block, weight, (((1,), (1,)), ((), ())), preferred_elemen...  13.7 us
    all_to_all x1, waiting for transfers between devices, body(): lax.all_to_all(outgoing, 'expert', split_axis=0, concat_axis=0, tiled=True)  11.9 us
    all_to_all x1, starting transfers between devices, body(): lax.all_to_all(outgoing, 'expert', split_axis=0, concat_axis=0, tiled=True)  8.36 us
    ppermute x4, waiting for transfers between devices, passed_along(): return lax.ppermute(block, axis, route)  5.07 us
    convert_element_type x1, other arithmetic, body(): (keep.astype(jnp.float32) + taken.astype(jnp.float32)).astype(jnp.bfloat16)  4.61 us
  transfers between devices with their start and end apart: 8, of which 4 were waited for; matrix products, arithmetic and copies ran while one was open for 9% of the time, Pallas kernels for 0%

profile of v14, /device:TPU:8, one launch (start us, length us, event | category | flops | bytes accessed | tf_op | source)
XLA Modules:
  0.0 195.8 jit_solution(17328034875915408159)
XLA Ops:
  6.5 2.1 %collective-permute-start = (s32[256,1]{0,1:T(1,128)}, s32[256,1]{0,1:T(1,128)S(1)}, u32[]{:S(2)}, u32[]{:S(2)}) collective-permute-start(s32[256,1]{0,1:T(1,128)} %param.11), channel_id=1, source_target_pairs={{16,0},{32,16},{48,32},{64,48},{80,64},{96,80},{112,96},{128,112},... | collective-permute-start | bytes 3080 | tf_op jit(solution)/shard_map/ppermute | solution.py:19
  8.6 0.7 collective-permute-start.1
  9.3 0.8 iota_compare_fusion.2
  10.1 0.7 fusion.60
  10.8 0.7 fusion.55
  11.5 0.7 pad_add_fusion
  12.2 1.2 reduce-window.6
  13.4 0.1 slice.56
  13.5 0.1 copy.20
  13.6 0.1 fusion.53
  13.7 0.7 multiply_add_fusion
  14.4 0.5 fusion.84
  15.0 0.1 broadcast_compare_fusion
  15.1 2.6 %gather_fusion = bf16[256,512]{1,0:T(8,128)(2,1)S(1)} fusion(bf16[1024,512]{1,0:T(8,128)(2,1)} %param.9, s32[1024]{0:T(1024)S(1)} %pad_clamp_fusion), kind=kCustom, calls=%fused_computation | custom fusion | bytes 525312 | tf_op jit(solution)/shard_map/gather | solution.py:39
  17.7 1.3 convolution_convert_fusion.2
  19.0 29.1 %all_to_all.20 = bf16[16,32,512]{2,1,0:T(8,128)(2,1)S(1)} all-to-all(bf16[16,32,512]{2,1,0:T(8,128)(2,1)S(1)} %bitcast.111), channel_id=1, replica_groups=mesh['chip'=8,'core'=2,'expert'=16] {'expert'}, dimensions={0} | all-to-all | bytes 1048576 | tf_op jit(solution)/shard_map/all_to_all | solution.py:79
  48.1 0.1 fusion.85
  48.2 0.1 slice_add_fusion
  48.2 0.1 fusion.83
  48.3 0.1 copy.29
  48.4 0.3 multiply_reduce_fusion
  48.7 0.9 multiply_convert_fusion.1
  49.6 0.0 all-gather.2.cloned.1.call-update
  49.6 0.0 reduce-scatter.2.cloned.1.call-start
  49.7 0.1 collective-permute-start.2
  49.8 5.1 %collective-permute-done.2 = f32[24]{0:T(128)S(1)} collective-permute-done((f32[24]{0:T(128)S(1)}, f32[24]{0:T(128)S(1)}, u32[]{:S(2)}, u32[]{:S(2)}) %collective-permute-start.2) | collective-permute-done | bytes 128 | tf_op jit(solution)/shard_map/ppermute | solution.py:19
  54.8 34.4 %all-gather.2.cloned.1.call-done = bf16[384,8192]{1,0:T(8,128)(2,1)} async-done(((bf16[24,8192]{1,0:T(8,128)(2,1)}), bf16[384,8192]{1,0:T(8,128)(2,1)}) %all-gather.2.cloned.1.call-update) | async-done | bytes 6291472 | tf_op jit(solution)/shard_map/all_gather | solution.py:94
  89.2 4.0 %fusion.2 = f32[192,192]{1,0:T(8,128)S(1)} fusion(bf16[1,192,8192]{2,1,0:T(8,128)(2,1)} %param.14, bf16[2,192,8192]{2,1,0:T(8,128)(2,1)} %bitcast.124, s32[]{:T(128)S(6)} %select_n.111), kind=kOutput, calls=%fused_computation.7 | convolution fusion | flops 603979776 | bytes 6438916 | tf_op jit(solution)/shard_map/dot_general | solution.py:23
  93.2 0.6 copy-done.2
  93.9 2.9 %fusion.29 = bf16[192,192]{1,0:T(8,128)(2,1)S(1)} fusion(bf16[1,192,8192]{2,1,0:T(8,128)(2,1)} %param.15, bf16[2,192,8192]{2,1,0:T(8,128)(2,1)S(1)} %bitcast.127, s32[]{:T(128)S(6)} %select_n.111, f32[192,192]{1,0:T(8,128)S(1)} %fusion.2), kind=kOutput, calls=%fused_computation.29 | convolution fusion | flops 604200960 | bytes 6561796 | tf_op jit(solution)/shard_map/dot_general | solution.py:23
  96.8 0.1 fusion.50
  96.9 2.6 %convolution_convert_fusion = bf16[192,8192]{1,0:T(8,128)(2,1)} fusion(bf16[192,192]{1,0:T(8,128)(2,1)S(1)} %bitcast.109, bf16[1,192,8192]{2,1,0:T(8,128)(2,1)S(1)} %copy-done), kind=kOutput, calls=%fused_computation.2 | convolution fusion | flops 605552640 | bytes 6365184 | tf_op jit(solution)/shard_map/dot_general | solution.py:109
  99.5 0.2 collective-permute-start.4
  99.7 4.0 %fusion.10 = f32[192,192]{1,0:T(8,128)S(1)} fusion(bf16[1,192,8192]{2,1,0:T(8,128)(2,1)} %param.14, bf16[2,192,8192]{2,1,0:T(8,128)(2,1)} %bitcast.125, s32[]{:T(128)S(6)} %select_n.109), kind=kOutput, calls=%fused_computation.15 | convolution fusion | flops 603979776 | bytes 6438916 | tf_op jit(solution)/shard_map/dot_general | solution.py:23
  103.7 2.9 %fusion.34 = bf16[192,192]{1,0:T(8,128)(2,1)S(1)} fusion(bf16[1,192,8192]{2,1,0:T(8,128)(2,1)S(1)} %copy-done.3, bf16[2,192,8192]{2,1,0:T(8,128)(2,1)} %bitcast.126, s32[]{:T(128)S(6)} %select_n.109, f32[192,192]{1,0:T(8,128)S(1)} %fusion.10), kind=kOutput, calls=%fused_computation.30 | convolution fusion | flops 604200960 | bytes 6512644 | tf_op jit(solution)/shard_map/dot_general | solution.py:23
  106.6 0.1 fusion.51
  106.7 1.0 convolution_convert_fusion.1
  107.7 4.6 %add_convert_fusion = bf16[192,8192]{1,0:T(8,128)(2,1)} fusion(bf16[192,8192]{1,0:T(8,128)(2,1)} %collective-permute-done.4, bf16[192,8192]{1,0:T(8,128)(2,1)S(1)} %convolution_convert_fusion.1), kind=kLoop, calls=%fused_computation.4 | loop fusion | flops 6291456 | bytes 9437184 | tf_op jit(solution)/shard_map/convert_element_type | solution.py:116
  112.3 0.0 reduce-scatter.2.cloned.1.call-update
  112.3 0.3 collective-permute-start.3
  112.7 49.2 %reduce-scatter.2.cloned.1.call-done = bf16[24,8192]{1,0:T(8,128)(2,1)} async-done(((bf16[192,8192]{1,0:T(8,128)(2,1)}), bf16[24,8192]{1,0:T(8,128)(2,1)}) %reduce-scatter.2.cloned.1.call-update) | async-done | bytes 393232 | tf_op jit(solution)/shard_map/reduce_scatter | solution.py:117
  161.8 1.1 multiply_convert_fusion
  163.0 0.8 copy.35
  163.7 8.4 %all-to-all-start.1 = ((bf16[16,24,512]{2,1,0:T(8,128)(2,1)}), bf16[16,24,512]{2,1,0:T(8,128)(2,1)S(1)}, u32[]{:S(2)}, u32[]{:S(2)}) async-start(bf16[16,24,512]{2,1,0:T(8,128)(2,1)} %bitcast.107), calls=%async_computation.2 | async-start | bytes 786432 | tf_op jit(solution)/shard_map/all_to_all | solution.py:120
  172.1 1.6 scatter_custom_fusion
  173.7 11.9 %all-to-all-done.1 = bf16[16,24,512]{2,1,0:T(8,128)(2,1)S(1)} async-done(((bf16[16,24,512]{2,1,0:T(8,128)(2,1)}), bf16[16,24,512]{2,1,0:T(8,128)(2,1)S(1)}, u32[]{:S(2)}, u32[]{:S(2)}) %all-to-all-start.1) | async-done | bytes 393248 | tf_op jit(solution)/shard_map/all_to_all | solution.py:120
  185.6 0.8 fusion.18
  186.4 2.6 %add_convert_fusion.1 = bf16[1024,512]{1,0:T(8,128)(2,1)} fusion(f32[1024,512]{1,0:T(8,128)S(1)} %fusion.18, bf16[1024,512]{1,0:T(8,128)(2,1)} %collective-permute-done.3), kind=kLoop, calls=%fused_computation.23 | loop fusion | flops 1572864 | bytes 4194304 | tf_op jit(solution)/shard_map/convert_element_type | solution.py:130
  (24 shorter events, 0.2 us)
Async XLA Ops:
  6.5 90.3 %copy-start = (bf16[1,192,8192]{2,1,0:T(8,128)(2,1)S(1)}, bf16[1,192,8192]{2,1,0:T(8,128)(2,1)}, u32[]{:S(2)}) copy-start(bf16[1,192,8192]{2,1,0:T(8,128)(2,1)} %param.16) | copy-start | bytes 9437188
  6.5 82.7 %all-gather.2.cloned.1.call-start = ((), (), s32[]{:S(2)}) async-start(), calls=%async_computation.3 | async-start | bytes 6684672 | tf_op jit(solution)/shard_map/all_gather | solution.py:94
  6.5 5.0 %collective-permute-start = (s32[256,1]{0,1:T(1,128)}, s32[256,1]{0,1:T(1,128)S(1)}, u32[]{:S(2)}, u32[]{:S(2)}) collective-permute-start(s32[256,1]{0,1:T(1,128)} %param.11), channel_id=1, source_target_pairs={{16,0},{32,16},{48,32},{64,48},{80,64},{96,80},{112,96},{128,112},... | collective-permute-start | bytes 3080 | tf_op jit(solution)/shard_map/ppermute | solution.py:19
  8.6 6.3 %collective-permute-start.1 = (s32[1,256]{1,0:T(1,128)}, s32[1,256]{1,0:T(1,128)S(1)}, u32[]{:S(2)}, u32[]{:S(2)}) collective-permute-start(s32[1,256]{1,0:T(1,128)} %param.10), channel_id=1, source_target_pairs={{16,0},{32,16},{48,32},{64,48},{80,64},{96,80},{112,96},{128,112},... | collective-permute-start | bytes 3080 | tf_op jit(solution)/shard_map/ppermute | solution.py:19
  49.6 112.2 %reduce-scatter.2.cloned.1.call-start = ((), (), s32[]{:S(2)}) async-start(), calls=%async_computation.4 | async-start | bytes 3538944 | tf_op jit(solution)/shard_map/reduce_scatter | solution.py:117
  49.7 5.2 %collective-permute-start.2 = (f32[24]{0:T(128)S(1)}, f32[24]{0:T(128)S(1)}, u32[]{:S(2)}, u32[]{:S(2)}) collective-permute-start(f32[24]{0:T(128)S(1)} %get-tuple-element.21), channel_id=1, source_target_pairs={{240,0},{0,16},{16,32},{32,48},{48,64},{64,80},{80,96},{96,112},{1... | collective-permute-start | bytes 296 | tf_op jit(solution)/shard_map/ppermute | solution.py:19
  89.2 4.6 %copy-start.2 = (bf16[384,8192]{1,0:T(8,128)(2,1)S(1)}, bf16[384,8192]{1,0:T(8,128)(2,1)}, u32[]{:S(2)}) copy-start(bf16[384,8192]{1,0:T(8,128)(2,1)} %all-gather.2.cloned.1.call-done) | copy-start | bytes 18874372
  99.5 8.2 %collective-permute-start.4 = (bf16[192,8192]{1,0:T(8,128)(2,1)}, bf16[192,8192]{1,0:T(8,128)(2,1)}, u32[]{:S(2)}, u32[]{:S(2)}) collective-permute-start(bf16[192,8192]{1,0:T(8,128)(2,1)} %convolution_convert_fusion), channel_id=1, source_target_pairs={{0,16},{16,0},{1,17},{17,1},{2,18},{18,2},{3,19},{19,3},{4,20},{20... | collective-permute-start | bytes 9437192 | tf_op jit(solution)/shard_map/ppermute | solution.py:113
  99.7 4.0 %copy-start.3 = (bf16[1,192,8192]{2,1,0:T(8,128)(2,1)S(1)}, bf16[1,192,8192]{2,1,0:T(8,128)(2,1)}, u32[]{:S(2)}) copy-start(bf16[1,192,8192]{2,1,0:T(8,128)(2,1)} %param.15) | copy-start | bytes 9437188
  112.3 59.8 %copy-start.1 = (s32[1,256]{1,0:T(1,128)S(1)}, s32[1,256]{1,0:T(1,128)}, u32[]{:S(2)}) copy-start(s32[1,256]{1,0:T(1,128)} %param.10) | copy-start | bytes 3076
  112.3 74.0 %collective-permute-start.3 = (bf16[1024,512]{1,0:T(8,128)(2,1)}, bf16[1024,512]{1,0:T(8,128)(2,1)}, u32[]{:S(2)}, u32[]{:S(2)}) collective-permute-start(bf16[1024,512]{1,0:T(8,128)(2,1)} %param.9), channel_id=1, source_target_pairs={{240,0},{0,16},{16,32},{32,48},{48,64},{64,80},{80,96},{96,112},{1... | collective-permute-start | bytes 3145736 | tf_op jit(solution)/shard_map/ppermute | solution.py:19
  163.7 21.9 %all-to-all-start.1 = ((bf16[16,24,512]{2,1,0:T(8,128)(2,1)}), bf16[16,24,512]{2,1,0:T(8,128)(2,1)S(1)}, u32[]{:S(2)}, u32[]{:S(2)}) async-start(bf16[16,24,512]{2,1,0:T(8,128)(2,1)} %bitcast.107), calls=%async_computation.2 | async-start | bytes 786432 | tf_op jit(solution)/shard_map/all_to_all | solution.py:120
Sparse Core Ops, SparseCore 0:
  49.7 39.4 all-gather.1
  112.5 49.3 reduce-scatter.1

commit v15 on v12

--- a/solution.py
+++ b/solution.py
@@ -92,10 +92,15 @@
     score_home = passed_along(score, SECTION, 1)
 
     block = lax.all_gather(normed, SECTION, axis=0, tiled=True)
-    block, score_home, leaving = lax.optimization_barrier((block, score_home, activations))
+    stacked = jnp.concatenate([gate_w[0], up_w[0]], axis=0)
+    block, score_home, leaving, stacked = lax.optimization_barrier(
+        (block, score_home, activations, stacked)
+    )
     arrived = passed_along(leaving, SECTION, 1)
-    gate = feature_product(block, gate_w[0])
-    upper = feature_product(block, up_w[0])
+    both_products = feature_product(block, stacked)
+    hidden_units = gate_w.shape[1]
+    gate = both_products[:, :hidden_units]
+    upper = both_products[:, hidden_units:]
     hidden = (jax.nn.silu(gate) * upper).astype(jnp.bfloat16)
     hidden_width = hidden.shape[1]
     order = []

time: 196 us -> 196 us (level)
  other arithmetic: 14.7 us -> 21 us
  waiting for transfers between devices: 105 us -> 99.2 us
    concatenate x0 -> x1, other arithmetic: none -> 6.21 us  [body(): stacked = jnp.concatenate([gate_w[0], up_w[0]], axis=0)]
    all_gather x1, waiting for transfers between devices: 34.4 us -> 28.3 us  [body(): block = lax.all_gather(normed, SECTION, axis=0, tiled=True)]
    dot_general x2 -> x1, matrix products: 8.29 us -> 8.2 us  [feature_product(): lax.dot_general(block, weight, (((1,), (1,)), ((), ())), preferred_elemen...]
  transfers between devices with their start and end apart: 8 -> 8, of which waited for: 5 -> 5; matrix products, arithmetic and copies ran while one was open for 6% -> 9% of each run, Pallas kernels for 0% -> 0%
where the time goes in v15:
time: 196 us
  waiting for transfers between devices  99.2 us (51%)
  blocking collectives  29.1 us (15%)
  other arithmetic  21 us (11%)
  matrix products  13.9 us (7%)
  between operations  13.6 us (7%)
  starting transfers between devices  12.4 us (6%)
  local copies, waits for them, and re-layouts  6.47 us (3%)
    reduce_scatter x1, waiting for transfers between devices, body(): summed = lax.psum_scatter(pair, 'chip', scatter_dimension=0, tiled=True)  49.3 us
    all_to_all x1, blocking collectives, body(): lax.all_to_all(buffer, 'expert', split_axis=0, concat_axis=2, tiled=True)[0]  29.1 us
    all_gather x1, waiting for transfers between devices, body(): block = lax.all_gather(normed, SECTION, axis=0, tiled=True)  28.3 us
    all_to_all x1, waiting for transfers between devices, body(): lax.all_to_all(outgoing, 'expert', split_axis=0, concat_axis=0, tiled=True)  11.8 us
    all_to_all x1, starting transfers between devices, body(): lax.all_to_all(outgoing, 'expert', split_axis=0, concat_axis=0, tiled=True)  8.81 us
    dot_general x1, matrix products, feature_product(): lax.dot_general(block, weight, (((1,), (1,)), ((), ())), preferred_elemen...  8.2 us
    concatenate x1, other arithmetic, body(): stacked = jnp.concatenate([gate_w[0], up_w[0]], axis=0)  6.21 us
    ppermute x4, waiting for transfers between devices, passed_along(): return lax.ppermute(block, axis, route)  5.08 us
  transfers between devices with their start and end apart: 8, of which 5 were waited for; matrix products, arithmetic and copies ran while one was open for 9% of the time, Pallas kernels for 0%

profile of v15, /device:TPU:8, one launch (start us, length us, event | category | flops | bytes accessed | tf_op | source)
XLA Modules:
  0.0 195.6 jit_solution(17597508050167331478)
XLA Ops:
  6.5 2.1 %collective-permute-start = (s32[256,1]{0,1:T(1,128)}, s32[256,1]{0,1:T(1,128)S(1)}, u32[]{:S(2)}, u32[]{:S(2)}) collective-permute-start(s32[256,1]{0,1:T(1,128)} %param.12), channel_id=1, source_target_pairs={{16,0},{32,16},{48,32},{64,48},{80,64},{96,80},{112,96},{128,112},... | collective-permute-start | bytes 3080 | tf_op jit(solution)/shard_map/ppermute | solution.py:19
  8.6 0.7 collective-permute-start.1
  9.3 0.7 fusion.27
  10.0 0.7 fusion.22
  10.7 0.8 iota_compare_fusion.2
  11.5 0.0 collective-permute-done
  11.5 0.7 pad_add_fusion
  12.2 1.2 reduce-window.6
  13.4 0.1 slice.66
  13.5 0.1 copy.22
  13.6 0.1 fusion.20
  13.7 0.7 multiply_add_fusion
  14.4 0.5 fusion.49
  15.0 0.1 broadcast_compare_fusion
  15.1 2.6 %gather_fusion = bf16[256,512]{1,0:T(8,128)(2,1)S(1)} fusion(bf16[1024,512]{1,0:T(8,128)(2,1)} %param.10, s32[1024]{0:T(1024)S(1)} %pad_clamp_fusion.1), kind=kCustom, calls=%fused_computation | custom fusion | bytes 525312 | tf_op jit(solution)/shard_map/gather | solution.py:39
  17.7 1.3 convolution_convert_fusion.2
  19.0 29.1 %all_to_all.20 = bf16[16,32,512]{2,1,0:T(8,128)(2,1)S(1)} all-to-all(bf16[16,32,512]{2,1,0:T(8,128)(2,1)S(1)} %bitcast.81), channel_id=1, replica_groups=mesh['chip'=8,'core'=2,'expert'=16] {'expert'}, dimensions={0} | all-to-all | bytes 1048576 | tf_op jit(solution)/shard_map/all_to_all | solution.py:79
  48.1 0.1 fusion.50
  48.2 0.1 slice_add_fusion
  48.2 0.1 fusion.48
  48.3 0.1 copy.32
  48.4 0.3 multiply_reduce_fusion
  48.7 0.9 multiply_convert_fusion.1
  49.6 0.0 all-gather.2.cloned.1.call-update
  49.6 0.0 reduce-scatter.2.cloned.1.call-start
  49.7 6.2 %pad_maximum_fusion = bf16[384,8192]{1,0:T(8,128)(2,1)} fusion(bf16[192,8192]{1,0:T(8,128)(2,1)} %bitcast.73, bf16[192,8192]{1,0:T(8,128)(2,1)} %bitcast.74), kind=kLoop, calls=%fused_computation.5 | loop fusion | flops 12582912 | bytes 12582912 | tf_op jit(solution)/shard_map/concatenate | solution.py:95
  55.9 5.1 %collective-permute-done.2 = f32[24]{0:T(128)S(1)} collective-permute-done((f32[24]{0:T(128)S(1)}, f32[24]{0:T(128)S(1)}, u32[]{:S(2)}, u32[]{:S(2)}) %collective-permute-start.2) | collective-permute-done | bytes 128 | tf_op jit(solution)/shard_map/ppermute | solution.py:19
  61.0 28.3 %all-gather.2.cloned.1.call-done = bf16[384,8192]{1,0:T(8,128)(2,1)} async-done(((bf16[24,8192]{1,0:T(8,128)(2,1)}), bf16[384,8192]{1,0:T(8,128)(2,1)}) %all-gather.2.cloned.1.call-update) | async-done | bytes 6291472 | tf_op jit(solution)/shard_map/all_gather | solution.py:94
  89.2 8.2 %fusion.51 = f32[384,384]{0,1:T(8,128)S(1)} fusion(bf16[384,8192]{1,0:T(8,128)(2,1)} %all-gather.2.cloned.1.call-done, bf16[384,8192]{1,0:T(8,128)(2,1)} %pad_maximum_fusion), kind=kOutput, calls=%fused_computation.100 | convolution fusion | flops 2415919104 | bytes 13172736 | tf_op jit(solution)/shard_map/dot_general | solution.py:23
  97.4 0.1 fusion.7
  97.5 0.1 copy.26
  97.7 0.6 gather_fusion.1
  98.3 2.6 %convolution_convert_fusion = bf16[192,8192]{1,0:T(8,128)(2,1)} fusion(bf16[1,192,8192]{2,1,0:T(8,128)(2,1)S(1)} %copy-done, bf16[2,192,192]{2,1,0:T(8,128)(2,1)S(1)} %bitcast.78, s32[]{:T(128)S(6)} %select_n.116), kind=kOutput, calls=%fused_computation.3 | convolution fusion | flops 605552640 | bytes 6389764 | tf_op jit(solution)/shard_map/dot_general | solution.py:117
  100.9 0.3 collective-permute-start.4
  101.2 1.0 convolution_convert_fusion.1
  102.1 4.8 %collective-permute-done.4 = bf16[192,8192]{1,0:T(8,128)(2,1)} collective-permute-done((bf16[192,8192]{1,0:T(8,128)(2,1)}, bf16[192,8192]{1,0:T(8,128)(2,1)}, u32[]{:S(2)}, u32[]{:S(2)}) %collective-permute-start.4) | collective-permute-done | bytes 3145760 | tf_op jit(solution)/shard_map/ppermute | solution.py:121
  106.9 4.6 %add_convert_fusion = bf16[192,8192]{1,0:T(8,128)(2,1)} fusion(bf16[192,8192]{1,0:T(8,128)(2,1)} %collective-permute-done.4, bf16[192,8192]{1,0:T(8,128)(2,1)S(1)} %convolution_convert_fusion.1), kind=kLoop, calls=%fused_computation.6 | loop fusion | flops 6291456 | bytes 9437184 | tf_op jit(solution)/shard_map/convert_element_type | solution.py:123
  111.5 0.0 reduce-scatter.2.cloned.1.call-update
  111.5 0.5 collective-permute-start.3
  112.1 49.3 %reduce-scatter.2.cloned.1.call-done = bf16[24,8192]{1,0:T(8,128)(2,1)} async-done(((bf16[192,8192]{1,0:T(8,128)(2,1)}), bf16[24,8192]{1,0:T(8,128)(2,1)}) %reduce-scatter.2.cloned.1.call-update) | async-done | bytes 393232 | tf_op jit(solution)/shard_map/reduce_scatter | solution.py:124
  161.3 1.1 multiply_convert_fusion
  162.5 0.8 copy.38
  163.2 8.8 %all-to-all-start.1 = ((bf16[16,24,512]{2,1,0:T(8,128)(2,1)}), bf16[16,24,512]{2,1,0:T(8,128)(2,1)S(1)}, u32[]{:S(2)}, u32[]{:S(2)}) async-start(bf16[16,24,512]{2,1,0:T(8,128)(2,1)} %bitcast.76), calls=%async_computation.2 | async-start | bytes 786432 | tf_op jit(solution)/shard_map/all_to_all | solution.py:127
  172.1 1.6 scatter_custom_fusion
  173.6 11.8 %all-to-all-done.1 = bf16[16,24,512]{2,1,0:T(8,128)(2,1)S(1)} async-done(((bf16[16,24,512]{2,1,0:T(8,128)(2,1)}), bf16[16,24,512]{2,1,0:T(8,128)(2,1)S(1)}, u32[]{:S(2)}, u32[]{:S(2)}) %all-to-all-start.1) | async-done | bytes 393248 | tf_op jit(solution)/shard_map/all_to_all | solution.py:127
  185.5 0.8 fusion.2
  186.2 0.0 collective-permute-done.3
  186.2 2.6 %add_convert_fusion.1 = bf16[1024,512]{1,0:T(8,128)(2,1)} fusion(f32[1024,512]{1,0:T(8,128)S(1)} %fusion.2, bf16[1024,512]{1,0:T(8,128)(2,1)} %collective-permute-done.3), kind=kLoop, calls=%fused_computation.9 | loop fusion | flops 1572864 | bytes 4194304 | tf_op jit(solution)/shard_map/convert_element_type | solution.py:137
  (22 shorter events, 0.2 us)
Async XLA Ops:
  6.5 91.7 %copy-start = (bf16[1,192,8192]{2,1,0:T(8,128)(2,1)S(1)}, bf16[1,192,8192]{2,1,0:T(8,128)(2,1)}, u32[]{:S(2)}) copy-start(bf16[1,192,8192]{2,1,0:T(8,128)(2,1)} %param.17) | copy-start | bytes 9437188
  6.5 82.7 %all-gather.2.cloned.1.call-start = ((), (), s32[]{:S(2)}) async-start(), calls=%async_computation.3 | async-start | bytes 6684672 | tf_op jit(solution)/shard_map/all_gather | solution.py:94
  6.5 5.0 %collective-permute-start = (s32[256,1]{0,1:T(1,128)}, s32[256,1]{0,1:T(1,128)S(1)}, u32[]{:S(2)}, u32[]{:S(2)}) collective-permute-start(s32[256,1]{0,1:T(1,128)} %param.12), channel_id=1, source_target_pairs={{16,0},{32,16},{48,32},{64,48},{80,64},{96,80},{112,96},{128,112},... | collective-permute-start | bytes 3080 | tf_op jit(solution)/shard_map/ppermute | solution.py:19
  8.6 6.3 %collective-permute-start.1 = (s32[1,256]{1,0:T(1,128)}, s32[1,256]{1,0:T(1,128)S(1)}, u32[]{:S(2)}, u32[]{:S(2)}) collective-permute-start(s32[1,256]{1,0:T(1,128)} %param.11), channel_id=1, source_target_pairs={{16,0},{32,16},{48,32},{64,48},{80,64},{96,80},{112,96},{128,112},... | collective-permute-start | bytes 3080 | tf_op jit(solution)/shard_map/ppermute | solution.py:19
  48.0 1.6 copy-start.2
  49.6 111.7 %reduce-scatter.2.cloned.1.call-start = ((), (), s32[]{:S(2)}) async-start(), calls=%async_computation.4 | async-start | bytes 3538944 | tf_op jit(solution)/shard_map/reduce_scatter | solution.py:124
  55.9 5.1 %collective-permute-start.2 = (f32[24]{0:T(128)S(1)}, f32[24]{0:T(128)S(1)}, u32[]{:S(2)}, u32[]{:S(2)}) collective-permute-start(f32[24]{0:T(128)S(1)} %get-tuple-element.23), channel_id=1, source_target_pairs={{240,0},{0,16},{16,32},{32,48},{48,64},{64,80},{80,96},{96,112},{1... | collective-permute-start | bytes 296 | tf_op jit(solution)/shard_map/ppermute | solution.py:19
  100.9 6.0 %collective-permute-start.4 = (bf16[192,8192]{1,0:T(8,128)(2,1)}, bf16[192,8192]{1,0:T(8,128)(2,1)}, u32[]{:S(2)}, u32[]{:S(2)}) collective-permute-start(bf16[192,8192]{1,0:T(8,128)(2,1)} %convolution_convert_fusion), channel_id=1, source_target_pairs={{0,16},{16,0},{1,17},{17,1},{2,18},{18,2},{3,19},{19,3},{4,20},{20... | collective-permute-start | bytes 9437192 | tf_op jit(solution)/shard_map/ppermute | solution.py:121
  111.5 60.5 %copy-start.1 = (s32[1,256]{1,0:T(1,128)S(1)}, s32[1,256]{1,0:T(1,128)}, u32[]{:S(2)}) copy-start(s32[1,256]{1,0:T(1,128)} %param.11) | copy-start | bytes 3076
  111.5 74.7 %collective-permute-start.3 = (bf16[1024,512]{1,0:T(8,128)(2,1)}, bf16[1024,512]{1,0:T(8,128)(2,1)}, u32[]{:S(2)}, u32[]{:S(2)}) collective-permute-start(bf16[1024,512]{1,0:T(8,128)(2,1)} %param.10), channel_id=1, source_target_pairs={{240,0},{0,16},{16,32},{32,48},{48,64},{64,80},{80,96},{96,112},{1... | collective-permute-start | bytes 3145736 | tf_op jit(solution)/shard_map/ppermute | solution.py:19
  163.2 22.2 %all-to-all-start.1 = ((bf16[16,24,512]{2,1,0:T(8,128)(2,1)}), bf16[16,24,512]{2,1,0:T(8,128)(2,1)S(1)}, u32[]{:S(2)}, u32[]{:S(2)}) async-start(bf16[16,24,512]{2,1,0:T(8,128)(2,1)} %bitcast.76), calls=%async_computation.2 | async-start | bytes 786432 | tf_op jit(solution)/shard_map/all_to_all | solution.py:127
Sparse Core Ops, SparseCore 0:
  49.7 39.4 all-gather.1
  111.7 49.6 reduce-scatter.1

commit v16 on v12

--- a/solution.py
+++ b/solution.py
@@ -117,8 +117,8 @@
     keep = down_part(lax.dynamic_index_in_dim(hidden, core, axis=0, keepdims=False))
     pair = (keep.astype(jnp.float32) + taken.astype(jnp.float32)).astype(jnp.bfloat16)
     summed = lax.psum_scatter(pair, "chip", scatter_dimension=0, tiled=True)
-    update_rows = (score_home[:, None] * summed.astype(jnp.float32)).astype(jnp.bfloat16)
-    outgoing = update_rows.reshape(capacity, n_exp_dev, local_width).transpose(1, 0, 2)
+    by_block = summed.reshape(capacity, n_exp_dev, local_width).transpose(1, 0, 2)
+    outgoing = (score_home[None, :, None] * by_block.astype(jnp.float32)).astype(jnp.bfloat16)
     back = lax.all_to_all(outgoing, "expert", split_axis=0, concat_axis=0, tiled=True)
     flat_back = back.reshape(expert_count * capacity, local_width)
 

time: 196 us -> 196 us (level)
  no operation moved by 1% of the time
where the time goes in v16:
time: 196 us
  waiting for transfers between devices  105 us (54%)
  blocking collectives  29.1 us (15%)
  other arithmetic  15.5 us (8%)
  matrix products  13.9 us (7%)
  between operations  13.6 us (7%)
  starting transfers between devices  12.1 us (6%)
  local copies, waits for them, and re-layouts  6.06 us (3%)
    reduce_scatter x1, waiting for transfers between devices, body(): summed = lax.psum_scatter(pair, 'chip', scatter_dimension=0, tiled=True)  49.3 us
    all_gather x1, waiting for transfers between devices, body(): block = lax.all_gather(normed, SECTION, axis=0, tiled=True)  34.4 us
    all_to_all x1, blocking collectives, body(): lax.all_to_all(buffer, 'expert', split_axis=0, concat_axis=2, tiled=True)[0]  29.1 us
    all_to_all x1, waiting for transfers between devices, body(): lax.all_to_all(outgoing, 'expert', split_axis=0, concat_axis=0, tiled=True)  11.9 us
    all_to_all x1, starting transfers between devices, body(): lax.all_to_all(outgoing, 'expert', split_axis=0, concat_axis=0, tiled=True)  8.69 us
    dot_general x2, matrix products, feature_product(): lax.dot_general(block, weight, (((1,), (1,)), ((), ())), preferred_elemen...  8.29 us
    ppermute x4, waiting for transfers between devices, passed_along(): return lax.ppermute(block, axis, route)  5.07 us
    ppermute x1, waiting for transfers between devices, body(): taken = lax.ppermute(give, 'core', [(0, 1), (1, 0)])  4.78 us
  transfers between devices with their start and end apart: 8, of which 5 were waited for; matrix products, arithmetic and copies ran while one was open for 6% of the time, Pallas kernels for 0%

profile of v16, /device:TPU:8, one launch (start us, length us, event | category | flops | bytes accessed | tf_op | source)
XLA Modules:
  0.0 195.8 jit_solution(15382221513255900075)
XLA Ops:
  6.5 2.1 %collective-permute-start = (s32[256,1]{0,1:T(1,128)}, s32[256,1]{0,1:T(1,128)S(1)}, u32[]{:S(2)}, u32[]{:S(2)}) collective-permute-start(s32[256,1]{0,1:T(1,128)} %param.12), channel_id=1, source_target_pairs={{16,0},{32,16},{48,32},{64,48},{80,64},{96,80},{112,96},{128,112},... | collective-permute-start | bytes 3080 | tf_op jit(solution)/shard_map/ppermute | solution.py:19
  8.6 0.7 collective-permute-start.1
  9.3 0.7 fusion.32
  10.0 0.7 fusion.27
  10.7 0.8 iota_compare_fusion.2
  11.5 0.0 collective-permute-done
  11.5 0.7 pad_add_fusion
  12.2 1.2 reduce-window.6
  13.4 0.1 slice.58
  13.5 0.1 copy.22
  13.6 0.1 fusion.25
  13.7 0.7 multiply_add_fusion
  14.4 0.6 fusion.54
  15.0 0.1 broadcast_compare_fusion
  15.1 2.6 %gather_fusion = bf16[256,512]{1,0:T(8,128)(2,1)S(1)} fusion(bf16[1024,512]{1,0:T(8,128)(2,1)} %param.10, s32[1024]{0:T(1024)S(1)} %pad_clamp_fusion.1), kind=kCustom, calls=%fused_computation | custom fusion | bytes 525312 | tf_op jit(solution)/shard_map/gather | solution.py:39
  17.7 1.3 convolution_convert_fusion.2
  19.0 29.1 %all_to_all.20 = bf16[16,32,512]{2,1,0:T(8,128)(2,1)S(1)} all-to-all(bf16[16,32,512]{2,1,0:T(8,128)(2,1)S(1)} %bitcast.86), channel_id=1, replica_groups=mesh['chip'=8,'core'=2,'expert'=16] {'expert'}, dimensions={0} | all-to-all | bytes 1048576 | tf_op jit(solution)/shard_map/all_to_all | solution.py:79
  48.1 0.1 fusion.55
  48.2 0.1 slice_add_fusion
  48.3 0.1 fusion.53
  48.3 0.1 copy.32
  48.4 0.3 multiply_reduce_fusion
  48.7 0.9 multiply_convert_fusion
  49.6 0.0 all-gather.2.cloned.1.call-update
  49.6 0.0 reduce-scatter.2.cloned.1.call-start
  49.7 0.1 collective-permute-start.2
  49.8 5.1 %collective-permute-done.2 = f32[24]{0:T(128)S(1)} collective-permute-done((f32[24]{0:T(128)S(1)}, f32[24]{0:T(128)S(1)}, u32[]{:S(2)}, u32[]{:S(2)}) %collective-permute-start.2) | collective-permute-done | bytes 128 | tf_op jit(solution)/shard_map/ppermute | solution.py:19
  54.9 34.4 %all-gather.2.cloned.1.call-done = bf16[384,8192]{1,0:T(8,128)(2,1)} async-done(((bf16[24,8192]{1,0:T(8,128)(2,1)}), bf16[384,8192]{1,0:T(8,128)(2,1)}) %all-gather.2.cloned.1.call-update) | async-done | bytes 6291472 | tf_op jit(solution)/shard_map/all_gather | solution.py:94
  89.3 6.1 %fusion.4 = f32[384,192]{0,1:T(8,128)S(1)} fusion(bf16[384,8192]{1,0:T(8,128)(2,1)} %all-gather.2.cloned.1.call-done, bf16[1,192,8192]{2,1,0:T(8,128)(2,1)} %param.15), kind=kOutput, calls=%fused_computation.10 | convolution fusion | flops 1207959552 | bytes 9732096 | tf_op jit(solution)/shard_map/dot_general | solution.py:23
  95.3 0.3 copy-done.4
  95.7 2.2 %multiply_convert_fusion.1 = bf16[384,192]{0,1:T(8,128)(2,1)S(1)} fusion(f32[384,192]{0,1:T(8,128)S(1)} %fusion.4, bf16[384,8192]{1,0:T(8,128)(2,1)S(1)} %copy-done.3, bf16[1,192,8192]{2,1,0:T(8,128)(2,1)S(1)} %copy-done.4), kind=kOutput, calls=%fused_computation.27 | convolution fusion | flops 1208401920 | bytes 9879552 | tf_op jit(solution)/shard_map/dot_general | solution.py:23
  97.9 0.1 copy.26
  98.1 0.6 gather_fusion.1
  98.6 2.6 %convolution_convert_fusion = bf16[192,8192]{1,0:T(8,128)(2,1)} fusion(bf16[1,192,8192]{2,1,0:T(8,128)(2,1)S(1)} %copy-done, bf16[2,192,192]{2,1,0:T(8,128)(2,1)S(1)} %bitcast.83, s32[]{:T(128)S(6)} %select_n.116), kind=kOutput, calls=%fused_computation.3 | convolution fusion | flops 605552640 | bytes 6389764 | tf_op jit(solution)/shard_map/dot_general | solution.py:112
  101.3 0.2 collective-permute-start.4
  101.5 1.0 convolution_convert_fusion.1
  102.5 4.8 %collective-permute-done.4 = bf16[192,8192]{1,0:T(8,128)(2,1)} collective-permute-done((bf16[192,8192]{1,0:T(8,128)(2,1)}, bf16[192,8192]{1,0:T(8,128)(2,1)}, u32[]{:S(2)}, u32[]{:S(2)}) %collective-permute-start.4) | collective-permute-done | bytes 3145760 | tf_op jit(solution)/shard_map/ppermute | solution.py:116
  107.3 4.6 %add_convert_fusion = bf16[192,8192]{1,0:T(8,128)(2,1)} fusion(bf16[192,8192]{1,0:T(8,128)(2,1)} %collective-permute-done.4, bf16[192,8192]{1,0:T(8,128)(2,1)S(1)} %convolution_convert_fusion.1), kind=kLoop, calls=%fused_computation.5 | loop fusion | flops 6291456 | bytes 9437184 | tf_op jit(solution)/shard_map/convert_element_type | solution.py:118
  111.9 0.0 reduce-scatter.2.cloned.1.call-update
  111.9 0.3 collective-permute-start.3
  112.3 49.3 %reduce-scatter.2.cloned.1.call-done = bf16[24,8192]{1,0:T(8,128)(2,1)} async-done(((bf16[192,8192]{1,0:T(8,128)(2,1)}), bf16[24,8192]{1,0:T(8,128)(2,1)}) %reduce-scatter.2.cloned.1.call-update) | async-done | bytes 393232 | tf_op jit(solution)/shard_map/reduce_scatter | solution.py:119
  161.5 1.0 convert_element_type.116
  162.6 0.9 fusion.12
  163.5 8.7 %all-to-all-start.1 = ((bf16[16,24,512]{2,1,0:T(8,128)(2,1)}), bf16[16,24,512]{2,1,0:T(8,128)(2,1)S(1)}, u32[]{:S(2)}, u32[]{:S(2)}) async-start(bf16[16,24,512]{2,1,0:T(8,128)(2,1)} %fusion.12), calls=%async_computation.2 | async-start | bytes 786432 | tf_op jit(solution)/shard_map/all_to_all | solution.py:122
  172.2 1.6 scatter_custom_fusion
  173.7 11.9 %all-to-all-done.1 = bf16[16,24,512]{2,1,0:T(8,128)(2,1)S(1)} async-done(((bf16[16,24,512]{2,1,0:T(8,128)(2,1)}), bf16[16,24,512]{2,1,0:T(8,128)(2,1)S(1)}, u32[]{:S(2)}, u32[]{:S(2)}) %all-to-all-start.1) | async-done | bytes 393248 | tf_op jit(solution)/shard_map/all_to_all | solution.py:122
  185.7 0.8 fusion.6
  186.4 2.6 %add_convert_fusion.1 = bf16[1024,512]{1,0:T(8,128)(2,1)} fusion(f32[1024,512]{1,0:T(8,128)S(1)} %fusion.6, bf16[1024,512]{1,0:T(8,128)(2,1)} %collective-permute-done.3), kind=kLoop, calls=%fused_computation.12 | loop fusion | flops 1572864 | bytes 4194304 | tf_op jit(solution)/shard_map/convert_element_type | solution.py:132
  (25 shorter events, 0.2 us)
Async XLA Ops:
  6.5 92.1 %copy-start = (bf16[1,192,8192]{2,1,0:T(8,128)(2,1)S(1)}, bf16[1,192,8192]{2,1,0:T(8,128)(2,1)}, u32[]{:S(2)}) copy-start(bf16[1,192,8192]{2,1,0:T(8,128)(2,1)} %param.17) | copy-start | bytes 9437188
  6.5 82.7 %all-gather.2.cloned.1.call-start = ((), (), s32[]{:S(2)}) async-start(), calls=%async_computation.3 | async-start | bytes 6684672 | tf_op jit(solution)/shard_map/all_gather | solution.py:94
  6.5 5.0 %collective-permute-start = (s32[256,1]{0,1:T(1,128)}, s32[256,1]{0,1:T(1,128)S(1)}, u32[]{:S(2)}, u32[]{:S(2)}) collective-permute-start(s32[256,1]{0,1:T(1,128)} %param.12), channel_id=1, source_target_pairs={{16,0},{32,16},{48,32},{64,48},{80,64},{96,80},{112,96},{128,112},... | collective-permute-start | bytes 3080 | tf_op jit(solution)/shard_map/ppermute | solution.py:19
  8.6 6.4 %collective-permute-start.1 = (s32[1,256]{1,0:T(1,128)}, s32[1,256]{1,0:T(1,128)S(1)}, u32[]{:S(2)}, u32[]{:S(2)}) collective-permute-start(s32[1,256]{1,0:T(1,128)} %param.11), channel_id=1, source_target_pairs={{16,0},{32,16},{48,32},{64,48},{80,64},{96,80},{112,96},{128,112},... | collective-permute-start | bytes 3080 | tf_op jit(solution)/shard_map/ppermute | solution.py:19
  48.1 1.6 copy-start.2
  49.6 111.9 %reduce-scatter.2.cloned.1.call-start = ((), (), s32[]{:S(2)}) async-start(), calls=%async_computation.4 | async-start | bytes 3538944 | tf_op jit(solution)/shard_map/reduce_scatter | solution.py:119
  49.7 5.2 %collective-permute-start.2 = (f32[24]{0:T(128)S(1)}, f32[24]{0:T(128)S(1)}, u32[]{:S(2)}, u32[]{:S(2)}) collective-permute-start(f32[24]{0:T(128)S(1)} %get-tuple-element.21), channel_id=1, source_target_pairs={{240,0},{0,16},{16,32},{32,48},{48,64},{64,80},{80,96},{96,112},{1... | collective-permute-start | bytes 296 | tf_op jit(solution)/shard_map/ppermute | solution.py:19
  89.3 6.1 %copy-start.3 = (bf16[384,8192]{1,0:T(8,128)(2,1)S(1)}, bf16[384,8192]{1,0:T(8,128)(2,1)}, u32[]{:S(2)}) copy-start(bf16[384,8192]{1,0:T(8,128)(2,1)} %all-gather.2.cloned.1.call-done) | copy-start | bytes 18874372
  89.3 6.4 %copy-start.4 = (bf16[1,192,8192]{2,1,0:T(8,128)(2,1)S(1)}, bf16[1,192,8192]{2,1,0:T(8,128)(2,1)}, u32[]{:S(2)}) copy-start(bf16[1,192,8192]{2,1,0:T(8,128)(2,1)} %param.16) | copy-start | bytes 9437188
  101.3 6.0 %collective-permute-start.4 = (bf16[192,8192]{1,0:T(8,128)(2,1)}, bf16[192,8192]{1,0:T(8,128)(2,1)}, u32[]{:S(2)}, u32[]{:S(2)}) collective-permute-start(bf16[192,8192]{1,0:T(8,128)(2,1)} %convolution_convert_fusion), channel_id=1, source_target_pairs={{0,16},{16,0},{1,17},{17,1},{2,18},{18,2},{3,19},{19,3},{4,20},{20... | collective-permute-start | bytes 9437192 | tf_op jit(solution)/shard_map/ppermute | solution.py:116
  111.9 60.3 %copy-start.1 = (s32[1,256]{1,0:T(1,128)S(1)}, s32[1,256]{1,0:T(1,128)}, u32[]{:S(2)}) copy-start(s32[1,256]{1,0:T(1,128)} %param.11) | copy-start | bytes 3076
  111.9 74.5 %collective-permute-start.3 = (bf16[1024,512]{1,0:T(8,128)(2,1)}, bf16[1024,512]{1,0:T(8,128)(2,1)}, u32[]{:S(2)}, u32[]{:S(2)}) collective-permute-start(bf16[1024,512]{1,0:T(8,128)(2,1)} %param.10), channel_id=1, source_target_pairs={{240,0},{0,16},{16,32},{32,48},{48,64},{64,80},{80,96},{96,112},{1... | collective-permute-start | bytes 3145736 | tf_op jit(solution)/shard_map/ppermute | solution.py:19
  163.5 22.2 %all-to-all-start.1 = ((bf16[16,24,512]{2,1,0:T(8,128)(2,1)}), bf16[16,24,512]{2,1,0:T(8,128)(2,1)S(1)}, u32[]{:S(2)}, u32[]{:S(2)}) async-start(bf16[16,24,512]{2,1,0:T(8,128)(2,1)} %fusion.12), calls=%async_computation.2 | async-start | bytes 786432 | tf_op jit(solution)/shard_map/all_to_all | solution.py:122
Sparse Core Ops, SparseCore 0:
  49.8 39.4 all-gather.1
  112.1 49.4 reduce-scatter.1

commit v17 on v15

--- a/solution.py
+++ b/solution.py
@@ -34,8 +34,9 @@
     capacity = max(2, 3 * sel_count // (2 * expert_count))
     groups = n_section
 
-    sel_next = passed_along(selected, SECTION, -1)[0]
-    routes_next = passed_along(routes, SECTION, -1)[:, 0]
+    lists_next = passed_along(jnp.concatenate([selected, routes.T], axis=0), SECTION, -1)
+    sel_next = lists_next[0]
+    routes_next = lists_next[1]
     rows = activations[sel_next]
     both = jnp.stack([routes_next, routes[:, 0]], axis=1)
     onehot = (both[:, :, None] == jnp.arange(expert_count, dtype=jnp.int32)[None, None, :]).astype(

time: 196 us -> 197 us (level)
    ppermute x4 -> x3, waiting for transfers between devices: 5.08 us -> 5.36 us  [passed_along(): return lax.ppermute(block, axis, route)]
  transfers between devices with their start and end apart: 8 -> 7, of which waited for: 5 -> 5; matrix products, arithmetic and copies ran while one was open for 9% -> 7% of each run, Pallas kernels for 0% -> 0%
where the time goes in v17:
time: 197 us; the launch traced here: 195 us
  waiting for transfers between devices  101 us (51%)
  blocking collectives  27.6 us (14%)
  other arithmetic  21.9 us (11%)
  matrix products  13.8 us (7%)
  between operations  13.6 us (7%)
  starting transfers between devices  10.9 us (6%)
  local copies, waits for them, and re-layouts  6.51 us (3%)
    reduce_scatter x1, waiting for transfers between devices, body(): summed = lax.psum_scatter(pair, 'chip', scatter_dimension=0, tiled=True)  49.4 us
    all_gather x1, waiting for transfers between devices, body(): block = lax.all_gather(normed, SECTION, axis=0, tiled=True)  29.4 us
    all_to_all x1, blocking collectives, body(): lax.all_to_all(buffer, 'expert', split_axis=0, concat_axis=2, tiled=True)[0]  27.6 us
    all_to_all x1, waiting for transfers between devices, body(): lax.all_to_all(outgoing, 'expert', split_axis=0, concat_axis=0, tiled=True)  11.9 us
    all_to_all x1, starting transfers between devices, body(): lax.all_to_all(outgoing, 'expert', split_axis=0, concat_axis=0, tiled=True)  8.22 us
    dot_general x1, matrix products, feature_product(): lax.dot_general(block, weight, (((1,), (1,)), ((), ())), preferred_elemen...  8.2 us
    concatenate x1, other arithmetic, body(): stacked = jnp.concatenate([gate_w[0], up_w[0]], axis=0)  6.21 us
    ppermute x3, waiting for transfers between devices, passed_along(): return lax.ppermute(block, axis, route)  5.36 us
  transfers between devices with their start and end apart: 7, of which 5 were waited for; matrix products, arithmetic and copies ran while one was open for 7% of the time, Pallas kernels for 0%

profile of v17, /device:TPU:8, one launch (start us, length us, event | category | flops | bytes accessed | tf_op | source)
XLA Modules:
  0.0 195.3 jit_solution(17663004068960849676)
XLA Ops:
  6.5 0.9 pad_add_fusion
  7.4 2.1 %collective-permute-start = (s32[2,256]{1,0:T(2,128)S(1)}, s32[2,256]{1,0:T(2,128)S(1)}, u32[]{:S(2)}, u32[]{:S(2)}) collective-permute-start(s32[2,256]{1,0:T(2,128)S(1)} %pad_add_fusion), channel_id=1, source_target_pairs={{16,0},{32,16},{48,32},{64,48},{80,64},{96,80},{112,96},{128,112},... | collective-permute-start | bytes 6152 | tf_op jit(solution)/shard_map/ppermute | solution.py:19
  9.5 0.7 fusion.27
  10.2 0.7 fusion.22
  10.9 0.8 iota_compare_fusion.2
  11.7 0.0 collective-permute-done
  11.7 0.7 pad_add_fusion.1
  12.4 1.2 reduce-window.6
  13.6 0.1 slice.75
  13.6 0.1 copy.22
  13.8 0.1 fusion.20
  13.9 0.7 multiply_add_fusion
  14.6 0.6 fusion.49
  15.2 0.1 broadcast_compare_fusion
  15.3 2.6 %gather_fusion = bf16[256,512]{1,0:T(8,128)(2,1)S(1)} fusion(bf16[1024,512]{1,0:T(8,128)(2,1)} %param.10, s32[1024]{0:T(1024)S(1)} %pad_clamp_fusion.1), kind=kCustom, calls=%fused_computation | custom fusion | bytes 525312 | tf_op jit(solution)/shard_map/gather | solution.py:40
  17.9 1.3 convolution_convert_fusion.2
  19.2 27.6 %all_to_all.20 = bf16[16,32,512]{2,1,0:T(8,128)(2,1)S(1)} all-to-all(bf16[16,32,512]{2,1,0:T(8,128)(2,1)S(1)} %bitcast.86), channel_id=1, replica_groups=mesh['chip'=8,'core'=2,'expert'=16] {'expert'}, dimensions={0} | all-to-all | bytes 1048576 | tf_op jit(solution)/shard_map/all_to_all | solution.py:80
  46.8 0.1 fusion.50
  46.9 0.1 slice_add_fusion
  47.0 0.1 fusion.48
  47.1 0.1 copy.32
  47.1 0.3 multiply_reduce_fusion
  47.4 0.9 multiply_convert_fusion.1
  48.3 0.0 all-gather.2.cloned.1.call-update
  48.4 0.0 reduce-scatter.2.cloned.1.call-start
  48.4 6.2 %pad_maximum_fusion = bf16[384,8192]{1,0:T(8,128)(2,1)} fusion(bf16[192,8192]{1,0:T(8,128)(2,1)} %bitcast.78, bf16[192,8192]{1,0:T(8,128)(2,1)} %bitcast.79), kind=kLoop, calls=%fused_computation.5 | loop fusion | flops 12582912 | bytes 12582912 | tf_op jit(solution)/shard_map/concatenate | solution.py:96
  54.7 0.0 collective-permute-start.1
  54.7 5.4 %collective-permute-done.1 = f32[24]{0:T(128)S(1)} collective-permute-done((f32[24]{0:T(128)S(1)}, f32[24]{0:T(128)S(1)}, u32[]{:S(2)}, u32[]{:S(2)}) %collective-permute-start.1) | collective-permute-done | bytes 128 | tf_op jit(solution)/shard_map/ppermute | solution.py:19
  60.0 29.4 %all-gather.2.cloned.1.call-done = bf16[384,8192]{1,0:T(8,128)(2,1)} async-done(((bf16[24,8192]{1,0:T(8,128)(2,1)}), bf16[384,8192]{1,0:T(8,128)(2,1)}) %all-gather.2.cloned.1.call-update) | async-done | bytes 6291472 | tf_op jit(solution)/shard_map/all_gather | solution.py:95
  89.5 8.2 %fusion.51 = f32[384,384]{0,1:T(8,128)S(1)} fusion(bf16[384,8192]{1,0:T(8,128)(2,1)} %all-gather.2.cloned.1.call-done, bf16[384,8192]{1,0:T(8,128)(2,1)} %pad_maximum_fusion), kind=kOutput, calls=%fused_computation.103 | convolution fusion | flops 2415919104 | bytes 13172736 | tf_op jit(solution)/shard_map/dot_general | solution.py:23
  97.7 0.1 fusion.7
  97.8 0.1 copy.26
  97.9 0.6 gather_fusion.1
  98.5 2.6 %convolution_convert_fusion = bf16[192,8192]{1,0:T(8,128)(2,1)} fusion(bf16[1,192,8192]{2,1,0:T(8,128)(2,1)S(1)} %copy-done, bf16[2,192,192]{2,1,0:T(8,128)(2,1)S(1)} %bitcast.83, s32[]{:T(128)S(6)} %select_n.116), kind=kOutput, calls=%fused_computation.3 | convolution fusion | flops 605552640 | bytes 6389764 | tf_op jit(solution)/shard_map/dot_general | solution.py:118
  101.1 0.3 collective-permute-start.3
  101.4 1.0 convolution_convert_fusion.1
  102.4 4.8 %collective-permute-done.3 = bf16[192,8192]{1,0:T(8,128)(2,1)} collective-permute-done((bf16[192,8192]{1,0:T(8,128)(2,1)}, bf16[192,8192]{1,0:T(8,128)(2,1)}, u32[]{:S(2)}, u32[]{:S(2)}) %collective-permute-start.3) | collective-permute-done | bytes 3145760 | tf_op jit(solution)/shard_map/ppermute | solution.py:122
  107.1 4.6 %add_convert_fusion = bf16[192,8192]{1,0:T(8,128)(2,1)} fusion(bf16[192,8192]{1,0:T(8,128)(2,1)} %collective-permute-done.3, bf16[192,8192]{1,0:T(8,128)(2,1)S(1)} %convolution_convert_fusion.1), kind=kLoop, calls=%fused_computation.6 | loop fusion | flops 6291456 | bytes 9437184 | tf_op jit(solution)/shard_map/convert_element_type | solution.py:124
  111.7 0.0 reduce-scatter.2.cloned.1.call-update
  111.8 0.3 collective-permute-start.2
  112.1 49.4 %reduce-scatter.2.cloned.1.call-done = bf16[24,8192]{1,0:T(8,128)(2,1)} async-done(((bf16[192,8192]{1,0:T(8,128)(2,1)}), bf16[24,8192]{1,0:T(8,128)(2,1)}) %reduce-scatter.2.cloned.1.call-update) | async-done | bytes 393232 | tf_op jit(solution)/shard_map/reduce_scatter | solution.py:125
  161.5 1.1 multiply_convert_fusion
  162.6 0.8 copy.38
  163.4 8.2 %all-to-all-start.1 = ((bf16[16,24,512]{2,1,0:T(8,128)(2,1)}), bf16[16,24,512]{2,1,0:T(8,128)(2,1)S(1)}, u32[]{:S(2)}, u32[]{:S(2)}) async-start(bf16[16,24,512]{2,1,0:T(8,128)(2,1)} %bitcast.81), calls=%async_computation.2 | async-start | bytes 786432 | tf_op jit(solution)/shard_map/all_to_all | solution.py:128
  171.6 1.6 scatter_custom_fusion
  173.2 11.9 %all-to-all-done.1 = bf16[16,24,512]{2,1,0:T(8,128)(2,1)S(1)} async-done(((bf16[16,24,512]{2,1,0:T(8,128)(2,1)}), bf16[16,24,512]{2,1,0:T(8,128)(2,1)S(1)}, u32[]{:S(2)}, u32[]{:S(2)}) %all-to-all-start.1) | async-done | bytes 393248 | tf_op jit(solution)/shard_map/all_to_all | solution.py:128
  185.1 0.8 fusion.2
  185.9 2.6 %add_convert_fusion.1 = bf16[1024,512]{1,0:T(8,128)(2,1)} fusion(f32[1024,512]{1,0:T(8,128)S(1)} %fusion.2, bf16[1024,512]{1,0:T(8,128)(2,1)} %collective-permute-done.2), kind=kLoop, calls=%fused_computation.9 | loop fusion | flops 1572864 | bytes 4194304 | tf_op jit(solution)/shard_map/convert_element_type | solution.py:138
  (22 shorter events, 0.2 us)
Async XLA Ops:
  6.5 91.9 %copy-start = (bf16[1,192,8192]{2,1,0:T(8,128)(2,1)S(1)}, bf16[1,192,8192]{2,1,0:T(8,128)(2,1)}, u32[]{:S(2)}) copy-start(bf16[1,192,8192]{2,1,0:T(8,128)(2,1)} %param.17) | copy-start | bytes 9437188
  6.5 82.9 %all-gather.2.cloned.1.call-start = ((), (), s32[]{:S(2)}) async-start(), calls=%async_computation.3 | async-start | bytes 6684672 | tf_op jit(solution)/shard_map/all_gather | solution.py:95
  7.4 4.3 %collective-permute-start = (s32[2,256]{1,0:T(2,128)S(1)}, s32[2,256]{1,0:T(2,128)S(1)}, u32[]{:S(2)}, u32[]{:S(2)}) collective-permute-start(s32[2,256]{1,0:T(2,128)S(1)} %pad_add_fusion), channel_id=1, source_target_pairs={{16,0},{32,16},{48,32},{64,48},{80,64},{96,80},{112,96},{128,112},... | collective-permute-start | bytes 6152 | tf_op jit(solution)/shard_map/ppermute | solution.py:19
  46.8 1.6 copy-start.2
  48.4 113.1 %reduce-scatter.2.cloned.1.call-start = ((), (), s32[]{:S(2)}) async-start(), calls=%async_computation.4 | async-start | bytes 3538944 | tf_op jit(solution)/shard_map/reduce_scatter | solution.py:125
  54.7 5.4 %collective-permute-start.1 = (f32[24]{0:T(128)S(1)}, f32[24]{0:T(128)S(1)}, u32[]{:S(2)}, u32[]{:S(2)}) collective-permute-start(f32[24]{0:T(128)S(1)} %get-tuple-element.23), channel_id=1, source_target_pairs={{240,0},{0,16},{16,32},{32,48},{48,64},{64,80},{80,96},{96,112},{1... | collective-permute-start | bytes 296 | tf_op jit(solution)/shard_map/ppermute | solution.py:19
  101.1 6.0 %collective-permute-start.3 = (bf16[192,8192]{1,0:T(8,128)(2,1)}, bf16[192,8192]{1,0:T(8,128)(2,1)}, u32[]{:S(2)}, u32[]{:S(2)}) collective-permute-start(bf16[192,8192]{1,0:T(8,128)(2,1)} %convolution_convert_fusion), channel_id=1, source_target_pairs={{0,16},{16,0},{1,17},{17,1},{2,18},{18,2},{3,19},{19,3},{4,20},{20... | collective-permute-start | bytes 9437192 | tf_op jit(solution)/shard_map/ppermute | solution.py:122
  111.7 59.9 %copy-start.1 = (s32[1,256]{1,0:T(1,128)S(1)}, s32[1,256]{1,0:T(1,128)}, u32[]{:S(2)}) copy-start(s32[1,256]{1,0:T(1,128)} %param.11) | copy-start | bytes 3076
  111.8 74.1 %collective-permute-start.2 = (bf16[1024,512]{1,0:T(8,128)(2,1)}, bf16[1024,512]{1,0:T(8,128)(2,1)}, u32[]{:S(2)}, u32[]{:S(2)}) collective-permute-start(bf16[1024,512]{1,0:T(8,128)(2,1)} %param.10), channel_id=1, source_target_pairs={{240,0},{0,16},{16,32},{32,48},{48,64},{64,80},{80,96},{96,112},{1... | collective-permute-start | bytes 3145736 | tf_op jit(solution)/shard_map/ppermute | solution.py:19
  163.4 21.7 %all-to-all-start.1 = ((bf16[16,24,512]{2,1,0:T(8,128)(2,1)}), bf16[16,24,512]{2,1,0:T(8,128)(2,1)S(1)}, u32[]{:S(2)}, u32[]{:S(2)}) async-start(bf16[16,24,512]{2,1,0:T(8,128)(2,1)} %bitcast.81), calls=%async_computation.2 | async-start | bytes 786432 | tf_op jit(solution)/shard_map/all_to_all | solution.py:128
Sparse Core Ops, SparseCore 0:
  48.5 40.9 all-gather.1
  111.9 49.5 reduce-scatter.1

commit v18 on v15

--- a/solution.py
+++ b/solution.py
@@ -107,19 +107,21 @@
     for core in range(n_core):
         for chip in range(n_chip):
             order.append((chip * n_core + core - 1) % n_section)
-    hidden = jnp.take(
-        hidden.reshape(groups, capacity, hidden_width), jnp.array(order, jnp.int32), axis=0
-    ).reshape(groups * capacity, hidden_width)
-    hidden = hidden.reshape(n_core, n_chip * capacity, hidden_width)
+    order = jnp.array(order, jnp.int32).reshape(n_core, n_chip)
+    grouped = hidden.reshape(groups, capacity, hidden_width)
     core = lax.axis_index("core")
+
+    def half_rows(which):
+        picked_groups = lax.dynamic_index_in_dim(order, which, axis=0, keepdims=False)
+        return jnp.take(grouped, picked_groups, axis=0).reshape(n_chip * capacity, hidden_width)
 
     def down_part(rows):
         part = jnp.dot(rows, down_w[0], preferred_element_type=jnp.float32)
         return lax.optimization_barrier(part.astype(jnp.bfloat16)).astype(jnp.float32).astype(jnp.bfloat16)
 
-    give = down_part(lax.dynamic_index_in_dim(hidden, 1 - core, axis=0, keepdims=False))
+    give = down_part(half_rows(1 - core))
     taken = lax.ppermute(give, "core", [(0, 1), (1, 0)])
-    keep = down_part(lax.dynamic_index_in_dim(hidden, core, axis=0, keepdims=False))
+    keep = down_part(half_rows(core))
     pair = (keep.astype(jnp.float32) + taken.astype(jnp.float32)).astype(jnp.bfloat16)
     summed = lax.psum_scatter(pair, "chip", scatter_dimension=0, tiled=True)
     update_rows = (score_home[:, None] * summed.astype(jnp.float32)).astype(jnp.bfloat16)

time: 196 us -> 196 us (level)
  no operation moved by 1% of the time
where the time goes in v18:
time: 196 us
  waiting for transfers between devices  98.7 us (50%)
  blocking collectives  29.1 us (15%)
  other arithmetic  21.2 us (11%)
  matrix products  13.9 us (7%)
  between operations  13.6 us (7%)
  starting transfers between devices  12.2 us (6%)
  local copies, waits for them, and re-layouts  7.06 us (4%)
    reduce_scatter x1, waiting for transfers between devices, body(): summed = lax.psum_scatter(pair, 'chip', scatter_dimension=0, tiled=True)  49.4 us
    all_to_all x1, blocking collectives, body(): lax.all_to_all(buffer, 'expert', split_axis=0, concat_axis=2, tiled=True)[0]  29.1 us
    all_gather x1, waiting for transfers between devices, body(): block = lax.all_gather(normed, SECTION, axis=0, tiled=True)  28.3 us
    all_to_all x1, waiting for transfers between devices, body(): lax.all_to_all(outgoing, 'expert', split_axis=0, concat_axis=0, tiled=True)  11.8 us
    all_to_all x1, starting transfers between devices, body(): lax.all_to_all(outgoing, 'expert', split_axis=0, concat_axis=0, tiled=True)  8.67 us
    dot_general x1, matrix products, feature_product(): lax.dot_general(block, weight, (((1,), (1,)), ((), ())), preferred_elemen...  8.21 us
    concatenate x1, other arithmetic, body(): stacked = jnp.concatenate([gate_w[0], up_w[0]], axis=0)  6.2 us
    ppermute x4, waiting for transfers between devices, passed_along(): return lax.ppermute(block, axis, route)  5.07 us
  transfers between devices with their start and end apart: 8, of which 5 were waited for; matrix products, arithmetic and copies ran while one was open for 9% of the time, Pallas kernels for 0%

profile of v18, /device:TPU:8, one launch (start us, length us, event | category | flops | bytes accessed | tf_op | source)
XLA Modules:
  0.0 195.8 jit_solution(11199907230713437711)
XLA Ops:
  6.5 2.1 %collective-permute-start = (s32[256,1]{0,1:T(1,128)}, s32[256,1]{0,1:T(1,128)S(1)}, u32[]{:S(2)}, u32[]{:S(2)}) collective-permute-start(s32[256,1]{0,1:T(1,128)} %param.14), channel_id=1, source_target_pairs={{16,0},{32,16},{48,32},{64,48},{80,64},{96,80},{112,96},{128,112},... | collective-permute-start | bytes 3080 | tf_op jit(solution)/shard_map/ppermute | solution.py:19
  8.6 0.7 collective-permute-start.1
  9.3 0.7 fusion.23
  10.0 0.7 fusion.18
  10.7 0.8 iota_compare_fusion.2
  11.5 0.7 pad_add_fusion
  12.2 1.2 reduce-window.6
  13.4 0.1 slice.68
  13.5 0.1 copy.22
  13.6 0.1 fusion.16
  13.7 0.7 multiply_add_fusion
  14.4 0.6 fusion.43
  15.0 0.1 broadcast_compare_fusion
  15.2 2.6 %gather_fusion = bf16[256,512]{1,0:T(8,128)(2,1)S(1)} fusion(bf16[1024,512]{1,0:T(8,128)(2,1)} %param.12, s32[1024]{0:T(1024)S(1)} %pad_clamp_fusion.2), kind=kCustom, calls=%fused_computation.2 | custom fusion | bytes 525312 | tf_op jit(solution)/shard_map/gather | solution.py:39
  17.7 1.3 convolution_convert_fusion.2
  19.0 29.1 %all_to_all.20 = bf16[16,32,512]{2,1,0:T(8,128)(2,1)S(1)} all-to-all(bf16[16,32,512]{2,1,0:T(8,128)(2,1)S(1)} %bitcast.85), channel_id=1, replica_groups=mesh['chip'=8,'core'=2,'expert'=16] {'expert'}, dimensions={0} | all-to-all | bytes 1048576 | tf_op jit(solution)/shard_map/all_to_all | solution.py:79
  48.1 0.1 fusion.44
  48.2 0.1 slice_add_fusion
  48.3 0.1 fusion.42
  48.3 0.1 copy.32
  48.4 0.3 multiply_reduce_fusion
  48.7 0.9 multiply_convert_fusion.1
  49.6 0.0 all-gather.2.cloned.1.call-update
  49.6 0.0 reduce-scatter.2.cloned.1.call-start
  49.7 6.2 %pad_maximum_fusion = bf16[384,8192]{1,0:T(8,128)(2,1)} fusion(bf16[192,8192]{1,0:T(8,128)(2,1)} %bitcast.76, bf16[192,8192]{1,0:T(8,128)(2,1)} %bitcast.77), kind=kLoop, calls=%fused_computation.6 | loop fusion | flops 12582912 | bytes 12582912 | tf_op jit(solution)/shard_map/concatenate | solution.py:95
  55.9 5.1 %collective-permute-done.2 = f32[24]{0:T(128)S(1)} collective-permute-done((f32[24]{0:T(128)S(1)}, f32[24]{0:T(128)S(1)}, u32[]{:S(2)}, u32[]{:S(2)}) %collective-permute-start.2) | collective-permute-done | bytes 128 | tf_op jit(solution)/shard_map/ppermute | solution.py:19
  61.0 28.3 %all-gather.2.cloned.1.call-done = bf16[384,8192]{1,0:T(8,128)(2,1)} async-done(((bf16[24,8192]{1,0:T(8,128)(2,1)}), bf16[384,8192]{1,0:T(8,128)(2,1)}) %all-gather.2.cloned.1.call-update) | async-done | bytes 6291472 | tf_op jit(solution)/shard_map/all_gather | solution.py:94
  89.3 8.2 %fusion.45 = f32[384,384]{0,1:T(8,128)S(1)} fusion(bf16[384,8192]{1,0:T(8,128)(2,1)} %all-gather.2.cloned.1.call-done, bf16[384,8192]{1,0:T(8,128)(2,1)} %pad_maximum_fusion), kind=kOutput, calls=%fused_computation.102 | convolution fusion | flops 2415919104 | bytes 13172736 | tf_op jit(solution)/shard_map/dot_general | solution.py:23
  97.5 0.1 fusion.7
  97.6 0.1 copy.26
  97.8 0.6 gather_fusion.2
  98.3 0.1 broadcast_select_fusion
  98.4 2.6 %convolution_convert_fusion = bf16[192,8192]{1,0:T(8,128)(2,1)} fusion(bf16[192,192]{1,0:T(8,128)(2,1)S(1)} %bitcast.83, bf16[1,192,8192]{2,1,0:T(8,128)(2,1)S(1)} %copy-done), kind=kOutput, calls=%fused_computation.4 | convolution fusion | flops 605552640 | bytes 6365184 | tf_op jit(solution)/shard_map/dot_general | solution.py:119
  101.1 0.2 collective-permute-start.4
  101.3 0.6 gather_fusion.1
  101.9 0.1 broadcast_select_fusion.1
  101.9 1.0 convolution_convert_fusion.1
  102.9 4.1 %collective-permute-done.4 = bf16[192,8192]{1,0:T(8,128)(2,1)} collective-permute-done((bf16[192,8192]{1,0:T(8,128)(2,1)}, bf16[192,8192]{1,0:T(8,128)(2,1)}, u32[]{:S(2)}, u32[]{:S(2)}) %collective-permute-start.4) | collective-permute-done | bytes 3145760 | tf_op jit(solution)/shard_map/ppermute | solution.py:123
  107.1 4.6 %add_convert_fusion = bf16[192,8192]{1,0:T(8,128)(2,1)} fusion(bf16[192,8192]{1,0:T(8,128)(2,1)} %collective-permute-done.4, bf16[192,8192]{1,0:T(8,128)(2,1)S(1)} %convolution_convert_fusion.1), kind=kLoop, calls=%fused_computation.7 | loop fusion | flops 6291456 | bytes 9437184 | tf_op jit(solution)/shard_map/convert_element_type | solution.py:125
  111.7 0.5 collective-permute-start.3
  112.2 49.4 %reduce-scatter.2.cloned.1.call-done = bf16[24,8192]{1,0:T(8,128)(2,1)} async-done(((bf16[192,8192]{1,0:T(8,128)(2,1)}), bf16[24,8192]{1,0:T(8,128)(2,1)}) %reduce-scatter.2.cloned.1.call-update) | async-done | bytes 393232 | tf_op jit(solution)/shard_map/reduce_scatter | solution.py:126
  161.6 1.1 multiply_convert_fusion
  162.8 0.8 copy.38
  163.5 8.7 %all-to-all-start.1 = ((bf16[16,24,512]{2,1,0:T(8,128)(2,1)}), bf16[16,24,512]{2,1,0:T(8,128)(2,1)S(1)}, u32[]{:S(2)}, u32[]{:S(2)}) async-start(bf16[16,24,512]{2,1,0:T(8,128)(2,1)} %bitcast.79), calls=%async_computation.2 | async-start | bytes 786432 | tf_op jit(solution)/shard_map/all_to_all | solution.py:129
  172.2 1.6 scatter_custom_fusion
  173.8 11.8 %all-to-all-done.1 = bf16[16,24,512]{2,1,0:T(8,128)(2,1)S(1)} async-done(((bf16[16,24,512]{2,1,0:T(8,128)(2,1)}), bf16[16,24,512]{2,1,0:T(8,128)(2,1)S(1)}, u32[]{:S(2)}, u32[]{:S(2)}) %all-to-all-start.1) | async-done | bytes 393248 | tf_op jit(solution)/shard_map/all_to_all | solution.py:129
  185.6 0.8 fusion.2
  186.4 2.6 %add_convert_fusion.1 = bf16[1024,512]{1,0:T(8,128)(2,1)} fusion(f32[1024,512]{1,0:T(8,128)S(1)} %fusion.2, bf16[1024,512]{1,0:T(8,128)(2,1)} %collective-permute-done.3), kind=kLoop, calls=%fused_computation.10 | loop fusion | flops 1572864 | bytes 4194304 | tf_op jit(solution)/shard_map/convert_element_type | solution.py:139
  (26 shorter events, 0.2 us)
Async XLA Ops:
  6.5 91.9 %copy-start = (bf16[1,192,8192]{2,1,0:T(8,128)(2,1)S(1)}, bf16[1,192,8192]{2,1,0:T(8,128)(2,1)}, u32[]{:S(2)}) copy-start(bf16[1,192,8192]{2,1,0:T(8,128)(2,1)} %param.19) | copy-start | bytes 9437188
  6.5 82.7 %all-gather.2.cloned.1.call-start = ((), (), s32[]{:S(2)}) async-start(), calls=%async_computation.3 | async-start | bytes 6684672 | tf_op jit(solution)/shard_map/all_gather | solution.py:94
  6.5 5.0 %collective-permute-start = (s32[256,1]{0,1:T(1,128)}, s32[256,1]{0,1:T(1,128)S(1)}, u32[]{:S(2)}, u32[]{:S(2)}) collective-permute-start(s32[256,1]{0,1:T(1,128)} %param.14), channel_id=1, source_target_pairs={{16,0},{32,16},{48,32},{64,48},{80,64},{96,80},{112,96},{128,112},... | collective-permute-start | bytes 3080 | tf_op jit(solution)/shard_map/ppermute | solution.py:19
  8.6 6.4 %collective-permute-start.1 = (s32[1,256]{1,0:T(1,128)}, s32[1,256]{1,0:T(1,128)S(1)}, u32[]{:S(2)}, u32[]{:S(2)}) collective-permute-start(s32[1,256]{1,0:T(1,128)} %param.13), channel_id=1, source_target_pairs={{16,0},{32,16},{48,32},{64,48},{80,64},{96,80},{112,96},{128,112},... | collective-permute-start | bytes 3080 | tf_op jit(solution)/shard_map/ppermute | solution.py:19
  48.1 1.6 copy-start.2
  49.6 112.0 %reduce-scatter.2.cloned.1.call-start = ((), (), s32[]{:S(2)}) async-start(), calls=%async_computation.4 | async-start | bytes 3538944 | tf_op jit(solution)/shard_map/reduce_scatter | solution.py:126
  55.9 5.1 %collective-permute-start.2 = (f32[24]{0:T(128)S(1)}, f32[24]{0:T(128)S(1)}, u32[]{:S(2)}, u32[]{:S(2)}) collective-permute-start(f32[24]{0:T(128)S(1)} %get-tuple-element.30), channel_id=1, source_target_pairs={{240,0},{0,16},{16,32},{32,48},{48,64},{64,80},{80,96},{96,112},{1... | collective-permute-start | bytes 296 | tf_op jit(solution)/shard_map/ppermute | solution.py:19
  101.1 6.0 %collective-permute-start.4 = (bf16[192,8192]{1,0:T(8,128)(2,1)}, bf16[192,8192]{1,0:T(8,128)(2,1)}, u32[]{:S(2)}, u32[]{:S(2)}) collective-permute-start(bf16[192,8192]{1,0:T(8,128)(2,1)} %convolution_convert_fusion), channel_id=1, source_target_pairs={{0,16},{16,0},{1,17},{17,1},{2,18},{18,2},{3,19},{19,3},{4,20},{20... | collective-permute-start | bytes 9437192 | tf_op jit(solution)/shard_map/ppermute | solution.py:123
  111.7 60.5 %copy-start.1 = (s32[1,256]{1,0:T(1,128)S(1)}, s32[1,256]{1,0:T(1,128)}, u32[]{:S(2)}) copy-start(s32[1,256]{1,0:T(1,128)} %param.13) | copy-start | bytes 3076
  111.7 74.7 %collective-permute-start.3 = (bf16[1024,512]{1,0:T(8,128)(2,1)}, bf16[1024,512]{1,0:T(8,128)(2,1)}, u32[]{:S(2)}, u32[]{:S(2)}) collective-permute-start(bf16[1024,512]{1,0:T(8,128)(2,1)} %param.12), channel_id=1, source_target_pairs={{240,0},{0,16},{16,32},{32,48},{48,64},{64,80},{80,96},{96,112},{1... | collective-permute-start | bytes 3145736 | tf_op jit(solution)/shard_map/ppermute | solution.py:19
  163.5 22.1 %all-to-all-start.1 = ((bf16[16,24,512]{2,1,0:T(8,128)(2,1)}), bf16[16,24,512]{2,1,0:T(8,128)(2,1)S(1)}, u32[]{:S(2)}, u32[]{:S(2)}) async-start(bf16[16,24,512]{2,1,0:T(8,128)(2,1)} %bitcast.79), calls=%async_computation.2 | async-start | bytes 786432 | tf_op jit(solution)/shard_map/all_to_all | solution.py:129
Sparse Core Ops, SparseCore 0:
  49.8 39.4 all-gather.1
  111.8 49.7 reduce-scatter.1
